TPU v7x, 256 devices: a whole 4x4x8 slice. The times are simulated.
256 devices in a mesh: rows: 128 (over x, y, z), help: 2 (over core).
Axes of the slice: x: 4, y: 4, z: 8, core: 2. Of those that a mesh axis runs over, the one named last changes fastest.
Arguments:
- density: float32 [256, 5, 256, 256], P('rows', None, None, 'help'), as said below
- pattern: int32 [256, 5], P('rows'), may hold values from 0 to 1, as said below
- truncation: int32 [2, 256, 5], P(None, 'rows'), may hold values from 0 to 1, as said below
Outputs:
- purified: float32 [256, 5, 256, 256], P('rows', None, None, 'help')
Inputs may be any that keep to these rules, and one draw needn't show every extreme that they name: pattern[i, 2] = 1; pattern[i, s] = pattern[i + s - 2, 4 - s]; pattern[i, s] = 0 where i + s - 2 lies outside 0 to 255. truncation[t] obeys the same three rules as pattern for every t. density is symmetric: tile slot s of block row i is the transpose of slot 4 - s of block row i + s - 2 wherever both lie inside the matrix.
All inputs are finite; a program needn't handle non-finite values.
Results may differ from a plain program's by a relative error of at most 0.0002.
Values sent between devices are 32-bit elements; how exact they have to be, the bound alone decides.
No kernel may reach another device: no remote copies, remote signals or barrier semaphores. Data moves between devices by JAX's collectives and lax.ppermute only.
A program may use at most 64 MiB of HBM per device.

v0:
```python
import jax
import jax.numpy as jnp
from jax import lax
from jax.sharding import PartitionSpec as P

STEPS = 2


def padded(cells, sides, width):
    for axis, dim in sides:
        count = lax.axis_size(axis)
        ends = count - 1
        head = lax.slice_in_dim(cells, 0, width, axis=dim)
        tail = lax.slice_in_dim(cells, cells.shape[dim] - width, cells.shape[dim], axis=dim)
        cells = jnp.concatenate(
            [
                lax.ppermute(tail, axis, [(i, (i + 1) % count) for i in range(ends)]),
                cells,
                lax.ppermute(head, axis, [((i + 1) % count, i) for i in range(ends)]),
            ],
            axis=dim,
        )
    return cells


def in_order(parts, dim):
    lengths = list(parts.shape[1:])
    lengths[dim] *= parts.shape[0]
    return jnp.moveaxis(parts, 0, dim).reshape(lengths)


def copy_for_each(value, axis):
    peers = lax.axis_size(axis)
    return lax.all_to_all(
        jnp.broadcast_to(value[None], (peers, *value.shape)), axis, 0, 0, tiled=True
    )


def gather_directly(value, axis, dim):
    return in_order(copy_for_each(value, axis), dim)


def band_square(matrix):
    row_count, slot_count, tile_rows, half_cols = matrix.shape
    band_reach = (slot_count - 1) // 2
    extended = padded(matrix, (("rows", 0),), band_reach)
    columns = gather_directly(matrix, "help", 3)
    result = jnp.zeros_like(matrix)
    for offset_k in range(-band_reach, band_reach + 1):
        left_tile = columns[:, offset_k + band_reach]
        right_slab = extended[band_reach + offset_k : band_reach + offset_k + row_count]
        low_slot = max(0, -offset_k)
        high_slot = min(slot_count, slot_count - offset_k)
        product_term = jnp.einsum(
            "rab,rtbc->rtac",
            left_tile,
            right_slab[:, low_slot:high_slot],
            precision=lax.Precision.HIGHEST,
        )
        result = result.at[:, low_slot + offset_k : high_slot + offset_k].add(product_term)
    return result


def local(density, pattern, truncation):
    matrix = density * pattern[:, :, None, None].astype(jnp.float32)
    for step_index in range(STEPS):
        squared = band_square(matrix)
        if step_index % 2 == 0:
            stepped = squared
        else:
            stepped = 2.0 * matrix - squared
        matrix = stepped * truncation[step_index][:, :, None, None].astype(jnp.float32)
    return matrix


def solution(mesh):
    return jax.shard_map(
        local,
        mesh=mesh,
        in_specs=(P("rows", None, None, "help"), P("rows", None), P(None, "rows", None)),
        out_specs=P("rows", None, None, "help"),
        check_vma=False,
    )
```

profile of v0, /device:TPU:6, one launch (start us, length us, event | category | flops | bytes accessed | tf_op | source)
XLA Modules:
  0.0 99.6 jit_solution(5282977779816857062)
XLA Ops:
  0.0 1.7 %copy.8 = f32[2,5,256,128]{2,3,1,0:T(8,128)S(1)} copy(f32[2,5,256,128]{3,2,1,0:T(8,128)} %param.27) | data formatting | bytes 2621440 | tf_op args[0]
  1.8 0.2 broadcast_multiply_fusion.1
  2.0 3.8 %collective-permute-start = (f32[2,5,256,128]{2,3,1,0:T(8,128)S(1)}, f32[2,5,256,128]{2,3,1,0:T(8,128)}, u32[]{:S(2)}, u32[]{:S(2)}) collective-permute-start(f32[2,5,256,128]{2,3,1,0:T(8,128)S(1)} %broadcast_multiply_fusion.1), channel_id=1, source_target_pairs={{0,2},{2,4},{4,6},{6,8},{8,10},{10,12},{12,14},{14,16},{16,18},{18... | collective-permute-start | bytes 3932168 | tf_op jit(solution)/shard_map/ppermute | solution.py:17
  5.8 8.6 %collective-permute-start.1 = (f32[2,5,256,128]{2,3,1,0:T(8,128)S(1)}, f32[2,5,256,128]{2,3,1,0:T(8,128)}, u32[]{:S(2)}, u32[]{:S(2)}) collective-permute-start(f32[2,5,256,128]{2,3,1,0:T(8,128)S(1)} %broadcast_multiply_fusion.1), channel_id=1, source_target_pairs={{2,0},{4,2},{6,4},{8,6},{10,8},{12,10},{14,12},{16,14},{18,16},{20... | collective-permute-start | bytes 3932168 | tf_op jit(solution)/shard_map/ppermute | solution.py:19
  14.4 0.4 copy.9
  14.8 1.8 %broadcast_in_dim.4 = f32[2,2,5,256,128]{4,3,1,2,0:T(8,128)} broadcast(f32[2,5,256,128]{3,2,0,1:T(8,128)S(1)} %copy.9), dimensions={1,2,3,4} | broadcast | bytes 3932160 | tf_op jit(solution)/shard_map/broadcast_in_dim | solution.py:35
  16.6 5.1 %all-to-all-start = ((f32[2,2,5,256,128]{4,3,1,2,0:T(8,128)}), f32[2,2,5,256,128]{4,3,1,2,0:T(8,128)}, u32[]{:S(2)}, u32[]{:S(2)}) async-start(f32[2,2,5,256,128]{4,3,1,2,0:T(8,128)} %broadcast_in_dim.4), calls=%async_computation | async-start | bytes 5242880 | tf_op jit(solution)/shard_map/all_to_all | solution.py:34
  21.7 3.3 %all-to-all-done = f32[2,2,5,256,128]{4,3,1,2,0:T(8,128)} async-done(((f32[2,2,5,256,128]{4,3,1,2,0:T(8,128)}), f32[2,2,5,256,128]{4,3,1,2,0:T(8,128)}, u32[]{:S(2)}, u32[]{:S(2)}) %all-to-all-start) | async-done | bytes 2621472 | tf_op jit(solution)/shard_map/all_to_all | solution.py:34
  25.1 2.0 %copy_bitcast_fusion.1 = f32[2,5,256,256]{3,2,0,1:T(8,128)S(1)} fusion(f32[2,2,5,256,128]{4,3,1,2,0:T(8,128)} %all-to-all-done), kind=kLoop, calls=%fused_computation.1 | loop fusion | bytes 5242880 | tf_op jit(solution)/shard_map/reshape | solution.py:29
  27.0 14.3 %collective-permute-done = f32[2,5,256,128]{2,3,1,0:T(8,128)} collective-permute-done((f32[2,5,256,128]{2,3,1,0:T(8,128)S(1)}, f32[2,5,256,128]{2,3,1,0:T(8,128)}, u32[]{:S(2)}, u32[]{:S(2)}) %collective-permute-start) | collective-permute-done | bytes 1310752 | tf_op jit(solution)/shard_map/ppermute | solution.py:17
  41.3 2.0 %convolution_bitcast_fusion.5 = f32[2,3,256,128]{2,3,1,0:T(8,128)S(1)} fusion(f32[2,5,256,128]{2,3,1,0:T(8,128)} %collective-permute-done, f32[2,5,256,256]{3,2,0,1:T(8,128)S(1)} %copy_bitcast_fusion.1), kind=kOutput, calls=%fused_computation.32 | convolution fusion | flops 603979776 | bytes 2621440 | tf_op jit(solution)/shard_map/rab,rtbc->rtac/dot_general | solution.py:54
  43.3 0.1 scatter-add.26
  43.5 2.3 %add_dynamic-update-slice_fusion.1 = f32[2,5,256,128]{2,3,1,0:T(8,128)S(1)} fusion(f32[2,5,256,128]{2,3,1,0:T(8,128)S(1)} %scatter-add.26, f32[2,5,256,256]{3,2,0,1:T(8,128)S(1)} %copy_bitcast_fusion.1, f32[2,5,256,128]{2,3,1,0:T(8,128)S(1)} %broadcast_multiply_fusion.1, f32[2,5,256,128]{2,3,1,0:T(8,128)} %collective-permute-done), kind=kOutput, calls=%fused_computation.34 | convolution fusion | flops 806223872 | bytes 5242880 | tf_op jit(solution)/shard_map/rab,rtbc->rtac/dot_general | solution.py:54
  45.7 1.4 %fusion.16 = f32[2,5,256,128]{2,3,1,0:T(8,128)S(1)} fusion(f32[2,5,256,128]{2,3,1,0:T(8,128)S(1)} %add_dynamic-update-slice_fusion.1, f32[2,5,256,128]{2,3,1,0:T(8,128)S(1)} %broadcast_multiply_fusion.1, f32[2,5,256,256]{3,2,0,1:T(8,128)S(1)} %copy_bitcast_fusion.1), kind=kOutput, calls=%fused_computation.20 | convolution fusion | flops 1006960640 | bytes 4456448 | tf_op jit(solution)/shard_map/rab,rtbc->rtac/dot_general | solution.py:54
  47.1 2.1 %fusion.30 = f32[2,4,256,128]{2,3,1,0:T(8,128)S(1)} fusion(f32[2,5,256,128]{2,3,1,0:T(8,128)} %collective-permute-done.1, f32[2,5,256,128]{2,3,1,0:T(8,128)S(1)} %broadcast_multiply_fusion.1, f32[2,5,256,128]{2,3,1,0:T(8,128)S(1)} %fusion.16, f32[2,5,256,256]{3,2,0,1:T(8,128)S(1)} %copy_bitcast_fusion.1), kind=kOutput, calls=%fused_computation.26 | convolution fusion | flops 806223872 | bytes 5242880 | tf_op jit(solution)/shard_map/rab,rtbc->rtac/dot_general | solution.py:54
  49.4 2.0 %fusion.37 = f32[2,5,256,128]{2,3,1,0:T(8,128)S(1)} fusion(f32[2,5,256,128]{2,3,1,0:T(8,128)S(1)} %constant_dynamic-update-slice_fusion.1, f32[2,4,256,128]{2,3,1,0:T(8,128)S(1)} %fusion.30, f32[2,5,256,128]{2,3,1,0:T(8,128)} %collective-permute-done.1, f32[2,5,256,256]{3,2,0,1:T(8,128)S(1)} %copy_bitcast_fusion.1), kind=kOutput, calls=%fused_computation.38 | convolution fusion | flops 604176384 | bytes 3407872 | tf_op jit(solution)/shard_map/rab,rtbc->rtac/dot_general | solution.py:54
  51.4 0.2 broadcast_multiply_fusion
  51.6 1.9 %collective-permute-start.2 = (f32[2,5,256,128]{2,3,1,0:T(8,128)S(1)}, f32[2,5,256,128]{2,3,1,0:T(8,128)}, u32[]{:S(2)}, u32[]{:S(2)}) collective-permute-start(f32[2,5,256,128]{2,3,1,0:T(8,128)S(1)} %broadcast_multiply_fusion), channel_id=1, source_target_pairs={{0,2},{2,4},{4,6},{6,8},{8,10},{10,12},{12,14},{14,16},{16,18},{18... | collective-permute-start | bytes 3932168 | tf_op jit(solution)/shard_map/ppermute | solution.py:17
  53.6 8.1 %collective-permute-start.3 = (f32[2,5,256,128]{2,3,1,0:T(8,128)S(1)}, f32[2,5,256,128]{2,3,1,0:T(8,128)}, u32[]{:S(2)}, u32[]{:S(2)}) collective-permute-start(f32[2,5,256,128]{2,3,1,0:T(8,128)S(1)} %broadcast_multiply_fusion), channel_id=1, source_target_pairs={{2,0},{4,2},{6,4},{8,6},{10,8},{12,10},{14,12},{16,14},{18,16},{20... | collective-permute-start | bytes 3932168 | tf_op jit(solution)/shard_map/ppermute | solution.py:19
  61.7 1.5 %copy.11 = f32[2,5,256,128]{3,2,0,1:T(8,128)} copy(f32[2,5,256,128]{2,3,1,0:T(8,128)S(1)} %broadcast_multiply_fusion) | data formatting | bytes 2621440 | tf_op jit(solution)/shard_map/mul | solution.py:72
  63.2 1.6 %broadcast_in_dim.5 = f32[2,2,5,256,128]{4,3,1,2,0:T(8,128)S(1)} broadcast(f32[2,5,256,128]{3,2,0,1:T(8,128)} %copy.11), dimensions={1,2,3,4} | broadcast | bytes 3932160 | tf_op jit(solution)/shard_map/broadcast_in_dim | solution.py:35
  64.8 5.8 %all_to_all.10 = f32[2,2,5,256,128]{4,3,1,2,0:T(8,128)S(1)} all-to-all(f32[2,2,5,256,128]{4,3,1,2,0:T(8,128)S(1)} %broadcast_in_dim.5), channel_id=1, replica_groups=mesh['rows'=128,'help'=2] {'help'}, dimensions={0} | all-to-all | bytes 5242880 | tf_op jit(solution)/shard_map/all_to_all | solution.py:34
  70.6 0.2 copy_bitcast_fusion
  70.8 17.0 %collective-permute-done.2 = f32[2,5,256,128]{2,3,1,0:T(8,128)} collective-permute-done((f32[2,5,256,128]{2,3,1,0:T(8,128)S(1)}, f32[2,5,256,128]{2,3,1,0:T(8,128)}, u32[]{:S(2)}, u32[]{:S(2)}) %collective-permute-start.2) | collective-permute-done | bytes 1310752 | tf_op jit(solution)/shard_map/ppermute | solution.py:17
  87.8 2.0 %convolution_bitcast_fusion.3 = f32[2,3,256,128]{2,3,1,0:T(8,128)S(1)} fusion(f32[2,5,256,128]{2,3,1,0:T(8,128)} %collective-permute-done.2, f32[2,5,256,256]{3,2,0,1:T(8,128)S(1)} %copy_bitcast_fusion), kind=kOutput, calls=%fused_computation.30 | convolution fusion | flops 603979776 | bytes 2621440 | tf_op jit(solution)/shard_map/rab,rtbc->rtac/dot_general | solution.py:54
  89.8 0.1 scatter-add.34
  89.9 2.3 %add_dynamic-update-slice_fusion = f32[2,5,256,128]{2,3,1,0:T(8,128)S(1)} fusion(f32[2,5,256,128]{2,3,1,0:T(8,128)S(1)} %scatter-add.34, f32[2,5,256,256]{3,2,0,1:T(8,128)S(1)} %copy_bitcast_fusion, f32[2,5,256,128]{2,3,1,0:T(8,128)S(1)} %broadcast_multiply_fusion, f32[2,5,256,128]{2,3,1,0:T(8,128)} %collective-permute-done.2), kind=kOutput, calls=%fused_computation.33 | convolution fusion | flops 806223872 | bytes 5242880 | tf_op jit(solution)/shard_map/rab,rtbc->rtac/dot_general | solution.py:54
  92.2 1.3 %fusion.17 = f32[2,5,256,128]{2,3,1,0:T(8,128)S(1)} fusion(f32[2,5,256,128]{2,3,1,0:T(8,128)S(1)} %add_dynamic-update-slice_fusion, f32[2,5,256,128]{2,3,1,0:T(8,128)S(1)} %broadcast_multiply_fusion, f32[2,5,256,256]{3,2,0,1:T(8,128)S(1)} %copy_bitcast_fusion), kind=kOutput, calls=%fused_computation.21 | convolution fusion | flops 1006960640 | bytes 4456448 | tf_op jit(solution)/shard_map/rab,rtbc->rtac/dot_general | solution.py:54
  93.6 2.2 %fusion.33 = f32[2,4,256,128]{2,3,1,0:T(8,128)S(1)} fusion(f32[2,5,256,128]{2,3,1,0:T(8,128)} %collective-permute-done.3, f32[2,5,256,128]{2,3,1,0:T(8,128)S(1)} %broadcast_multiply_fusion, f32[2,5,256,128]{2,3,1,0:T(8,128)S(1)} %fusion.17, f32[2,5,256,256]{3,2,0,1:T(8,128)S(1)} %copy_bitcast_fusion), kind=kOutput, calls=%fused_computation.27 | convolution fusion | flops 806223872 | bytes 5242880 | tf_op jit(solution)/shard_map/rab,rtbc->rtac/dot_general | solution.py:54
  95.9 2.0 %fusion.36 = f32[2,5,256,128]{2,3,1,0:T(8,128)S(1)} fusion(f32[2,5,256,128]{2,3,1,0:T(8,128)S(1)} %constant_dynamic-update-slice_fusion, f32[2,4,256,128]{2,3,1,0:T(8,128)S(1)} %fusion.33, f32[2,5,256,128]{2,3,1,0:T(8,128)} %collective-permute-done.3, f32[2,5,256,256]{3,2,0,1:T(8,128)S(1)} %copy_bitcast_fusion), kind=kOutput, calls=%fused_computation.36 | convolution fusion | flops 604176384 | bytes 3407872 | tf_op jit(solution)/shard_map/rab,rtbc->rtac/dot_general | solution.py:54
  97.9 0.3 subtract_multiply_fusion
  98.1 1.5 %copy.13 = f32[2,5,256,128]{3,2,1,0:T(8,128)} copy(f32[2,5,256,128]{2,3,1,0:T(8,128)S(1)} %subtract_multiply_fusion) | data formatting | bytes 2621440 | tf_op jit(solution)/shard_map/mul | solution.py:72
  (10 shorter events, 0.2 us)
Async XLA Ops:
  0.0 1.7 %copy-start.1 = (s32[2,5]{1,0:T(2,128)S(1)}, s32[2,5]{1,0:T(2,128)}, u32[]{:S(2)}) copy-start(s32[2,5]{1,0:T(2,128)} %param.28) | copy-start | bytes 124
  2.0 39.4 %collective-permute-start = (f32[2,5,256,128]{2,3,1,0:T(8,128)S(1)}, f32[2,5,256,128]{2,3,1,0:T(8,128)}, u32[]{:S(2)}, u32[]{:S(2)}) collective-permute-start(f32[2,5,256,128]{2,3,1,0:T(8,128)S(1)} %broadcast_multiply_fusion.1), channel_id=1, source_target_pairs={{0,2},{2,4},{4,6},{6,8},{8,10},{10,12},{12,14},{14,16},{16,18},{18... | collective-permute-start | bytes 3932168 | tf_op jit(solution)/shard_map/ppermute | solution.py:17
  5.8 41.3 %collective-permute-start.1 = (f32[2,5,256,128]{2,3,1,0:T(8,128)S(1)}, f32[2,5,256,128]{2,3,1,0:T(8,128)}, u32[]{:S(2)}, u32[]{:S(2)}) collective-permute-start(f32[2,5,256,128]{2,3,1,0:T(8,128)S(1)} %broadcast_multiply_fusion.1), channel_id=1, source_target_pairs={{2,0},{4,2},{6,4},{8,6},{10,8},{12,10},{14,12},{16,14},{18,16},{20... | collective-permute-start | bytes 3932168 | tf_op jit(solution)/shard_map/ppermute | solution.py:19
  16.6 5.2 %copy-start = (s32[2,2,5]{2,1,0:T(2,128)S(1)}, s32[2,2,5]{2,1,0:T(2,128)}, u32[]{:S(2)}) copy-start(s32[2,2,5]{2,1,0:T(2,128)} %param.29) | copy-start | bytes 244
  16.6 8.5 %all-to-all-start = ((f32[2,2,5,256,128]{4,3,1,2,0:T(8,128)}), f32[2,2,5,256,128]{4,3,1,2,0:T(8,128)}, u32[]{:S(2)}, u32[]{:S(2)}) async-start(f32[2,2,5,256,128]{4,3,1,2,0:T(8,128)} %broadcast_in_dim.4), calls=%async_computation | async-start | bytes 5242880 | tf_op jit(solution)/shard_map/all_to_all | solution.py:34
  51.6 36.2 %collective-permute-start.2 = (f32[2,5,256,128]{2,3,1,0:T(8,128)S(1)}, f32[2,5,256,128]{2,3,1,0:T(8,128)}, u32[]{:S(2)}, u32[]{:S(2)}) collective-permute-start(f32[2,5,256,128]{2,3,1,0:T(8,128)S(1)} %broadcast_multiply_fusion), channel_id=1, source_target_pairs={{0,2},{2,4},{4,6},{6,8},{8,10},{10,12},{12,14},{14,16},{16,18},{18... | collective-permute-start | bytes 3932168 | tf_op jit(solution)/shard_map/ppermute | solution.py:17
  53.6 40.0 %collective-permute-start.3 = (f32[2,5,256,128]{2,3,1,0:T(8,128)S(1)}, f32[2,5,256,128]{2,3,1,0:T(8,128)}, u32[]{:S(2)}, u32[]{:S(2)}) collective-permute-start(f32[2,5,256,128]{2,3,1,0:T(8,128)S(1)} %broadcast_multiply_fusion), channel_id=1, source_target_pairs={{2,0},{4,2},{6,4},{8,6},{10,8},{12,10},{14,12},{16,14},{18,16},{20... | collective-permute-start | bytes 3932168 | tf_op jit(solution)/shard_map/ppermute | solution.py:19
where the time goes:
time: 100 us; the launch traced here: 99.6 us
  waiting for transfers between devices  34.6 us (35%)
  starting transfers between devices  27.6 us (28%)
  matrix products  19.7 us (20%)
  local copies, waits for them, and re-layouts  11 us (11%)
  blocking collectives  5.84 us (6%)
    ppermute x2, waiting for transfers between devices, padded(): lax.ppermute(tail, axis, [(i, (i + 1) % count) for i in range(ends)])  31.2 us
    dot_general x10, matrix products, band_square(): jnp.einsum('rab,rtbc->rtac', left_tile, right_slab[:, low_slot:high_slot]...  19.7 us
    ppermute x2, starting transfers between devices, padded(): lax.ppermute(head, axis, [((i + 1) % count, i) for i in range(ends)])  16.7 us
    all_to_all x1, blocking collectives, copy_for_each(): lax.all_to_all(jnp.broadcast_to(value[None], (peers, *value.shape)), axis...  5.84 us
    ppermute x2, starting transfers between devices, padded(): lax.ppermute(tail, axis, [(i, (i + 1) % count) for i in range(ends)])  5.75 us
    all_to_all x1, starting transfers between devices, copy_for_each(): lax.all_to_all(jnp.broadcast_to(value[None], (peers, *value.shape)), axis...  5.14 us
    broadcast_in_dim x2, local copies, waits for them, and re-layouts, copy_for_each(): jnp.broadcast_to(value[None], (peers, *value.shape))  3.37 us
    all_to_all x1, waiting for transfers between devices, copy_for_each(): lax.all_to_all(jnp.broadcast_to(value[None], (peers, *value.shape)), axis...  3.33 us
  transfers between devices with their start and end apart: 5, of which 3 were waited for; matrix products, arithmetic and copies ran while one was open for 19% of the time, Pallas kernels for 0%

commit v1 on v0

--- a/solution.py
+++ b/solution.py
@@ -6,45 +6,46 @@
 STEPS = 2
 
 
-def padded(cells, sides, width):
-    for axis, dim in sides:
-        count = lax.axis_size(axis)
-        ends = count - 1
-        head = lax.slice_in_dim(cells, 0, width, axis=dim)
-        tail = lax.slice_in_dim(cells, cells.shape[dim] - width, cells.shape[dim], axis=dim)
-        cells = jnp.concatenate(
-            [
-                lax.ppermute(tail, axis, [(i, (i + 1) % count) for i in range(ends)]),
-                cells,
-                lax.ppermute(head, axis, [((i + 1) % count, i) for i in range(ends)]),
-            ],
-            axis=dim,
-        )
-    return cells
+def swap_help(value):
+    return lax.ppermute(value, "help", [(0, 1), (1, 0)])
 
 
-def in_order(parts, dim):
-    lengths = list(parts.shape[1:])
-    lengths[dim] *= parts.shape[0]
-    return jnp.moveaxis(parts, 0, dim).reshape(lengths)
-
-
-def copy_for_each(value, axis):
-    peers = lax.axis_size(axis)
-    return lax.all_to_all(
-        jnp.broadcast_to(value[None], (peers, *value.shape)), axis, 0, 0, tiled=True
+def halo_rows(matrix, full):
+    count = lax.axis_size("rows")
+    half = matrix.shape[3]
+    side = lax.axis_index("help")
+    block = jnp.stack([matrix[0, 2], matrix[0, 3], matrix[1, 1], matrix[1, 2]])
+    from_left = lax.ppermute(block, "rows", [(i, i + 1) for i in range(count - 1)])
+    from_right = lax.ppermute(block, "rows", [(i + 1, i) for i in range(count - 1)])
+    own_half = lax.dynamic_slice_in_dim(full, side * half, half, axis=2)
+    flipped = jnp.swapaxes(own_half, 2, 3)
+    zero = jnp.zeros_like(matrix[0, 0])
+    left = jnp.stack(
+        [
+            jnp.stack([zero, zero, from_left[0], from_left[1], flipped[0, 0]]),
+            jnp.stack([zero, from_left[2], from_left[3], flipped[0, 1], flipped[1, 0]]),
+        ]
     )
-
-
-def gather_directly(value, axis, dim):
-    return in_order(copy_for_each(value, axis), dim)
+    right = jnp.stack(
+        [
+            jnp.stack([flipped[0, 4], flipped[1, 3], from_right[0], from_right[1], zero]),
+            jnp.stack([flipped[1, 4], from_right[2], from_right[3], zero, zero]),
+        ]
+    )
+    return jnp.concatenate([left, matrix, right], axis=0)
 
 
 def band_square(matrix):
     row_count, slot_count, tile_rows, half_cols = matrix.shape
     band_reach = (slot_count - 1) // 2
-    extended = padded(matrix, (("rows", 0),), band_reach)
-    columns = gather_directly(matrix, "help", 3)
+    other = swap_help(matrix)
+    side = lax.axis_index("help")
+    columns = jnp.where(
+        side == 0,
+        jnp.concatenate([matrix, other], axis=3),
+        jnp.concatenate([other, matrix], axis=3),
+    )
+    extended = halo_rows(matrix, columns)
     result = jnp.zeros_like(matrix)
     for offset_k in range(-band_reach, band_reach + 1):
         left_tile = columns[:, offset_k + band_reach]

time: 100 us -> 105 us (1.050)
  other arithmetic: 0.64 us -> 11 us
  starting transfers between devices: 27.6 us -> 18.6 us
  blocking collectives: 5.84 us -> 0 us
  matrix products: 19.7 us -> 24.9 us
  local copies, waits for them, and re-layouts: 11 us -> 16 us
  waiting for transfers between devices: 34.6 us -> 33.2 us
    all_to_all x1 -> x0, blocking collectives: 5.84 us -> none  [copy_for_each(): lax.all_to_all(jnp.broadcast_to(value[None], (peers, *value.shape)), axis...]
    dot_general x10, matrix products: 19.7 us -> 24.9 us  [band_square(): jnp.einsum('rab,rtbc->rtac', left_tile, right_slab[:, low_slot:high_slot]...]
    all_to_all x1 -> x0, starting transfers between devices: 5.14 us -> none  [copy_for_each(): lax.all_to_all(jnp.broadcast_to(value[None], (peers, *value.shape)), axis...]
    slice x0 -> x4, local copies, waits for them, and re-layouts: none -> 4.4 us  [the longest x2 2.61 us: halo_rows(): from_left[0]]
    another operation x0 -> x6, other arithmetic: none -> 4.38 us  [the longest x3 3.41 us: halo_rows(): jnp.stack([jnp.stack([flipped[0, 4], flipped[1, 3], from_right[0], from_r...]
    another operation x0 -> x17, local copies, waits for them, and re-layouts: none -> 3.98 us  [the longest x1 1.08 us: halo_rows(): jnp.stack([jnp.stack([flipped[0, 4], flipped[1, 3], from_right[0], from_r...]
    unnamed x5 -> x24, local copies, waits for them, and re-layouts: 1.73 us -> 5.64 us
    ppermute x4 -> x6, starting transfers between devices: 22.5 us -> 18.6 us  [the longest x2 12.4 us: halo_rows(): lax.ppermute(block, 'rows', [(i + 1, i) for i in range(count - 1)])]
  transfers between devices with their start and end apart: 5 -> 6, of which waited for: 3 -> 4; matrix products, arithmetic and copies ran while one was open for 19% -> 6% of each run, Pallas kernels for 0% -> 0%
where the time goes in v1:
time: 105 us; the launch traced here: 104 us
  waiting for transfers between devices  33.2 us (32%)
  matrix products  24.9 us (24%)
  starting transfers between devices  18.6 us (18%)
  local copies, waits for them, and re-layouts  16 us (15%)
  other arithmetic  11 us (10%)
    dot_general x10, matrix products, band_square(): jnp.einsum('rab,rtbc->rtac', left_tile, right_slab[:, low_slot:high_slot]...  24.9 us
    ppermute x2, waiting for transfers between devices, halo_rows(): lax.ppermute(block, 'rows', [(i + 1, i) for i in range(count - 1)])  20.5 us
    ppermute x2, waiting for transfers between devices, halo_rows(): lax.ppermute(block, 'rows', [(i, i + 1) for i in range(count - 1)])  12.7 us
    ppermute x2, starting transfers between devices, halo_rows(): lax.ppermute(block, 'rows', [(i + 1, i) for i in range(count - 1)])  12.4 us
    ppermute x2, starting transfers between devices, halo_rows(): lax.ppermute(block, 'rows', [(i, i + 1) for i in range(count - 1)])  5.84 us
    unnamed x24, local copies, waits for them, and re-layouts  5.64 us
    another operation x3, other arithmetic, halo_rows(): jnp.stack([jnp.stack([flipped[0, 4], flipped[1, 3], from_right[0], from_r...  3.41 us
    slice x2, local copies, waits for them, and re-layouts, halo_rows(): from_left[0]  2.61 us
  transfers between devices with their start and end apart: 6, of which 4 were waited for; matrix products, arithmetic and copies ran while one was open for 6% of the time, Pallas kernels for 0%

profile of v1, /device:TPU:6, one launch (start us, length us, event | category | flops | bytes accessed | tf_op | source)
XLA Modules:
  0.0 104.1 jit_solution(5677490605559727864)
XLA Ops:
  0.8 1.6 %copy_multiply_fusion = f32[2,5,256,128]{3,2,0,1:T(8,128)S(1)} fusion(f32[2,5,256,128]{3,2,1,0:T(8,128)} %param.27, f32[2,5]{0,1:T(8,128)S(1)} %copy.4), kind=kLoop, calls=%fused_computation.34 | loop fusion | flops 327680 | bytes 2621480 | tf_op jit(solution)/shard_map/mul | solution.py:66
  3.4 10.5 %collective-permute-start.2 = (f32[4,256,128]{2,1,0:T(8,128)}, f32[4,256,128]{2,1,0:T(8,128)}, u32[]{:S(2)}, u32[]{:S(2)}) collective-permute-start(f32[4,256,128]{2,1,0:T(8,128)} %pad_maximum_fusion.11), channel_id=1, source_target_pairs={{2,0},{4,2},{6,4},{8,6},{10,8},{12,10},{14,12},{16,14},{18,16},{20... | collective-permute-start | bytes 1572872 | tf_op jit(solution)/shard_map/ppermute | solution.py:19
  13.9 1.9 %collective-permute-start = (f32[4,256,128]{2,1,0:T(8,128)}, f32[4,256,128]{2,1,0:T(8,128)}, u32[]{:S(2)}, u32[]{:S(2)}) collective-permute-start(f32[4,256,128]{2,1,0:T(8,128)} %pad_maximum_fusion.11), channel_id=1, source_target_pairs={{0,2},{2,4},{4,6},{6,8},{8,10},{10,12},{12,14},{14,16},{16,18},{18... | collective-permute-start | bytes 1572872 | tf_op jit(solution)/shard_map/ppermute | solution.py:18
  15.9 10.2 %collective-permute-done.2 = f32[4,256,128]{2,1,0:T(8,128)} collective-permute-done((f32[4,256,128]{2,1,0:T(8,128)}, f32[4,256,128]{2,1,0:T(8,128)}, u32[]{:S(2)}, u32[]{:S(2)}) %collective-permute-start.2) | collective-permute-done | bytes 524320 | tf_op jit(solution)/shard_map/ppermute | solution.py:19
  26.1 1.1 %fusion.83 = (f32[2,256,128]{2,1,0:T(8,128)S(1)}, f32[2,256,128]{2,1,0:T(8,128)S(1)}) fusion(f32[4,256,128]{2,1,0:T(8,128)} %collective-permute-done.2), kind=kLoop, calls=%fused_computation.122 | loop fusion | bytes 1048576 | tf_op jit(solution)/shard_map/slice | solution.py:32
  27.1 7.3 %collective-permute-done = f32[4,256,128]{2,1,0:T(8,128)} collective-permute-done((f32[4,256,128]{2,1,0:T(8,128)}, f32[4,256,128]{2,1,0:T(8,128)}, u32[]{:S(2)}, u32[]{:S(2)}) %collective-permute-start) | collective-permute-done | bytes 524320 | tf_op jit(solution)/shard_map/ppermute | solution.py:18
  34.4 1.9 %fusion.84 = (f32[2,256,128]{2,1,0:T(8,128)}, f32[2,256,128]{2,1,0:T(8,128)}) fusion(f32[4,256,128]{2,1,0:T(8,128)} %collective-permute-done), kind=kLoop, calls=%fused_computation.123 | loop fusion | bytes 1048576 | tf_op jit(solution)/shard_map/slice | solution.py:25
  36.7 1.4 %copy-done = f32[2,5,256,256]{3,2,0,1:T(8,128)} copy-done((f32[2,5,256,256]{3,2,0,1:T(8,128)}, f32[2,5,256,256]{3,2,0,1:T(8,128)S(1)}, u32[]{:S(2)}) %copy-start) | copy-done | bytes 2621464
  39.5 1.4 %copy-done.1 = f32[2,5,256,256]{3,2,0,1:T(8,128)S(1)} copy-done((f32[2,5,256,256]{3,2,0,1:T(8,128)S(1)}, f32[2,5,256,256]{3,2,0,1:T(8,128)}, u32[]{:S(2)}) %copy-start.1) | copy-done | bytes 2621464
  40.9 1.5 %fusion.50 = f32[2,3,256,128]{2,3,1,0:T(8,128)S(1)} fusion(f32[1,5,256,128]{3,2,1,0:T(8,128)S(1)} %get-tuple-element.187, f32[1,5,256,128]{3,2,1,0:T(8,128)S(1)} %get-tuple-element.176, f32[2,5,256,256]{3,2,0,1:T(8,128)S(1)} %copy-done.1), kind=kOutput, calls=%fused_computation.45 | convolution fusion | flops 604307456 | bytes 2621440 | tf_op jit(solution)/shard_map/rab,rtbc->rtac/dot_general | solution.py:55
  42.7 2.1 %fusion.23 = f32[2,5,256,128]{2,3,1,0:T(8,128)S(1)} fusion(f32[2,5,256,128]{2,3,1,0:T(8,128)S(1)} %scatter-add.26, f32[2,4,256,128]{3,2,0,1:T(8,128)S(1)} %get-tuple-element.158, f32[2,5,256,256]{3,2,0,1:T(8,128)S(1)} %copy-done.1), kind=kOutput, calls=%fused_computation.21 | convolution fusion | flops 805568512 | bytes 3670016 | tf_op jit(solution)/shard_map/rab,rtbc->rtac/dot_general | solution.py:55
  44.8 2.3 %fusion.8 = f32[2,5,256,128]{2,3,1,0:T(8,128)S(1)} fusion(f32[2,5,256,128]{2,3,1,0:T(8,128)S(1)} %fusion.23, f32[2,5,256,256]{3,2,0,1:T(8,128)S(1)} %copy-done.1, f32[2,5,256,128]{3,2,0,1:T(8,128)S(1)} %copy_multiply_fusion), kind=kOutput, calls=%fused_computation.12 | convolution fusion | flops 1006960640 | bytes 4456448 | tf_op jit(solution)/shard_map/rab,rtbc->rtac/dot_general | solution.py:55
  47.1 2.2 %constant_dynamic-update-slice_fusion.1 = (f32[2,5,256,128]{2,3,1,0:T(8,128)S(1)}, f32[2,4,256,128]{2,3,1,0:T(8,128)S(1)}) fusion(f32[2,5,256,128]{2,3,1,0:T(8,128)S(1)} %fusion.8, f32[2,5,256,256]{3,2,0,1:T(8,128)S(1)} %copy-done.1, f32[2,4,256,128]{3,2,0,1:T(8,128)S(1)} %get-tuple-element.157), kind=kOutput, calls=%fused_computation.111 | convolution fusion | flops 805568512 | bytes 4718592 | tf_op jit(solution)/shard_map/rab,rtbc->rtac/dot_general | solution.py:55
  49.3 1.5 %fusion.37 = f32[2,5,256,128]{2,3,1,0:T(8,128)S(1)} fusion(f32[2,5,256,128]{2,3,1,0:T(8,128)S(1)} %get-tuple-element.182, f32[2,4,256,128]{2,3,1,0:T(8,128)S(1)} %get-tuple-element.183, f32[2,5,256,256]{3,2,0,1:T(8,128)S(1)} %copy-done.1, f32[1,5,256,128]{3,2,0,1:T(8,128)S(1)} %get-tuple-element.175, f32[1,5,256,128]{3,2,0,1:T(8,128)S(1)} %get-tuple-element.186), kind=kOutput, calls=%fused_computation.40 | convolution fusion | flops 604372992 | bytes 3407872 | tf_op jit(solution)/shard_map/rab,rtbc->rtac/dot_general | solution.py:55
  51.7 1.9 %collective-permute-start.5 = (f32[4,256,128]{2,1,0:T(8,128)S(1)}, f32[4,256,128]{2,1,0:T(8,128)S(1)}, u32[]{:S(2)}, u32[]{:S(2)}) collective-permute-start(f32[4,256,128]{2,1,0:T(8,128)S(1)} %pad_maximum_fusion.12), channel_id=1, source_target_pairs={{2,0},{4,2},{6,4},{8,6},{10,8},{12,10},{14,12},{16,14},{18,16},{20... | collective-permute-start | bytes 1572872 | tf_op jit(solution)/shard_map/ppermute | solution.py:19
  53.7 3.9 %collective-permute-start.3 = (f32[4,256,128]{2,1,0:T(8,128)S(1)}, f32[4,256,128]{2,1,0:T(8,128)S(1)}, u32[]{:S(2)}, u32[]{:S(2)}) collective-permute-start(f32[4,256,128]{2,1,0:T(8,128)S(1)} %pad_maximum_fusion.12), channel_id=1, source_target_pairs={{0,2},{2,4},{4,6},{6,8},{8,10},{10,12},{12,14},{14,16},{16,18},{18... | collective-permute-start | bytes 1572872 | tf_op jit(solution)/shard_map/ppermute | solution.py:18
  57.6 10.4 %collective-permute-done.5 = f32[4,256,128]{2,1,0:T(8,128)S(1)} collective-permute-done((f32[4,256,128]{2,1,0:T(8,128)S(1)}, f32[4,256,128]{2,1,0:T(8,128)S(1)}, u32[]{:S(2)}, u32[]{:S(2)}) %collective-permute-start.5) | collective-permute-done | bytes 524320 | tf_op jit(solution)/shard_map/ppermute | solution.py:19
  68.7 5.4 %collective-permute-done.3 = f32[4,256,128]{2,1,0:T(8,128)S(1)} collective-permute-done((f32[4,256,128]{2,1,0:T(8,128)S(1)}, f32[4,256,128]{2,1,0:T(8,128)S(1)}, u32[]{:S(2)}, u32[]{:S(2)}) %collective-permute-start.3) | collective-permute-done | bytes 524320 | tf_op jit(solution)/shard_map/ppermute | solution.py:18
  74.8 2.1 %maximum_select_fusion.1 = f32[2,5,256,256]{2,3,1,0:T(8,128)S(1)} fusion(f32[2,5,256,128]{2,3,1,0:T(8,128)} %collective-permute-done.4, f32[2,5,256,128]{2,3,1,0:T(8,128)S(1)} %broadcast_multiply_fusion, pred[]{:T(512)S(6)} %eq.4), kind=kLoop, calls=%fused_computation.1 | loop fusion | flops 1966080 | bytes 5242881 | tf_op jit(solution)/shard_map/jit(_where)/select_n | solution.py:43
  77.1 1.4 %copy-done.2 = f32[2,5,256,256]{2,3,1,0:T(8,128)} copy-done((f32[2,5,256,256]{2,3,1,0:T(8,128)}, f32[2,5,256,256]{2,3,1,0:T(8,128)S(1)}, u32[]{:S(2)}) %copy-start.2) | copy-done | bytes 2621464
  79.4 1.0 fusion.61
  80.4 1.1 %copy.29 = f32[1,5,256,128]{2,3,1,0:T(8,128)} copy(f32[1,5,256,128]{3,2,1,0:T(8,128)S(1)} %get-tuple-element.178) | data formatting | bytes 1310720 | tf_op jit(solution)/shard_map/stack | solution.py:23
  81.4 2.1 %fusion.59 = (f32[1,5,256,128]{3,2,1,0:T(8,128)}, f32[1,5,256,128]{3,2,1,0:T(8,128)S(1)}) fusion(f32[2,256,128]{2,1,0:T(8,128)S(1)} %broadcast.199, f32[2,256,128]{2,1,0:T(8,128)} %get-tuple-element.165, f32[1,256,128]{2,1,0:T(8,128)} %get-tuple-element.141, f32[1,256,128]{2,1,0:T(8,128)} %get-tuple-element.146, f32[2,256,128]{2,1,0:T(8,128)} %get-tuple-element.167), kind=kLoop, calls=%fused_computation.63 | loop fusion | flops 655360 | bytes 2359296 | tf_op jit(solution)/shard_map/stack | solution.py:29
  83.5 2.5 %fusion.47 = f32[2,3,256,128]{2,3,1,0:T(8,128)S(1)} fusion(f32[1,5,256,128]{3,2,1,0:T(8,128)S(1)} %get-tuple-element.178, f32[1,5,256,128]{3,2,1,0:T(8,128)S(1)} %get-tuple-element.174, f32[2,5,256,256]{2,3,1,0:T(8,128)} %copy-done.2), kind=kOutput, calls=%fused_computation.44 | convolution fusion | flops 604307456 | bytes 2621440 | tf_op jit(solution)/shard_map/rab,rtbc->rtac/dot_general | solution.py:55
  86.2 1.0 copy-done.5
  87.1 2.3 %fusion.19 = f32[2,5,256,128]{2,3,1,0:T(8,128)S(1)} fusion(f32[2,5,256,128]{2,3,1,0:T(8,128)S(1)} %scatter-add.34, f32[2,5,256,128]{2,3,1,0:T(8,128)S(1)} %broadcast_multiply_fusion, f32[1,5,256,128]{2,3,1,0:T(8,128)S(1)} %copy-done.5, f32[2,5,256,256]{2,3,1,0:T(8,128)} %copy-done.2), kind=kOutput, calls=%fused_computation.17 | convolution fusion | flops 806060032 | bytes 4587520 | tf_op jit(solution)/shard_map/rab,rtbc->rtac/dot_general | solution.py:55
  89.4 3.5 %fusion.9 = f32[2,5,256,128]{2,3,1,0:T(8,128)} fusion(f32[2,5,256,128]{2,3,1,0:T(8,128)S(1)} %fusion.19, f32[2,5,256,128]{2,3,1,0:T(8,128)S(1)} %broadcast_multiply_fusion, f32[2,5,256,256]{2,3,1,0:T(8,128)} %copy-done.2), kind=kOutput, calls=%fused_computation.13 | convolution fusion | flops 1006960640 | bytes 4456448 | tf_op jit(solution)/shard_map/rab,rtbc->rtac/dot_general | solution.py:55
  93.0 1.1 %copy.32 = f32[1,5,256,128]{2,3,1,0:T(8,128)} copy(f32[1,5,256,128]{3,2,1,0:T(8,128)S(1)} %copy-done.3) | data formatting | bytes 1310720 | tf_op jit(solution)/shard_map/stack | solution.py:29
  94.0 3.7 %constant_dynamic-update-slice_fusion = (f32[2,5,256,128]{2,3,1,0:T(8,128)}, f32[2,4,256,128]{2,3,1,0:T(8,128)S(1)}) fusion(f32[2,5,256,128]{2,3,1,0:T(8,128)} %fusion.9, f32[2,5,256,256]{2,3,1,0:T(8,128)} %copy-done.2, f32[1,5,256,128]{2,3,1,0:T(8,128)} %copy.32, f32[2,5,256,128]{2,3,1,0:T(8,128)S(1)} %broadcast_multiply_fusion), kind=kOutput, calls=%fused_computation.110 | convolution fusion | flops 806060032 | bytes 5636096 | tf_op jit(solution)/shard_map/rab,rtbc->rtac/dot_general | solution.py:55
  97.7 3.4 %fusion.44 = f32[2,5,256,128]{2,3,1,0:T(8,128)} fusion(f32[2,5,256,128]{2,3,1,0:T(8,128)} %get-tuple-element.184, f32[1,5,256,128]{3,2,1,0:T(8,128)S(1)} %copy-done.6, f32[1,5,256,128]{3,2,1,0:T(8,128)S(1)} %copy-done.3, f32[2,4,256,128]{2,3,1,0:T(8,128)S(1)} %get-tuple-element.185, f32[2,5,256,256]{2,3,1,0:T(8,128)} %copy-done.2), kind=kOutput, calls=%fused_computation.43 | convolution fusion | flops 604504064 | bytes 3407872 | tf_op jit(solution)/shard_map/rab,rtbc->rtac/dot_general | solution.py:55
  101.1 1.6 %subtract_multiply_fusion = f32[2,5,256,128]{2,3,1,0:T(8,128)S(1)} fusion(f32[2,5,256,128]{2,3,1,0:T(8,128)} %fusion.44, f32[2,5]{1,0:T(2,128)S(1)} %get-tuple-element.180, f32[2,5,256,128]{2,3,1,0:T(8,128)S(1)} %fusion.37, f32[2,5]{1,0:T(2,128)S(1)} %get-tuple-element.181), kind=kLoop, calls=%fused_computation.35 | loop fusion | flops 1310720 | bytes 3932240 | tf_op jit(solution)/shard_map/mul | solution.py:73
  102.7 1.5 %copy.36 = f32[2,5,256,128]{3,2,1,0:T(8,128)} copy(f32[2,5,256,128]{2,3,1,0:T(8,128)S(1)} %subtract_multiply_fusion) | data formatting | bytes 2621440 | tf_op jit(solution)/shard_map/mul | solution.py:73
  (55 shorter events, 7.4 us)
Async XLA Ops:
  0.8 1.7 %copy-start.4 = (f32[2,5,256,128]{3,2,1,0:T(8,128)S(1)}, f32[2,5,256,128]{3,2,1,0:T(8,128)}, u32[]{:S(2)}) copy-start(f32[2,5,256,128]{3,2,1,0:T(8,128)} %param.27) | copy-start | bytes 3932164
  2.4 13.5 %copy-start.11 = (s32[2,2,5]{2,1,0:T(2,128)S(1)}, s32[2,2,5]{2,1,0:T(2,128)}, u32[]{:S(2)}) copy-start(s32[2,2,5]{2,1,0:T(2,128)} %param.29) | copy-start | bytes 244
  2.4 33.9 %collective-permute-start.1 = (f32[2,5,256,128]{3,2,0,1:T(8,128)S(1)}, f32[2,5,256,128]{3,2,0,1:T(8,128)S(1)}, u32[]{:S(2)}, u32[]{:S(2)}) collective-permute-start(f32[2,5,256,128]{3,2,0,1:T(8,128)S(1)} %copy_multiply_fusion), channel_id=1, source_target_pairs={{0,1},{1,0},{2,3},{3,2},{4,5},{5,4},{6,7},{7,6},{8,9},{9,8},{10,11... | collective-permute-start | bytes 3932168 | tf_op jit(solution)/shard_map/ppermute | solution.py:10
  3.4 22.6 %collective-permute-start.2 = (f32[4,256,128]{2,1,0:T(8,128)}, f32[4,256,128]{2,1,0:T(8,128)}, u32[]{:S(2)}, u32[]{:S(2)}) collective-permute-start(f32[4,256,128]{2,1,0:T(8,128)} %pad_maximum_fusion.11), channel_id=1, source_target_pairs={{2,0},{4,2},{6,4},{8,6},{10,8},{12,10},{14,12},{16,14},{18,16},{20... | collective-permute-start | bytes 1572872 | tf_op jit(solution)/shard_map/ppermute | solution.py:19
  13.9 20.5 %collective-permute-start = (f32[4,256,128]{2,1,0:T(8,128)}, f32[4,256,128]{2,1,0:T(8,128)}, u32[]{:S(2)}, u32[]{:S(2)}) collective-permute-start(f32[4,256,128]{2,1,0:T(8,128)} %pad_maximum_fusion.11), channel_id=1, source_target_pairs={{0,2},{2,4},{4,6},{6,8},{8,10},{10,12},{12,14},{14,16},{16,18},{18... | collective-permute-start | bytes 1572872 | tf_op jit(solution)/shard_map/ppermute | solution.py:18
  36.5 1.5 %copy-start = (f32[2,5,256,256]{3,2,0,1:T(8,128)}, f32[2,5,256,256]{3,2,0,1:T(8,128)S(1)}, u32[]{:S(2)}) copy-start(f32[2,5,256,256]{3,2,0,1:T(8,128)S(1)} %maximum_select_fusion) | copy-start | bytes 7864324
  38.1 1.0 copy-start.9
  38.1 1.0 copy-start.10
  38.8 0.8 copy-start.7
  39.2 1.7 %copy-start.1 = (f32[2,5,256,256]{3,2,0,1:T(8,128)S(1)}, f32[2,5,256,256]{3,2,0,1:T(8,128)}, u32[]{:S(2)}) copy-start(f32[2,5,256,256]{3,2,0,1:T(8,128)} %copy-done) | copy-start | bytes 7864324
  51.0 23.9 %collective-permute-start.4 = (f32[2,5,256,128]{2,3,1,0:T(8,128)S(1)}, f32[2,5,256,128]{2,3,1,0:T(8,128)}, u32[]{:S(2)}, u32[]{:S(2)}) collective-permute-start(f32[2,5,256,128]{2,3,1,0:T(8,128)S(1)} %broadcast_multiply_fusion), channel_id=1, source_target_pairs={{0,1},{1,0},{2,3},{3,2},{4,5},{5,4},{6,7},{7,6},{8,9},{9,8},{10,11... | collective-permute-start | bytes 3932168 | tf_op jit(solution)/shard_map/ppermute | solution.py:10
  51.7 16.2 %collective-permute-start.5 = (f32[4,256,128]{2,1,0:T(8,128)S(1)}, f32[4,256,128]{2,1,0:T(8,128)S(1)}, u32[]{:S(2)}, u32[]{:S(2)}) collective-permute-start(f32[4,256,128]{2,1,0:T(8,128)S(1)} %pad_maximum_fusion.12), channel_id=1, source_target_pairs={{2,0},{4,2},{6,4},{8,6},{10,8},{12,10},{14,12},{16,14},{18,16},{20... | collective-permute-start | bytes 1572872 | tf_op jit(solution)/shard_map/ppermute | solution.py:19
  53.7 20.4 %collective-permute-start.3 = (f32[4,256,128]{2,1,0:T(8,128)S(1)}, f32[4,256,128]{2,1,0:T(8,128)S(1)}, u32[]{:S(2)}, u32[]{:S(2)}) collective-permute-start(f32[4,256,128]{2,1,0:T(8,128)S(1)} %pad_maximum_fusion.12), channel_id=1, source_target_pairs={{0,2},{2,4},{4,6},{6,8},{8,10},{10,12},{12,14},{14,16},{16,18},{18... | collective-permute-start | bytes 1572872 | tf_op jit(solution)/shard_map/ppermute | solution.py:18
  77.0 1.5 %copy-start.2 = (f32[2,5,256,256]{2,3,1,0:T(8,128)}, f32[2,5,256,256]{2,3,1,0:T(8,128)S(1)}, u32[]{:S(2)}) copy-start(f32[2,5,256,256]{2,3,1,0:T(8,128)S(1)} %maximum_select_fusion.1) | copy-start | bytes 7864324
  78.5 0.9 copy-start.8
  86.0 1.1 %copy-start.5 = (f32[1,5,256,128]{2,3,1,0:T(8,128)S(1)}, f32[1,5,256,128]{2,3,1,0:T(8,128)}, u32[]{:S(2)}) copy-start(f32[1,5,256,128]{2,3,1,0:T(8,128)} %copy.29) | copy-start | bytes 1966084
  89.4 3.5 %copy-start.3 = (f32[1,5,256,128]{3,2,1,0:T(8,128)S(1)}, f32[1,5,256,128]{3,2,1,0:T(8,128)}, u32[]{:S(2)}) copy-start(f32[1,5,256,128]{3,2,1,0:T(8,128)} %get-tuple-element.177) | copy-start | bytes 1966084
  94.0 3.7 %copy-start.6 = (f32[1,5,256,128]{3,2,1,0:T(8,128)S(1)}, f32[1,5,256,128]{3,2,1,0:T(8,128)}, u32[]{:S(2)}) copy-start(f32[1,5,256,128]{3,2,1,0:T(8,128)} %get-tuple-element.173) | copy-start | bytes 1966084

commit v2 on v1

v2 whole, which is shorter than its diff:
```python
import jax
import jax.numpy as jnp
from jax import lax
from jax.sharding import PartitionSpec as P

STEPS = 2
DIAG = ((2, 3), (1, 2))
OFF = ((0, 1, 4), (0, 3, 4))
BLOCK = ((0, 2), (0, 3), (1, 1), (1, 2))


def swap_help(value):
    return lax.ppermute(value, "help", [(0, 1), (1, 0)])


def send_block(block):
    count = lax.axis_size("rows")
    from_left = lax.ppermute(block, "rows", [(i, i + 1) for i in range(count - 1)])
    from_right = lax.ppermute(block, "rows", [(i + 1, i) for i in range(count - 1)])
    return from_left, from_right


def full_tiles(matrix):
    half = matrix.shape[3]
    side = lax.axis_index("help")
    other = swap_help(matrix)
    full = jnp.where(
        side == 0,
        jnp.concatenate([matrix, other], axis=3),
        jnp.concatenate([other, matrix], axis=3),
    )
    own_half = lax.dynamic_slice_in_dim(full, side * half, half, axis=2)
    return full, jnp.swapaxes(own_half, 2, 3)


def right_tile(k, j, matrix, flipped, from_left, from_right):
    if abs(k - j) > 2:
        return None
    if k in (0, 1):
        return matrix[k, j - k + 2]
    if j in (0, 1):
        return flipped[j, k - j + 2]
    if k < 0:
        return from_left[2 * (k + 2) + (j + 2)]
    return from_right[2 * (k - 2) + (j - 2)]


def products(full, matrix, flipped, from_left, from_right, slots):
    zero = jnp.zeros_like(matrix[0, 0])
    rows = []
    for row, row_slots in enumerate(slots):
        by_k = []
        for offset in range(5):
            k = row + offset - 2
            tiles = []
            for slot in row_slots:
                tile = right_tile(k, row + slot - 2, matrix, flipped, from_left, from_right)
                tiles.append(zero if tile is None else tile)
            by_k.append(jnp.concatenate(tiles, axis=1))
        rows.append(jnp.stack(by_k))
    right = jnp.stack(rows)
    out = jnp.einsum("asxy,asyn->axn", full, right, precision=lax.Precision.HIGHEST)
    half = matrix.shape[3]
    return [
        [out[row, :, n * half : (n + 1) * half] for n in range(len(row_slots))]
        for row, row_slots in enumerate(slots)
    ]


def assemble(diag, off):
    tiles = {}
    for row in range(2):
        for slot, tile in zip(DIAG[row], diag[row]):
            tiles[(row, slot)] = tile
        for slot, tile in zip(OFF[row], off[row]):
            tiles[(row, slot)] = tile
    return jnp.stack([jnp.stack([tiles[(row, slot)] for slot in range(5)]) for row in range(2)])


def local(density, pattern, truncation):
    keep = [truncation[t].astype(jnp.float32) for t in range(STEPS)]
    matrix = density * pattern[:, :, None, None].astype(jnp.float32)
    block = jnp.stack([matrix[row, slot] for row, slot in BLOCK])
    halo = send_block(block)
    for step_index in range(STEPS):
        full, flipped = full_tiles(matrix)
        diag = products(full, matrix, flipped, None, None, DIAG)
        if step_index % 2 == 1:
            diag = [[2.0 * matrix[row, slot] - tile for slot, tile in zip(DIAG[row], diag[row])] for row in range(2)]
        diag = [[tile * keep[step_index][row, slot] for slot, tile in zip(DIAG[row], diag[row])] for row in range(2)]
        if step_index + 1 < STEPS:
            next_block = jnp.stack([diag[0][0], diag[0][1], diag[1][0], diag[1][1]])
            next_halo = send_block(next_block)
        off = products(full, matrix, flipped, halo[0], halo[1], OFF)
        if step_index % 2 == 1:
            off = [[2.0 * matrix[row, slot] - tile for slot, tile in zip(OFF[row], off[row])] for row in range(2)]
        off = [[tile * keep[step_index][row, slot] for slot, tile in zip(OFF[row], off[row])] for row in range(2)]
        matrix = assemble(diag, off)
        if step_index + 1 < STEPS:
            halo = next_halo
    return matrix


def solution(mesh):
    return jax.shard_map(
        local,
        mesh=mesh,
        in_specs=(P("rows", None, None, "help"), P("rows", None), P(None, "rows", None)),
        out_specs=P("rows", None, None, "help"),
        check_vma=False,
    )
```

time: 105 us -> 111 us (1.057)
  other arithmetic: 11 us -> 37.5 us
  waiting for transfers between devices: 33.2 us -> 8.44 us
  matrix products: 24.9 us -> 19.3 us
  local copies, waits for them, and re-layouts: 16 us -> 20.8 us
  starting transfers between devices: 18.6 us -> 22.6 us
    ppermute x4, waiting for transfers between devices: 33.2 us -> 8.44 us  [the longest x2 8.43 us: send_block(): lax.ppermute(block, 'rows', [(i, i + 1) for i in range(count - 1)])]
    unnamed x0 -> x20, other arithmetic: none -> 12.3 us
    squeeze x0 -> x8, local copies, waits for them, and re-layouts: none -> 7.25 us  [the longest x2 2.35 us: right_tile(): return from_right[2 * (k - 2) + (j - 2)]]
    another operation x6 -> x16, other arithmetic: 4.38 us -> 11.5 us  [the longest x4 5.35 us: assemble(): jnp.stack([tiles[row, slot] for slot in range(5)])]
    dot_general x10 -> x4, matrix products: 24.9 us -> 19.3 us  [products(): jnp.einsum('asxy,asyn->axn', full, right, precision=lax.Precision.HIGHEST)]
    ppermute x4, starting transfers between devices: 18.2 us -> 22.5 us  [the longest x2 16.7 us: send_block(): lax.ppermute(block, 'rows', [(i + 1, i) for i in range(count - 1)])]
    slice x0 -> x3, other arithmetic: none -> 3.98 us  [products(): out[row, :, n * half:(n + 1) * half]]
    another operation x17 -> x8, local copies, waits for them, and re-layouts: 3.98 us -> 0.73 us  [the longest x5 0.49 us: products(): rows.append(jnp.stack(by_k))]
  transfers between devices with their start and end apart: 6 -> 6, of which waited for: 4 -> 2; matrix products, arithmetic and copies ran while one was open for 6% -> 15% of each run, Pallas kernels for 0% -> 0%
where the time goes in v2:
time: 111 us; the launch traced here: 109 us
  other arithmetic  37.5 us (34%)
  starting transfers between devices  22.6 us (20%)
  local copies, waits for them, and re-layouts  20.8 us (19%)
  matrix products  19.3 us (17%)
  waiting for transfers between devices  8.44 us (8%)
    dot_general x4, matrix products, products(): jnp.einsum('asxy,asyn->axn', full, right, precision=lax.Precision.HIGHEST)  19.3 us
    ppermute x2, starting transfers between devices, send_block(): lax.ppermute(block, 'rows', [(i + 1, i) for i in range(count - 1)])  16.7 us
    unnamed x20, other arithmetic  12.3 us
    ppermute x2, waiting for transfers between devices, send_block(): lax.ppermute(block, 'rows', [(i, i + 1) for i in range(count - 1)])  8.43 us
    unnamed x47, local copies, waits for them, and re-layouts  6.8 us
    ppermute x2, starting transfers between devices, send_block(): lax.ppermute(block, 'rows', [(i, i + 1) for i in range(count - 1)])  5.72 us
    another operation x4, other arithmetic, assemble(): jnp.stack([tiles[row, slot] for slot in range(5)])  5.35 us
    select_n x2, other arithmetic, full_tiles(): jnp.where(side == 0, jnp.concatenate([matrix, other], axis=3), jnp.concat...  4.26 us
  transfers between devices with their start and end apart: 6, of which 2 were waited for; matrix products, arithmetic and copies ran while one was open for 15% of the time, Pallas kernels for 0%

profile of v2, /device:TPU:6, one launch (start us, length us, event | category | flops | bytes accessed | tf_op | source)
XLA Modules:
  0.0 109.4 jit_solution(6767469414360758943)
XLA Ops:
  0.7 1.5 %broadcast_multiply_fusion = f32[2,5,256,128]{3,2,1,0:T(8,128)S(1)} fusion(f32[2,5,256,128]{3,2,1,0:T(8,128)} %param.3, f32[2,5]{1,0:T(2,128)S(1)} %convert_element_type.16), kind=kLoop, calls=%fused_computation.37 | loop fusion | flops 327680 | bytes 2621480 | tf_op jit(solution)/shard_map/mul | solution.py:82
  3.9 3.8 %collective-permute-start.1 = (f32[4,256,128]{2,1,0:T(8,128)}, f32[4,256,128]{2,1,0:T(8,128)}, u32[]{:S(2)}, u32[]{:S(2)}) collective-permute-start(f32[4,256,128]{2,1,0:T(8,128)} %pad_maximum_fusion.13), channel_id=1, source_target_pairs={{0,2},{2,4},{4,6},{6,8},{8,10},{10,12},{12,14},{14,16},{16,18},{18... | collective-permute-start | bytes 1572872 | tf_op jit(solution)/shard_map/ppermute | solution.py:18
  7.8 8.6 %collective-permute-start.2 = (f32[4,256,128]{2,1,0:T(8,128)}, f32[4,256,128]{2,1,0:T(8,128)}, u32[]{:S(2)}, u32[]{:S(2)}) collective-permute-start(f32[4,256,128]{2,1,0:T(8,128)} %pad_maximum_fusion.13), channel_id=1, source_target_pairs={{2,0},{4,2},{6,4},{8,6},{10,8},{12,10},{14,12},{16,14},{18,16},{20... | collective-permute-start | bytes 1572872 | tf_op jit(solution)/shard_map/ppermute | solution.py:19
  18.5 8.2 %collective-permute-done.1 = f32[4,256,128]{2,1,0:T(8,128)} collective-permute-done((f32[4,256,128]{2,1,0:T(8,128)}, f32[4,256,128]{2,1,0:T(8,128)}, u32[]{:S(2)}, u32[]{:S(2)}) %collective-permute-start.1) | collective-permute-done | bytes 524320 | tf_op jit(solution)/shard_map/ppermute | solution.py:18
  26.6 1.1 %slice_bitcast_fusion.31 = (f32[256,128]{1,0:T(8,128)S(1)}, f32[256,128]{1,0:T(8,128)S(1)}, f32[256,128]{1,0:T(8,128)S(1)}, f32[256,128]{1,0:T(8,128)S(1)}) fusion(f32[4,256,128]{2,1,0:T(8,128)} %collective-permute-done.1), kind=kLoop, calls=%fused_computation.163 | loop fusion | bytes 1048576 | tf_op jit(solution)/shard_map/squeeze | solution.py:44
  28.1 1.2 %slice_bitcast_fusion.21 = (f32[256,128]{1,0:T(8,128)S(1)}, f32[256,128]{1,0:T(8,128)S(1)}, f32[256,128]{1,0:T(8,128)S(1)}, f32[256,128]{1,0:T(8,128)S(1)}) fusion(f32[4,256,128]{2,1,0:T(8,128)} %collective-permute-done.2), kind=kLoop, calls=%fused_computation.153 | loop fusion | bytes 1048576 | tf_op jit(solution)/shard_map/squeeze | solution.py:45
  29.5 2.1 %maximum_select_fusion = f32[2,5,256,256]{2,3,1,0:T(8,128)S(1)} fusion(f32[2,5,256,128]{2,3,1,0:T(8,128)} %collective-permute-done, f32[2,5,256,128]{2,3,1,0:T(8,128)S(1)} %copy-done.1, pred[]{:T(512)S(6)} %eq.4), kind=kLoop, calls=%fused_computation.8 | loop fusion | flops 1966080 | bytes 5242881 | tf_op jit(solution)/shard_map/jit(_where)/select_n | solution.py:27
  33.3 4.4 %fusion.19 = f32[2,256,384]{2,1,0:T(8,128)S(1)} fusion(f32[2,5,256,256]{2,3,1,0:T(8,128)S(1)} %maximum_select_fusion, f32[1,5,256,384]{3,2,1,0:T(8,128)S(1)} %bitcast.319, f32[1,5,256,384]{3,2,1,0:T(8,128)S(1)} %bitcast.321), kind=kOutput, calls=%fused_computation.23 | convolution fusion | flops 3020881920 | bytes 7340032 | tf_op jit(solution)/shard_map/asxy,asyn->axn/dot_general | solution.py:62
  38.6 1.4 %fusion.97 = (f32[1,256,128]{2,1,0:T(8,128)}, f32[1,256,128]{2,1,0:T(8,128)}, f32[1,256,128]{2,1,0:T(8,128)}, f32[5,256,128]{2,1,0:T(8,128)S(1)}) fusion(f32[2,256,384]{2,1,0:T(8,128)S(1)} %fusion.19, f32[]{:T(128)} %bitcast.61), kind=kLoop, calls=%fused_computation.216 | loop fusion | flops 32767 | bytes 1048580 | tf_op jit(solution)/shard_map/slice | solution.py:65
  40.0 1.7 %copy.47 = f32[1,256,128]{1,2,0:T(8,128)} copy(f32[1,256,128]{2,1,0:T(8,128)} %get-tuple-element.46) | data formatting | bytes 262144
  41.6 1.7 %copy.48 = f32[1,256,128]{1,2,0:T(8,128)} copy(f32[1,256,128]{2,1,0:T(8,128)} %get-tuple-element.45) | data formatting | bytes 262144
  43.3 1.7 %fusion.72 = (f32[5,256,256]{2,1,0:T(8,128)}, f32[5,256,256]{2,1,0:T(8,128)S(1)}) fusion(f32[5,256,256]{2,1,0:T(8,128)} %bitcast_dynamic-update-slice_fusion.7, f32[256,128]{1,0:T(8,128)} %get-tuple-element.23, f32[256,128]{1,0:T(8,128)} %get-tuple-element.24), kind=kLoop, calls=%fused_computation.105 | loop fusion | flops 65535 | bytes 786432
  45.0 1.7 %fusion.70 = (f32[5,256,256]{2,1,0:T(8,128)}, f32[5,256,256]{2,1,0:T(8,128)S(1)}) fusion(f32[5,256,256]{2,1,0:T(8,128)} %get-tuple-element.102, f32[256,128]{1,0:T(8,128)} %get-tuple-element.27, f32[256,128]{1,0:T(8,128)} %get-tuple-element.26, f32[5,256,256]{2,1,0:T(8,128)S(1)} %get-tuple-element.103), kind=kLoop, calls=%fused_computation.103 | loop fusion | flops 65536 | bytes 786432
  46.7 1.7 %fusion.68 = (f32[5,256,256]{2,1,0:T(8,128)}, f32[5,256,256]{2,1,0:T(8,128)S(1)}) fusion(f32[5,256,256]{2,1,0:T(8,128)} %get-tuple-element.100, f32[256,128]{1,0:T(8,128)} %get-tuple-element.28, f32[256,128]{1,0:T(8,128)} %get-tuple-element.25, f32[5,256,256]{2,1,0:T(8,128)S(1)} %get-tuple-element.101), kind=kLoop, calls=%fused_computation.101 | loop fusion | flops 65536 | bytes 786432
  49.2 5.8 %fusion.25 = f32[2,256,256]{1,2,0:T(8,128)S(1)} fusion(f32[2,5,256,256]{2,3,1,0:T(8,128)S(1)} %maximum_select_fusion, f32[1,5,256,256]{3,2,1,0:T(8,128)S(1)} %bitcast.325, f32[1,5,256,256]{3,2,1,0:T(8,128)} %bitcast.323), kind=kOutput, calls=%fused_computation.31 | convolution fusion | flops 2013921280 | bytes 5767168 | tf_op jit(solution)/shard_map/asxy,asyn->axn/dot_general | solution.py:62
  60.2 1.9 %collective-permute-start.4 = (f32[4,256,128]{2,1,0:T(8,128)}, f32[4,256,128]{2,1,0:T(8,128)}, u32[]{:S(2)}, u32[]{:S(2)}) collective-permute-start(f32[4,256,128]{2,1,0:T(8,128)} %pad_maximum_fusion.14), channel_id=1, source_target_pairs={{0,2},{2,4},{4,6},{6,8},{8,10},{10,12},{12,14},{14,16},{16,18},{18... | collective-permute-start | bytes 1572872 | tf_op jit(solution)/shard_map/ppermute | solution.py:18
  62.1 8.2 %collective-permute-start.5 = (f32[4,256,128]{2,1,0:T(8,128)}, f32[4,256,128]{2,1,0:T(8,128)}, u32[]{:S(2)}, u32[]{:S(2)}) collective-permute-start(f32[4,256,128]{2,1,0:T(8,128)} %pad_maximum_fusion.14), channel_id=1, source_target_pairs={{2,0},{4,2},{6,4},{8,6},{10,8},{12,10},{14,12},{16,14},{18,16},{20... | collective-permute-start | bytes 1572872 | tf_op jit(solution)/shard_map/ppermute | solution.py:19
  70.3 1.5 %fusion.86 = f32[5,256,128]{2,1,0:T(8,128)S(1)} fusion(f32[5,256,128]{2,1,0:T(8,128)S(1)} %get-tuple-element.9, f32[2,256,384]{2,1,0:T(8,128)} %copy-done.2, f32[]{:T(128)} %bitcast.64), kind=kLoop, calls=%fused_computation.141 | loop fusion | flops 32768 | bytes 262148
  71.8 1.5 %fusion.85 = f32[5,256,128]{2,1,0:T(8,128)S(1)} fusion(f32[5,256,128]{2,1,0:T(8,128)S(1)} %fusion.86, f32[2,256,384]{2,1,0:T(8,128)} %copy-done.2, f32[]{:T(128)} %bitcast.65), kind=kLoop, calls=%fused_computation.139 | loop fusion | flops 32768 | bytes 262148 | tf_op jit(solution)/shard_map/stack | solution.py:77
  75.2 1.2 %pad_maximum_fusion = f32[2,5,256,128]{2,3,1,0:T(8,128)} fusion(f32[1,5,256,128]{2,3,1,0:T(8,128)S(1)} %copy.16, f32[1,5,256,128]{2,3,1,0:T(8,128)S(1)} %bitcast.308), kind=kLoop, calls=%fused_computation.18 | loop fusion | flops 327680 | bytes 2621440 | tf_op jit(solution)/shard_map/stack | solution.py:77
  77.8 1.7 %copy.33 = f32[1,1,256,128]{3,2,1,0:T(8,128)} copy(f32[1,1,256,128]{2,3,1,0:T(8,128)} %get-tuple-element.48) | data formatting | bytes 262144 | tf_op jit(solution)/shard_map/slice | solution.py:40
  82.0 1.1 %slice_bitcast_fusion.7 = (f32[256,128]{1,0:T(8,128)S(1)}, f32[256,128]{1,0:T(8,128)S(1)}, f32[256,128]{1,0:T(8,128)S(1)}, f32[256,128]{1,0:T(8,128)S(1)}) fusion(f32[4,256,128]{2,1,0:T(8,128)} %collective-permute-done.5), kind=kLoop, calls=%fused_computation.131 | loop fusion | bytes 1048576 | tf_op jit(solution)/shard_map/squeeze | solution.py:45
  83.2 2.1 %maximum_select_fusion.1 = f32[2,5,256,256]{2,3,1,0:T(8,128)S(1)} fusion(f32[2,5,256,128]{2,3,1,0:T(8,128)} %collective-permute-done.3, f32[1,5,256,128]{2,3,1,0:T(8,128)S(1)} %copy.16, f32[1,5,256,128]{2,3,1,0:T(8,128)S(1)} %bitcast.310, pred[]{:T(512)S(6)} %eq.4), kind=kLoop, calls=%fused_computation.13 | loop fusion | flops 3276800 | bytes 5242881 | tf_op jit(solution)/shard_map/jit(_where)/select_n | solution.py:27
  85.6 4.6 %fusion.16 = f32[2,256,384]{2,1,0:T(8,128)S(1)} fusion(f32[2,5,256,256]{2,3,1,0:T(8,128)S(1)} %maximum_select_fusion.1, f32[1,5,256,384]{3,2,1,0:T(8,128)S(1)} %bitcast.320, f32[1,5,256,384]{3,2,1,0:T(8,128)S(1)} %bitcast.322), kind=kOutput, calls=%fused_computation.22 | convolution fusion | flops 3020881920 | bytes 7340032 | tf_op jit(solution)/shard_map/asxy,asyn->axn/dot_general | solution.py:62
  90.2 1.3 %fusion.96 = (f32[1,256,128]{2,1,0:T(8,128)S(1)}, f32[1,256,128]{2,1,0:T(8,128)S(1)}, f32[5,256,128]{2,1,0:T(8,128)}) fusion(f32[2,256,384]{2,1,0:T(8,128)S(1)} %fusion.16, f32[]{:T(128)} %bitcast.128, f32[1,5,256,128]{3,2,1,0:T(8,128)S(1)} %bitcast.314), kind=kLoop, calls=%fused_computation.215 | loop fusion | flops 98303 | bytes 917508 | tf_op jit(solution)/shard_map/slice | solution.py:65
  91.7 4.5 %fusion.22 = f32[2,256,256]{2,1,0:T(8,128)S(1)} fusion(f32[2,5,256,256]{2,3,1,0:T(8,128)S(1)} %maximum_select_fusion.1, f32[1,5,256,256]{3,2,1,0:T(8,128)S(1)} %bitcast.326, f32[1,5,256,256]{3,2,1,0:T(8,128)S(1)} %bitcast.324), kind=kOutput, calls=%fused_computation.30 | convolution fusion | flops 2013921280 | bytes 5767168 | tf_op jit(solution)/shard_map/asxy,asyn->axn/dot_general | solution.py:62
  96.2 1.4 %fusion.99 = (f32[1,256,128]{2,1,0:T(8,128)S(1)}, f32[1,256,128]{2,1,0:T(8,128)S(1)}, f32[5,256,128]{2,1,0:T(8,128)}) fusion(f32[2,256,256]{2,1,0:T(8,128)S(1)} %fusion.22, f32[5,256,128]{2,1,0:T(8,128)} %get-tuple-element.43, f32[]{:T(128)} %bitcast.130, f32[1,5,256,128]{3,2,1,0:T(8,128)S(1)} %bitcast.315), kind=kLoop, calls=%fused_computation.218 | loop fusion | flops 98304 | bytes 918016 | tf_op jit(solution)/shard_map/slice | solution.py:65
  98.0 3.3 %fusion.88 = (f32[1,256,128]{1,2,0:T(8,128)S(1)}, f32[1,256,128]{1,2,0:T(8,128)S(1)}, f32[1,256,128]{1,2,0:T(8,128)S(1)}, f32[1,256,128]{1,2,0:T(8,128)}) fusion(f32[1,256,128]{1,2,0:T(8,128)S(1)} %copy.55, f32[1,5,256,128]{2,3,1,0:T(8,128)S(1)} %bitcast.311, f32[]{:T(128)} %bitcast.123, f32[]{:T(128)} %bitcast.98, f32[1,256,128]{1,2,0:T(8,128)S(1)} %copy.53, ...), kind=kLoop, calls=%fused_computation.167 | loop fusion | flops 393216 | bytes 1572880 | tf_op jit(solution)/shard_map/mul | solution.py:90
  102.6 1.3 %fusion.78 = f32[5,256,128]{2,1,0:T(8,128)} fusion(f32[5,256,128]{2,1,0:T(8,128)} %get-tuple-element.65, f32[2,256,256]{2,1,0:T(8,128)S(1)} %fusion.22, f32[1,5,256,128]{3,2,1,0:T(8,128)S(1)} %bitcast.316, f32[]{:T(128)} %bitcast.132), kind=kLoop, calls=%fused_computation.114 | loop fusion | flops 98304 | bytes 393728
  104.0 1.9 %fusion.84 = (f32[5,256,128]{2,1,0:T(8,128)S(1)}, f32[5,256,128]{2,1,0:T(8,128)}) fusion(f32[5,256,128]{2,1,0:T(8,128)S(1)} %constant_dynamic-update-slice_fusion.8, f32[2,256,384]{2,1,0:T(8,128)S(1)} %fusion.16, f32[1,1,256,128]{3,2,1,0:T(8,128)S(1)} %copy-done.12, f32[]{:T(128)} %bitcast.125, f32[5,256,128]{2,1,0:T(8,128)} %fusion.78, f32[]{:T(128)} %bitcast.134, ...), kind=kLoop, calls=%fused_computation.123 | loop fusion | flops 196608 | bytes 787456 | tf_op jit(solution)/shard_map/stack | solution.py:77
  105.9 1.2 %fusion.74 = f32[5,256,128]{2,1,0:T(8,128)} fusion(f32[5,256,128]{2,1,0:T(8,128)} %get-tuple-element.40, f32[2,256,384]{2,1,0:T(8,128)S(1)} %fusion.16, f32[1,5,256,128]{3,2,1,0:T(8,128)S(1)} %bitcast.318, f32[]{:T(128)} %bitcast.136), kind=kLoop, calls=%fused_computation.108 | loop fusion | flops 98304 | bytes 393728 | tf_op jit(solution)/shard_map/stack | solution.py:77
  107.1 2.2 %pad_maximum_fusion.1 = f32[2,5,256,128]{3,2,1,0:T(8,128)} fusion(f32[1,5,256,128]{3,2,1,0:T(8,128)} %bitcast.137, f32[1,5,256,128]{3,2,1,0:T(8,128)S(1)} %bitcast.327), kind=kLoop, calls=%fused_computation.19 | loop fusion | flops 327680 | bytes 2621440 | tf_op jit(solution)/shard_map/stack | solution.py:77
  (106 shorter events, 21.1 us)
Async XLA Ops:
  3.1 13.8 %copy-start.14 = (s32[2,2,5]{2,1,0:T(2,128)S(1)}, s32[2,2,5]{2,1,0:T(2,128)}, u32[]{:S(2)}) copy-start(s32[2,2,5]{2,1,0:T(2,128)} %param.5) | copy-start | bytes 244
  3.9 22.7 %collective-permute-start.1 = (f32[4,256,128]{2,1,0:T(8,128)}, f32[4,256,128]{2,1,0:T(8,128)}, u32[]{:S(2)}, u32[]{:S(2)}) collective-permute-start(f32[4,256,128]{2,1,0:T(8,128)} %pad_maximum_fusion.13), channel_id=1, source_target_pairs={{0,2},{2,4},{4,6},{6,8},{8,10},{10,12},{12,14},{14,16},{16,18},{18... | collective-permute-start | bytes 1572872 | tf_op jit(solution)/shard_map/ppermute | solution.py:18
  7.8 20.3 %collective-permute-start.2 = (f32[4,256,128]{2,1,0:T(8,128)}, f32[4,256,128]{2,1,0:T(8,128)}, u32[]{:S(2)}, u32[]{:S(2)}) collective-permute-start(f32[4,256,128]{2,1,0:T(8,128)} %pad_maximum_fusion.13), channel_id=1, source_target_pairs={{2,0},{4,2},{6,4},{8,6},{10,8},{12,10},{14,12},{16,14},{18,16},{20... | collective-permute-start | bytes 1572872 | tf_op jit(solution)/shard_map/ppermute | solution.py:19
  16.8 11.2 %copy-start = (f32[2,5,256,128]{2,3,1,0:T(8,128)}, f32[2,5,256,128]{2,3,1,0:T(8,128)S(1)}, u32[]{:S(2)}) copy-start(f32[2,5,256,128]{2,3,1,0:T(8,128)S(1)} %copy.5) | copy-start | bytes 3932164
  16.8 12.6 %collective-permute-start = (f32[2,5,256,128]{2,3,1,0:T(8,128)S(1)}, f32[2,5,256,128]{2,3,1,0:T(8,128)}, u32[]{:S(2)}, u32[]{:S(2)}) collective-permute-start(f32[2,5,256,128]{2,3,1,0:T(8,128)S(1)} %copy.5), channel_id=1, source_target_pairs={{0,1},{1,0},{2,3},{3,2},{4,5},{5,4},{6,7},{7,6},{8,9},{9,8},{10,11... | collective-permute-start | bytes 3932168 | tf_op jit(solution)/shard_map/ppermute | solution.py:13
  28.0 1.6 %copy-start.1 = (f32[2,5,256,128]{2,3,1,0:T(8,128)S(1)}, f32[2,5,256,128]{2,3,1,0:T(8,128)}, u32[]{:S(2)}) copy-start(f32[2,5,256,128]{2,3,1,0:T(8,128)} %copy-done) | copy-start | bytes 3932164
  37.7 0.9 copy-start.2
  43.3 5.2 %copy-start.8 = (f32[256,128]{1,0:T(8,128)S(1)}, f32[256,128]{1,0:T(8,128)}, u32[]{:S(2)}) copy-start(f32[256,128]{1,0:T(8,128)} %get-tuple-element.21) | copy-start | bytes 393220
  43.3 5.2 %copy-start.9 = (f32[256,128]{1,0:T(8,128)S(1)}, f32[256,128]{1,0:T(8,128)}, u32[]{:S(2)}) copy-start(f32[256,128]{1,0:T(8,128)} %get-tuple-element.22) | copy-start | bytes 393220
  49.2 5.8 %copy-start.11 = (f32[1,256,128]{1,2,0:T(8,128)S(1)}, f32[1,256,128]{1,2,0:T(8,128)}, u32[]{:S(2)}) copy-start(f32[1,256,128]{1,2,0:T(8,128)} %copy.47) | copy-start | bytes 393220
  49.2 6.5 %copy-start.10 = (f32[1,256,128]{1,2,0:T(8,128)S(1)}, f32[1,256,128]{1,2,0:T(8,128)}, u32[]{:S(2)}) copy-start(f32[1,256,128]{1,2,0:T(8,128)} %copy.48) | copy-start | bytes 393220
  59.4 15.1 %copy-start.13 = (f32[1,256,128]{2,1,0:T(8,128)S(1)}, f32[1,256,128]{2,1,0:T(8,128)}, u32[]{:S(2)}) copy-start(f32[1,256,128]{2,1,0:T(8,128)} %get-tuple-element.44) | copy-start | bytes 393220
  60.2 19.5 %collective-permute-start.4 = (f32[4,256,128]{2,1,0:T(8,128)}, f32[4,256,128]{2,1,0:T(8,128)}, u32[]{:S(2)}, u32[]{:S(2)}) collective-permute-start(f32[4,256,128]{2,1,0:T(8,128)} %pad_maximum_fusion.14), channel_id=1, source_target_pairs={{0,2},{2,4},{4,6},{6,8},{8,10},{10,12},{12,14},{14,16},{16,18},{18... | collective-permute-start | bytes 1572872 | tf_op jit(solution)/shard_map/ppermute | solution.py:18
  62.1 19.8 %collective-permute-start.5 = (f32[4,256,128]{2,1,0:T(8,128)}, f32[4,256,128]{2,1,0:T(8,128)}, u32[]{:S(2)}, u32[]{:S(2)}) collective-permute-start(f32[4,256,128]{2,1,0:T(8,128)} %pad_maximum_fusion.14), channel_id=1, source_target_pairs={{2,0},{4,2},{6,4},{8,6},{10,8},{12,10},{14,12},{16,14},{18,16},{20... | collective-permute-start | bytes 1572872 | tf_op jit(solution)/shard_map/ppermute | solution.py:19
  76.4 6.8 %collective-permute-start.3 = (f32[2,5,256,128]{2,3,1,0:T(8,128)}, f32[2,5,256,128]{2,3,1,0:T(8,128)}, u32[]{:S(2)}, u32[]{:S(2)}) collective-permute-start(f32[2,5,256,128]{2,3,1,0:T(8,128)} %pad_maximum_fusion), channel_id=1, source_target_pairs={{0,1},{1,0},{2,3},{3,2},{4,5},{5,4},{6,7},{7,6},{8,9},{9,8},{10,11... | collective-permute-start | bytes 3932168 | tf_op jit(solution)/shard_map/ppermute | solution.py:13
  80.9 0.9 copy-start.3
  80.9 1.0 copy-start.4
  80.9 1.0 copy-start.5
  90.1 1.4 %copy-start.6 = (f32[256,128]{1,0:T(8,128)S(1)}, f32[256,128]{1,0:T(8,128)}, u32[]{:S(2)}) copy-start(f32[256,128]{1,0:T(8,128)} %get-tuple-element.58) | copy-start | bytes 393220
  90.1 1.4 %copy-start.7 = (f32[256,128]{1,0:T(8,128)S(1)}, f32[256,128]{1,0:T(8,128)}, u32[]{:S(2)}) copy-start(f32[256,128]{1,0:T(8,128)} %get-tuple-element.59) | copy-start | bytes 393220
  101.2 2.7 %copy-start.12 = (f32[1,1,256,128]{3,2,1,0:T(8,128)S(1)}, f32[1,1,256,128]{3,2,1,0:T(8,128)}, u32[]{:S(2)}) copy-start(f32[1,1,256,128]{3,2,1,0:T(8,128)} %copy.33) | copy-start | bytes 393220

commit v3 on v1

v3 whole, which is shorter than its diff:
```python
import functools

import jax
import jax.numpy as jnp
from jax import lax
from jax.experimental import pallas as pl
from jax.experimental.pallas import tpu as pltpu
from jax.sharding import PartitionSpec as P


STEPS = 2
DIAG = ((0, 2), (0, 3), (1, 1), (1, 2))
OFF = ((0, 0), (0, 1), (0, 4), (1, 0), (1, 3), (1, 4))
CONTRACT = (((1,), (0,)), ((), ()))
CONTRACT_T = (((1,), (1,)), ((), ()))


def swap_help(value):
    return lax.ppermute(value, "help", [(0, 1), (1, 0)])


def send_block(block):
    count = lax.axis_size("rows")
    from_left = lax.ppermute(block, "rows", [(i, i + 1) for i in range(count - 1)])
    from_right = lax.ppermute(block, "rows", [(i + 1, i) for i in range(count - 1)])
    return from_left, from_right


def dot(a, b, dims):
    return lax.dot_general(a, b, dims, precision=lax.Precision.HIGHEST, preferred_element_type=jnp.float32)


def band_kernel(tiles, odd, side_ref, keep_ref, mine_ref, other_ref, *rest):
    if len(rest) == 3:
        left_ref, right_ref, out_ref = rest
    else:
        left_ref = right_ref = None
        (out_ref,) = rest
    half = mine_ref.shape[3]
    side = side_ref[0]
    own = pl.ds(pl.multiple_of(side * half, half), half)
    far = pl.ds(pl.multiple_of((1 - side) * half, half), half)
    for index, (row, slot) in enumerate(tiles):
        col = row + slot - 2
        acc = jnp.zeros(out_ref.shape[1:], jnp.float32)
        for k in range(max(row, col) - 2, min(row, col) + 3):
            lm = mine_ref[row, k - row + 2]
            lo = other_ref[row, k - row + 2]
            if k in (0, 1) or col not in (0, 1):
                if k in (0, 1):
                    src, a, b = mine_ref, k, col - k + 2
                elif k < 0:
                    src, a, b = left_ref, 0, 2 * (k + 2) + (col + 2)
                else:
                    src, a, b = right_ref, 0, 2 * (k - 2) + (col - 2)
                if src is mine_ref:
                    r_own = src[a, b, own, :]
                    r_far = src[a, b, far, :]
                else:
                    r_own = src[b, own, :]
                    r_far = src[b, far, :]
                acc += dot(lm, r_own, CONTRACT) + dot(lo, r_far, CONTRACT)
            else:
                s = k - col + 2
                acc += dot(lm, mine_ref[col, s, own, :], CONTRACT_T)
                acc += dot(lo, other_ref[col, s, own, :], CONTRACT_T)
        if odd:
            acc = 2.0 * mine_ref[row, slot] - acc
        out_ref[index] = acc * keep_ref[row, slot]


def band_call(tiles, odd, side, keep, mine, other, halo=None):
    smem = pl.BlockSpec(memory_space=pltpu.SMEM)
    vmem = pl.BlockSpec(memory_space=pltpu.VMEM)
    args = [side, keep, mine, other] + ([] if halo is None else list(halo))
    return pl.pallas_call(
        functools.partial(band_kernel, tiles, odd),
        out_shape=jax.ShapeDtypeStruct((len(tiles),) + mine.shape[2:], jnp.float32),
        in_specs=[smem, smem] + [vmem] * (len(args) - 2),
        out_specs=vmem,
    )(*args)


def assemble(diag, off):
    tiles = {}
    for index, key in enumerate(DIAG):
        tiles[key] = diag[index]
    for index, key in enumerate(OFF):
        tiles[key] = off[index]
    return jnp.stack([jnp.stack([tiles[(row, slot)] for slot in range(5)]) for row in range(2)])


def purify(density, pattern, truncation):
    side = lax.axis_index("help").astype(jnp.int32).reshape(1)
    matrix = density * pattern[:, :, None, None].astype(jnp.float32)
    halo = send_block(jnp.stack([matrix[row, slot] for row, slot in DIAG]))
    for step_index in range(STEPS):
        keep = truncation[step_index].astype(jnp.float32)
        odd = step_index % 2 == 1
        other = swap_help(matrix)
        diag = band_call(DIAG, odd, side, keep, matrix, other)
        if step_index + 1 < STEPS:
            next_halo = send_block(diag)
        off = band_call(OFF, odd, side, keep, matrix, other, halo)
        matrix = assemble(diag, off)
        if step_index + 1 < STEPS:
            halo = next_halo
    return matrix


def solution(mesh):
    return jax.shard_map(
        purify,
        mesh=mesh,
        in_specs=(P("rows", None, None, "help"), P("rows", None), P(None, "rows", None)),
        out_specs=P("rows", None, None, "help"),
        check_vma=False,
    )
```

time: 105 us -> 93.5 us (0.89)
  Pallas kernels: 0 us -> 27.4 us
  matrix products: 24.9 us -> 0 us
  other arithmetic: 11 us -> 4.19 us
  local copies, waits for them, and re-layouts: 16 us -> 10.1 us
  waiting for transfers between devices: 33.2 us -> 28.2 us
  starting transfers between devices: 18.6 us -> 22.8 us
    pallas_call x0 -> x4, Pallas kernels: none -> 27.4 us  [band_call(): pl.pallas_call(functools.partial(band_kernel, tiles, odd), out_shape=jax....]
    dot_general x10 -> x0, matrix products: 24.9 us -> none  [band_square(): jnp.einsum('rab,rtbc->rtac', left_tile, right_slab[:, low_slot:high_slot]...]
    ppermute x4, waiting for transfers between devices: 33.2 us -> 28.2 us  [the longest x2 17.7 us: send_block(): lax.ppermute(block, 'rows', [(i, i + 1) for i in range(count - 1)])]
    ppermute x4, starting transfers between devices: 18.2 us -> 22.6 us  [the longest x2 18.8 us: send_block(): lax.ppermute(block, 'rows', [(i + 1, i) for i in range(count - 1)])]
    another operation x17 -> x1, local copies, waits for them, and re-layouts: 3.98 us -> 0.04 us  [purify(): halo = send_block(jnp.stack([matrix[row, slot] for row, slot in DIAG]))]
    another operation x6, other arithmetic: 4.38 us -> 1.46 us  [the longest x5 1.42 us: assemble(): jnp.stack([jnp.stack([tiles[row, slot] for slot in range(5)]) for row in...]
    select_n x2 -> x0, other arithmetic: 2.42 us -> none  [band_square(): jnp.where(side == 0, jnp.concatenate([matrix, other], axis=3), jnp.concat...]
    mul x3 -> x1, other arithmetic: 3.36 us -> 1.49 us  [purify(): matrix = density * pattern[:, :, None, None].astype(jnp.float32)]
  transfers between devices with their start and end apart: 6 -> 6, of which waited for: 4 -> 4; matrix products, arithmetic and copies ran while one was open for 6% -> 1% of each run, Pallas kernels for 0% -> 0%
where the time goes in v3:
time: 93.5 us; the launch traced here: 93 us
  waiting for transfers between devices  28.2 us (30%)
  Pallas kernels  27.4 us (29%)
  starting transfers between devices  22.8 us (24%)
  local copies, waits for them, and re-layouts  10.1 us (11%)
  other arithmetic  4.19 us (4%)
    pallas_call x4, Pallas kernels, band_call(): pl.pallas_call(functools.partial(band_kernel, tiles, odd), out_shape=jax....  27.4 us
    ppermute x2, starting transfers between devices, send_block(): lax.ppermute(block, 'rows', [(i + 1, i) for i in range(count - 1)])  18.8 us
    ppermute x2, waiting for transfers between devices, send_block(): lax.ppermute(block, 'rows', [(i, i + 1) for i in range(count - 1)])  17.7 us
    ppermute x2, waiting for transfers between devices, send_block(): lax.ppermute(block, 'rows', [(i + 1, i) for i in range(count - 1)])  10.5 us
    slice x4, local copies, waits for them, and re-layouts, assemble(): tiles[key] = off[index]  4.1 us
    unnamed x16, local copies, waits for them, and re-layouts  3.85 us
    ppermute x2, starting transfers between devices, send_block(): lax.ppermute(block, 'rows', [(i, i + 1) for i in range(count - 1)])  3.83 us
    slice x2, local copies, waits for them, and re-layouts, assemble(): tiles[key] = diag[index]  2.13 us
  transfers between devices with their start and end apart: 6, of which 4 were waited for; matrix products, arithmetic and copies ran while one was open for 1% of the time, Pallas kernels for 0%

profile of v3, /device:TPU:6, one launch (start us, length us, event | category | flops | bytes accessed | tf_op | source)
XLA Modules:
  0.0 93.0 jit_solution(3458567884740487617)
XLA Ops:
  0.0 0.7 convert_element_type.18
  0.7 1.5 %broadcast_multiply_fusion.mine_ref = f32[2,5,256,128]{3,2,1,0:T(8,128)S(1)} fusion(f32[2,5,256,128]{3,2,1,0:T(8,128)} %param.3, f32[2,5]{1,0:T(2,128)S(1)} %convert_element_type.18), kind=kLoop, calls=%fused_computation.6 | loop fusion | flops 327680 | bytes 2621480 | tf_op jit(solution)/shard_map/mul | solution.py:95
  2.2 0.0 copy-start
  2.2 0.0 copy-start.7
  2.2 0.1 collective-permute-start
  2.4 10.5 %collective-permute-start.2 = (f32[4,256,128]{2,1,0:T(8,128)S(1)}, f32[4,256,128]{2,1,0:T(8,128)}, u32[]{:S(2)}, u32[]{:S(2)}) collective-permute-start(f32[4,256,128]{2,1,0:T(8,128)S(1)} %pad_maximum_fusion.2), channel_id=1, source_target_pairs={{2,0},{4,2},{6,4},{8,6},{10,8},{12,10},{14,12},{16,14},{18,16},{20... | collective-permute-start | bytes 1572872 | tf_op jit(solution)/shard_map/ppermute | solution.py:25
  12.9 1.9 %collective-permute-start.1 = (f32[4,256,128]{2,1,0:T(8,128)S(1)}, f32[4,256,128]{2,1,0:T(8,128)}, u32[]{:S(2)}, u32[]{:S(2)}) collective-permute-start(f32[4,256,128]{2,1,0:T(8,128)S(1)} %pad_maximum_fusion.2), channel_id=1, source_target_pairs={{0,2},{2,4},{4,6},{6,8},{8,10},{10,12},{12,14},{14,16},{16,18},{18... | collective-permute-start | bytes 1572872 | tf_op jit(solution)/shard_map/ppermute | solution.py:24
  14.8 0.6 convert_bitcast_fusion
  15.4 9.3 %collective-permute-done.2.rest_1_ = f32[4,256,128]{2,1,0:T(8,128)} collective-permute-done((f32[4,256,128]{2,1,0:T(8,128)S(1)}, f32[4,256,128]{2,1,0:T(8,128)}, u32[]{:S(2)}, u32[]{:S(2)}) %collective-permute-start.2) | collective-permute-done | bytes 524320 | tf_op jit(solution)/shard_map/ppermute | solution.py:25
  24.7 8.4 %collective-permute-done.1.rest_0_ = f32[4,256,128]{2,1,0:T(8,128)} collective-permute-done((f32[4,256,128]{2,1,0:T(8,128)S(1)}, f32[4,256,128]{2,1,0:T(8,128)}, u32[]{:S(2)}, u32[]{:S(2)}) %collective-permute-start.1) | collective-permute-done | bytes 524320 | tf_op jit(solution)/shard_map/ppermute | solution.py:24
  33.2 1.1 %copy-done.2 = f32[2,5,256,128]{3,2,1,0:T(8,128)} copy-done((f32[2,5,256,128]{3,2,1,0:T(8,128)}, f32[2,5,256,128]{3,2,1,0:T(8,128)S(1)}, u32[]{:S(2)}) %copy-start.2) | copy-done | bytes 1310744
  34.2 7.2 %shard_map.37 = f32[6,256,128]{2,1,0:T(8,128)} custom-call(s32[1]{0:T(128)} %bitcast.side_ref, f32[2,5]{1,0:T(2,128)} %get-tuple-element.21.keep_ref, f32[2,5,256,128]{3,2,1,0:T(8,128)} %copy-done, f32[2,5,256,128]{3,2,1,0:T(8,128)} %copy-done.2, f32[4,256,128]{2,1,0:T(8,128)} %collective-permute-done.1.rest_0_, f32[4,256,128]{2,1,0:T(8,128)} %collective-permute-done.2.rest_1_), custom_call_target="tpu_custom_call" | custom-call | tf_op jit(solution)/shard_map/pallas_call | solution.py:76
  41.4 1.0 %fusion.3 = (f32[1,256,128]{2,1,0:T(8,128)S(1)}, f32[1,256,128]{2,1,0:T(8,128)S(1)}) fusion(f32[6,256,128]{2,1,0:T(8,128)} %shard_map.37), kind=kLoop, calls=%fused_computation.17 | loop fusion | bytes 524288 | tf_op jit(solution)/shard_map/slice | solution.py:89
  42.4 1.1 %fusion.2 = (f32[2,256,128]{2,1,0:T(8,128)S(1)}, f32[2,256,128]{2,1,0:T(8,128)S(1)}) fusion(f32[6,256,128]{2,1,0:T(8,128)} %shard_map.37), kind=kLoop, calls=%fused_computation.16 | loop fusion | bytes 1048576 | tf_op jit(solution)/shard_map/slice | solution.py:89
  43.5 6.5 %shard_map.38 = f32[4,256,128]{2,1,0:T(8,128)} custom-call(s32[1]{0:T(128)} %bitcast.side_ref, f32[2,5]{1,0:T(2,128)} %get-tuple-element.21.keep_ref, f32[2,5,256,128]{3,2,1,0:T(8,128)} %copy-done, f32[2,5,256,128]{3,2,1,0:T(8,128)} %copy-done.2), custom_call_target="tpu_custom_call" | custom-call | tf_op jit(solution)/shard_map/pallas_call | solution.py:76
  50.0 1.1 %fusion.5 = (f32[2,256,128]{2,1,0:T(8,128)S(1)}, f32[2,256,128]{2,1,0:T(8,128)S(1)}) fusion(f32[4,256,128]{2,1,0:T(8,128)} %shard_map.38), kind=kLoop, calls=%fused_computation.19 | loop fusion | bytes 1048576 | tf_op jit(solution)/shard_map/slice | solution.py:87
  51.1 0.1 maximum_bitcast_fusion
  51.2 0.1 pad_maximum_fusion.mine_ref
  51.3 0.1 collective-permute-start.3
  51.4 0.9 copy-done.4
  52.3 1.9 %collective-permute-start.4 = (f32[4,256,128]{2,1,0:T(8,128)S(1)}, f32[4,256,128]{2,1,0:T(8,128)S(1)}, u32[]{:S(2)}, u32[]{:S(2)}) collective-permute-start(f32[4,256,128]{2,1,0:T(8,128)S(1)} %copy-done.4), channel_id=1, source_target_pairs={{0,2},{2,4},{4,6},{6,8},{8,10},{10,12},{12,14},{14,16},{16,18},{18... | collective-permute-start | bytes 1572872 | tf_op jit(solution)/shard_map/ppermute | solution.py:24
  54.2 8.3 %collective-permute-start.5 = (f32[4,256,128]{2,1,0:T(8,128)S(1)}, f32[4,256,128]{2,1,0:T(8,128)S(1)}, u32[]{:S(2)}, u32[]{:S(2)}) collective-permute-start(f32[4,256,128]{2,1,0:T(8,128)S(1)} %copy-done.4), channel_id=1, source_target_pairs={{2,0},{4,2},{6,4},{8,6},{10,8},{12,10},{14,12},{16,14},{18,16},{20... | collective-permute-start | bytes 1572872 | tf_op jit(solution)/shard_map/ppermute | solution.py:25
  62.5 9.3 %collective-permute-done.4.rest_0_ = f32[4,256,128]{2,1,0:T(8,128)S(1)} collective-permute-done((f32[4,256,128]{2,1,0:T(8,128)S(1)}, f32[4,256,128]{2,1,0:T(8,128)S(1)}, u32[]{:S(2)}, u32[]{:S(2)}) %collective-permute-start.4) | collective-permute-done | bytes 524320 | tf_op jit(solution)/shard_map/ppermute | solution.py:24
  71.8 1.2 %collective-permute-done.5.rest_1_ = f32[4,256,128]{2,1,0:T(8,128)S(1)} collective-permute-done((f32[4,256,128]{2,1,0:T(8,128)S(1)}, f32[4,256,128]{2,1,0:T(8,128)S(1)}, u32[]{:S(2)}, u32[]{:S(2)}) %collective-permute-start.5) | collective-permute-done | bytes 524320 | tf_op jit(solution)/shard_map/ppermute | solution.py:25
  73.0 0.8 copy-done.6
  73.8 1.1 %copy-done.3 = f32[2,5,256,128]{3,2,1,0:T(8,128)} copy-done((f32[2,5,256,128]{3,2,1,0:T(8,128)}, f32[2,5,256,128]{3,2,1,0:T(8,128)S(1)}, u32[]{:S(2)}) %copy-start.3) | copy-done | bytes 1310744
  74.9 7.2 %shard_map.39 = f32[6,256,128]{2,1,0:T(8,128)} custom-call(s32[1]{0:T(128)} %bitcast.side_ref, f32[2,5]{1,0:T(2,128)} %get-tuple-element.22.keep_ref, f32[2,5,256,128]{3,2,1,0:T(8,128)} %copy-done.1, f32[2,5,256,128]{3,2,1,0:T(8,128)} %copy-done.3, f32[4,256,128]{2,1,0:T(8,128)} %copy-done.5, f32[4,256,128]{2,1,0:T(8,128)} %copy-done.6), custom_call_target="tpu_custom_call" | custom-call | tf_op jit(solution)/shard_map/pallas_call | solution.py:76
  82.1 1.0 %fusion.1 = (f32[1,256,128]{2,1,0:T(8,128)S(1)}, f32[1,256,128]{2,1,0:T(8,128)S(1)}) fusion(f32[6,256,128]{2,1,0:T(8,128)} %shard_map.39), kind=kLoop, calls=%fused_computation.15 | loop fusion | bytes 524288 | tf_op jit(solution)/shard_map/slice | solution.py:89
  83.0 1.1 %fusion = (f32[2,256,128]{2,1,0:T(8,128)S(1)}, f32[2,256,128]{2,1,0:T(8,128)S(1)}) fusion(f32[6,256,128]{2,1,0:T(8,128)} %shard_map.39), kind=kLoop, calls=%fused_computation.14 | loop fusion | bytes 1048576 | tf_op jit(solution)/shard_map/slice | solution.py:89
  84.1 6.5 %shard_map.40 = f32[4,256,128]{2,1,0:T(8,128)} custom-call(s32[1]{0:T(128)} %bitcast.side_ref, f32[2,5]{1,0:T(2,128)} %get-tuple-element.22.keep_ref, f32[2,5,256,128]{3,2,1,0:T(8,128)} %copy-done.1, f32[2,5,256,128]{3,2,1,0:T(8,128)} %copy-done.3), custom_call_target="tpu_custom_call" | custom-call | tf_op jit(solution)/shard_map/pallas_call | solution.py:76
  90.6 1.1 %fusion.4 = (f32[2,256,128]{2,1,0:T(8,128)S(1)}, f32[2,256,128]{2,1,0:T(8,128)S(1)}) fusion(f32[4,256,128]{2,1,0:T(8,128)} %shard_map.40), kind=kLoop, calls=%fused_computation.18 | loop fusion | bytes 1048576 | tf_op jit(solution)/shard_map/slice | solution.py:87
  91.8 1.1 %pad_maximum_fusion.1 = f32[2,5,256,128]{3,2,1,0:T(8,128)} fusion(f32[1,5,256,128]{3,2,1,0:T(8,128)S(1)} %maximum_bitcast_fusion.3, f32[1,5,256,128]{3,2,1,0:T(8,128)S(1)} %maximum_bitcast_fusion.2), kind=kLoop, calls=%fused_computation.1 | loop fusion | flops 327680 | bytes 2621440 | tf_op jit(solution)/shard_map/stack | solution.py:90
  (16 shorter events, 0.2 us)
Async XLA Ops:
  2.2 31.0 %copy-start = (f32[2,5,256,128]{3,2,1,0:T(8,128)}, f32[2,5,256,128]{3,2,1,0:T(8,128)S(1)}, u32[]{:S(2)}) copy-start(f32[2,5,256,128]{3,2,1,0:T(8,128)S(1)} %broadcast_multiply_fusion.mine_ref) | copy-start | bytes 3932164
  2.2 12.6 %copy-start.7 = (s32[2,2,5]{2,1,0:T(2,128)S(1)}, s32[2,2,5]{2,1,0:T(2,128)}, u32[]{:S(2)}) copy-start(s32[2,2,5]{2,1,0:T(2,128)} %param.5) | copy-start | bytes 244
  2.2 30.9 %collective-permute-start = (f32[2,5,256,128]{3,2,1,0:T(8,128)S(1)}, f32[2,5,256,128]{3,2,1,0:T(8,128)S(1)}, u32[]{:S(2)}, u32[]{:S(2)}) collective-permute-start(f32[2,5,256,128]{3,2,1,0:T(8,128)S(1)} %broadcast_multiply_fusion.mine_ref), channel_id=1, source_target_pairs={{0,1},{1,0},{2,3},{3,2},{4,5},{5,4},{6,7},{7,6},{8,9},{9,8},{10,11... | collective-permute-start | bytes 3932168 | tf_op jit(solution)/shard_map/ppermute | solution.py:19
  2.4 22.3 %collective-permute-start.2 = (f32[4,256,128]{2,1,0:T(8,128)S(1)}, f32[4,256,128]{2,1,0:T(8,128)}, u32[]{:S(2)}, u32[]{:S(2)}) collective-permute-start(f32[4,256,128]{2,1,0:T(8,128)S(1)} %pad_maximum_fusion.2), channel_id=1, source_target_pairs={{2,0},{4,2},{6,4},{8,6},{10,8},{12,10},{14,12},{16,14},{18,16},{20... | collective-permute-start | bytes 1572872 | tf_op jit(solution)/shard_map/ppermute | solution.py:25
  12.9 20.3 %collective-permute-start.1 = (f32[4,256,128]{2,1,0:T(8,128)S(1)}, f32[4,256,128]{2,1,0:T(8,128)}, u32[]{:S(2)}, u32[]{:S(2)}) collective-permute-start(f32[4,256,128]{2,1,0:T(8,128)S(1)} %pad_maximum_fusion.2), channel_id=1, source_target_pairs={{0,2},{2,4},{4,6},{6,8},{8,10},{10,12},{12,14},{14,16},{16,18},{18... | collective-permute-start | bytes 1572872 | tf_op jit(solution)/shard_map/ppermute | solution.py:24
  33.1 1.1 %copy-start.2 = (f32[2,5,256,128]{3,2,1,0:T(8,128)}, f32[2,5,256,128]{3,2,1,0:T(8,128)S(1)}, u32[]{:S(2)}) copy-start(f32[2,5,256,128]{3,2,1,0:T(8,128)S(1)} %collective-permute-done.other_ref) | copy-start | bytes 3932164
  51.2 1.1 %copy-start.4 = (f32[4,256,128]{2,1,0:T(8,128)S(1)}, f32[4,256,128]{2,1,0:T(8,128)}, u32[]{:S(2)}) copy-start(f32[4,256,128]{2,1,0:T(8,128)} %shard_map.38) | copy-start | bytes 1572868
  51.3 22.5 %copy-start.1 = (f32[2,5,256,128]{3,2,1,0:T(8,128)}, f32[2,5,256,128]{3,2,1,0:T(8,128)S(1)}, u32[]{:S(2)}) copy-start(f32[2,5,256,128]{3,2,1,0:T(8,128)S(1)} %pad_maximum_fusion.mine_ref) | copy-start | bytes 3932164
  51.3 21.7 %collective-permute-start.3 = (f32[2,5,256,128]{3,2,1,0:T(8,128)S(1)}, f32[2,5,256,128]{3,2,1,0:T(8,128)S(1)}, u32[]{:S(2)}, u32[]{:S(2)}) collective-permute-start(f32[2,5,256,128]{3,2,1,0:T(8,128)S(1)} %pad_maximum_fusion.mine_ref), channel_id=1, source_target_pairs={{0,1},{1,0},{2,3},{3,2},{4,5},{5,4},{6,7},{7,6},{8,9},{9,8},{10,11... | collective-permute-start | bytes 3932168 | tf_op jit(solution)/shard_map/ppermute | solution.py:19
  52.3 19.5 %collective-permute-start.4 = (f32[4,256,128]{2,1,0:T(8,128)S(1)}, f32[4,256,128]{2,1,0:T(8,128)S(1)}, u32[]{:S(2)}, u32[]{:S(2)}) collective-permute-start(f32[4,256,128]{2,1,0:T(8,128)S(1)} %copy-done.4), channel_id=1, source_target_pairs={{0,2},{2,4},{4,6},{6,8},{8,10},{10,12},{12,14},{14,16},{16,18},{18... | collective-permute-start | bytes 1572872 | tf_op jit(solution)/shard_map/ppermute | solution.py:24
  54.2 18.8 %collective-permute-start.5 = (f32[4,256,128]{2,1,0:T(8,128)S(1)}, f32[4,256,128]{2,1,0:T(8,128)S(1)}, u32[]{:S(2)}, u32[]{:S(2)}) collective-permute-start(f32[4,256,128]{2,1,0:T(8,128)S(1)} %copy-done.4), channel_id=1, source_target_pairs={{2,0},{4,2},{6,4},{8,6},{10,8},{12,10},{14,12},{16,14},{18,16},{20... | collective-permute-start | bytes 1572872 | tf_op jit(solution)/shard_map/ppermute | solution.py:25
  71.8 2.0 %copy-start.5 = (f32[4,256,128]{2,1,0:T(8,128)}, f32[4,256,128]{2,1,0:T(8,128)S(1)}, u32[]{:S(2)}) copy-start(f32[4,256,128]{2,1,0:T(8,128)S(1)} %collective-permute-done.4.rest_0_) | copy-start | bytes 1572868
  73.0 0.8 copy-start.6
  73.8 1.1 %copy-start.3 = (f32[2,5,256,128]{3,2,1,0:T(8,128)}, f32[2,5,256,128]{3,2,1,0:T(8,128)S(1)}, u32[]{:S(2)}) copy-start(f32[2,5,256,128]{3,2,1,0:T(8,128)S(1)} %collective-permute-done.3.other_ref) | copy-start | bytes 3932164

commit v4 on v3

v4 whole, which is shorter than its diff:
```python
import functools

import jax
import jax.numpy as jnp
from jax import lax
from jax.experimental import pallas as pl
from jax.experimental.pallas import tpu as pltpu
from jax.sharding import PartitionSpec as P


STEPS = 2
DIAG = ((0, 2), (0, 3), (1, 1), (1, 2))
OFF = ((0, 0), (0, 1), (0, 4), (1, 0), (1, 3), (1, 4))
CONTRACT = (((1,), (0,)), ((), ()))
CONTRACT_T = (((1,), (1,)), ((), ()))


def swap_help(value):
    return lax.ppermute(value, "help", [(0, 1), (1, 0)])


def send_block(block):
    count = lax.axis_size("rows")
    from_left = lax.ppermute(block, "rows", [(i, i + 1) for i in range(count - 1)])
    from_right = lax.ppermute(block, "rows", [(i + 1, i) for i in range(count - 1)])
    return from_left, from_right


def split(x):
    high = x.astype(jnp.bfloat16)
    return high, (x - high.astype(jnp.float32)).astype(jnp.bfloat16)


def dot3(a_high, a_low, b, dims):
    b_high, b_low = split(b)

    def one(x, y):
        return lax.dot_general(x, y, dims, preferred_element_type=jnp.float32)

    return one(a_low, b_high) + one(a_high, b_low) + one(a_high, b_high)


def band_kernel(tiles, odd, side_ref, scale_ref, keep_ref, mine_ref, other_ref, *rest):
    if len(rest) == 6:
        left_ref, right_ref, diag_ref, out_ref, high_ref, low_ref = rest
    else:
        left_ref = right_ref = diag_ref = None
        out_ref, high_ref, low_ref = rest
    half = mine_ref.shape[3]
    side = side_ref[0]
    own = pl.ds(pl.multiple_of(side * half, half), half)
    far = pl.ds(pl.multiple_of((1 - side) * half, half), half)

    def scale(row, slot):
        return scale_ref[row, slot].astype(jnp.float32)

    for row in range(2):
        for slot in range(5):
            full = jnp.concatenate([mine_ref[row, slot], other_ref[row, slot]], axis=1) * scale(row, slot)
            high, low = split(full)
            high_ref[row, slot] = high
            low_ref[row, slot] = low
    for index, (row, slot) in enumerate(tiles):
        col = row + slot - 2
        acc = jnp.zeros(mine_ref.shape[2:], jnp.float32)
        for k in range(max(row, col) - 2, min(row, col) + 3):
            a_high = high_ref[row, k - row + 2]
            a_low = low_ref[row, k - row + 2]
            if k in (0, 1):
                b = col - k + 2
                right = jnp.concatenate([mine_ref[k, b, own, :], mine_ref[k, b, far, :]], axis=0) * scale(k, b)
                acc += dot3(a_high, a_low, right, CONTRACT)
            elif col not in (0, 1):
                src = left_ref if k < 0 else right_ref
                b = 2 * (k + 2) + (col + 2) if k < 0 else 2 * (k - 2) + (col - 2)
                right = jnp.concatenate([src[b, own, :], src[b, far, :]], axis=0)
                acc += dot3(a_high, a_low, right, CONTRACT)
            else:
                s = k - col + 2
                flipped = jnp.concatenate([mine_ref[col, s, own, :], other_ref[col, s, own, :]], axis=1) * scale(col, s)
                acc += dot3(a_high, a_low, flipped, CONTRACT_T)
        if odd:
            acc = 2.0 * mine_ref[row, slot] * scale(row, slot) - acc
        value = acc * keep_ref[row, slot].astype(jnp.float32)
        if diag_ref is None:
            out_ref[index] = value
        else:
            out_ref[row, slot] = value
    if diag_ref is not None:
        for index, (row, slot) in enumerate(DIAG):
            out_ref[row, slot] = diag_ref[index]


def band_call(tiles, odd, side, scale, keep, mine, other, halo=None, diag=None):
    smem = pl.BlockSpec(memory_space=pltpu.SMEM)
    vmem = pl.BlockSpec(memory_space=pltpu.VMEM)
    args = [side, scale, keep, mine, other]
    if halo is None:
        shape = (len(tiles),) + mine.shape[2:]
    else:
        args += [halo[0], halo[1], diag]
        shape = mine.shape
    full = mine.shape[:2] + (mine.shape[2], 2 * mine.shape[3])
    return pl.pallas_call(
        functools.partial(band_kernel, tiles, odd),
        out_shape=jax.ShapeDtypeStruct(shape, jnp.float32),
        in_specs=[smem, smem, smem] + [vmem] * (len(args) - 3),
        out_specs=vmem,
        scratch_shapes=[pltpu.VMEM(full, jnp.bfloat16), pltpu.VMEM(full, jnp.bfloat16)],
    )(*args)


def purify(density, pattern, truncation):
    side = lax.axis_index("help").astype(jnp.int32).reshape(1)
    block = jnp.stack([density[row, slot] * pattern[row, slot].astype(jnp.float32) for row, slot in DIAG])
    halo = send_block(block)
    matrix = density
    scale = pattern
    for step_index in range(STEPS):
        keep = truncation[step_index]
        odd = step_index % 2 == 1
        other = swap_help(matrix)
        diag = band_call(DIAG, odd, side, scale, keep, matrix, other)
        if step_index + 1 < STEPS:
            next_halo = send_block(diag)
        matrix = band_call(OFF, odd, side, scale, keep, matrix, other, halo, diag)
        scale = jnp.ones_like(pattern)
        if step_index + 1 < STEPS:
            halo = next_halo
    return matrix


def solution(mesh):
    return jax.shard_map(
        purify,
        mesh=mesh,
        in_specs=(P("rows", None, None, "help"), P("rows", None), P(None, "rows", None)),
        out_specs=P("rows", None, None, "help"),
        check_vma=False,
    )
```

time: 93.5 us -> 71.1 us (0.76)
  Pallas kernels: 27.4 us -> 20 us
  waiting for transfers between devices: 28.2 us -> 22.9 us
  starting transfers between devices: 22.8 us -> 18.2 us
  local copies, waits for them, and re-layouts: 10.1 us -> 5.85 us
  other arithmetic: 4.19 us -> 1.17 us
  between operations: 0.18 us -> 2.66 us
    pallas_call x4, Pallas kernels: 27.4 us -> 20 us  [band_call(): pl.pallas_call(functools.partial(band_kernel, tiles, odd), out_shape=jax....]
    ppermute x2, starting transfers between devices: 18.8 us -> 12.4 us  [send_block(): lax.ppermute(block, 'rows', [(i + 1, i) for i in range(count - 1)])]
    slice x6 -> x1, local copies, waits for them, and re-layouts: 6.23 us -> 1.5 us  [purify(): pattern[row, slot].astype(jnp.float32)]
    ppermute x2, waiting for transfers between devices: 17.7 us -> 14.5 us  [send_block(): lax.ppermute(block, 'rows', [(i, i + 1) for i in range(count - 1)])]
    ppermute x2, waiting for transfers between devices: 10.5 us -> 8.38 us  [send_block(): lax.ppermute(block, 'rows', [(i + 1, i) for i in range(count - 1)])]
    ppermute x2, starting transfers between devices: 3.83 us -> 5.84 us  [send_block(): lax.ppermute(block, 'rows', [(i, i + 1) for i in range(count - 1)])]
    another operation x6 -> x1, other arithmetic: 1.46 us -> 0.04 us  [purify(): jnp.stack([density[row, slot] * pattern[row, slot].astype(jnp.float32) fo...]
    convert_element_type x2 -> x0, other arithmetic: 1.23 us -> none  [the longest x1 0.68 us: purify(): matrix = density * pattern[:, :, None, None].astype(jnp.float32)]
  transfers between devices with their start and end apart: 6 -> 6, of which waited for: 4 -> 4; matrix products, arithmetic and copies ran while one was open for 1% -> 5% of each run, Pallas kernels for 0% -> 13%
where the time goes in v4:
time: 71.1 us; the launch traced here: 70.8 us
  waiting for transfers between devices  22.9 us (32%)
  Pallas kernels  20 us (28%)
  starting transfers between devices  18.2 us (26%)
  local copies, waits for them, and re-layouts  5.85 us (8%)
  between operations  2.66 us (4%)
  other arithmetic  1.17 us (2%)
    pallas_call x4, Pallas kernels, band_call(): pl.pallas_call(functools.partial(band_kernel, tiles, odd), out_shape=jax....  20 us
    ppermute x2, waiting for transfers between devices, send_block(): lax.ppermute(block, 'rows', [(i, i + 1) for i in range(count - 1)])  14.5 us
    ppermute x2, starting transfers between devices, send_block(): lax.ppermute(block, 'rows', [(i + 1, i) for i in range(count - 1)])  12.4 us
    ppermute x2, waiting for transfers between devices, send_block(): lax.ppermute(block, 'rows', [(i + 1, i) for i in range(count - 1)])  8.38 us
    ppermute x2, starting transfers between devices, send_block(): lax.ppermute(block, 'rows', [(i, i + 1) for i in range(count - 1)])  5.84 us
    unnamed x16, local copies, waits for them, and re-layouts  3.17 us
    slice x1, local copies, waits for them, and re-layouts, purify(): pattern[row, slot].astype(jnp.float32)  1.5 us
  transfers between devices with their start and end apart: 6, of which 4 were waited for; matrix products, arithmetic and copies ran while one was open for 5% of the time, Pallas kernels for 13%

profile of v4, /device:TPU:6, one launch (start us, length us, event | category | flops | bytes accessed | tf_op | source)
XLA Modules:
  0.0 70.8 jit_solution(9504600588675949937)
XLA Ops:
  0.0 0.0 copy-start.7
  0.0 0.0 collective-permute-start
  0.0 1.5 %fusion = (s32[1,1]{1,0:T(1,128)}, s32[1,1]{1,0:T(1,128)}, s32[1,1]{1,0:T(1,128)}, s32[1,1]{1,0:T(1,128)}) fusion(s32[2,5]{1,0:T(2,128)} %scale_ref.3), kind=kLoop, calls=%fused_computation.7 | loop fusion | bytes 32 | tf_op jit(solution)/shard_map/slice | solution.py:115
  4.1 1.1 %multiply_bitcast_fusion.3 = (f32[1,256,128]{2,1,0:T(8,128)S(1)}, f32[1,256,128]{2,1,0:T(8,128)S(1)}, f32[1,256,128]{2,1,0:T(8,128)S(1)}, f32[1,256,128]{2,1,0:T(8,128)S(1)}) fusion(f32[2,5,256,128]{3,2,1,0:T(8,128)} %mine_ref.3, f32[]{:T(128)} %bitcast.3, f32[]{:T(128)} %bitcast.9, f32[]{:T(128)} %bitcast.7, f32[]{:T(128)} %bitcast.5), kind=kLoop, calls=%fused_computation.4 | loop fusion | flops 131072 | bytes 1048592 | tf_op jit(solution)/shard_map/mul | solution.py:115
  5.3 10.5 %collective-permute-start.2 = (f32[4,256,128]{2,1,0:T(8,128)S(1)}, f32[4,256,128]{2,1,0:T(8,128)S(1)}, u32[]{:S(2)}, u32[]{:S(2)}) collective-permute-start(f32[4,256,128]{2,1,0:T(8,128)S(1)} %pad_maximum_fusion), channel_id=1, source_target_pairs={{2,0},{4,2},{6,4},{8,6},{10,8},{12,10},{14,12},{16,14},{18,16},{20... | collective-permute-start | bytes 1572872 | tf_op jit(solution)/shard_map/ppermute | solution.py:25
  15.8 1.9 %collective-permute-start.1 = (f32[4,256,128]{2,1,0:T(8,128)S(1)}, f32[4,256,128]{2,1,0:T(8,128)S(1)}, u32[]{:S(2)}, u32[]{:S(2)}) collective-permute-start(f32[4,256,128]{2,1,0:T(8,128)S(1)} %pad_maximum_fusion), channel_id=1, source_target_pairs={{0,2},{2,4},{4,6},{6,8},{8,10},{10,12},{12,14},{14,16},{16,18},{18... | collective-permute-start | bytes 1572872 | tf_op jit(solution)/shard_map/ppermute | solution.py:24
  17.7 0.0 copy-done.7
  17.7 0.6 slice_bitcast_fusion
  18.3 0.0 collective-permute-done.other_ref
  18.3 0.0 copy-start
  18.3 1.1 %copy-done = f32[2,5,256,128]{3,2,1,0:T(8,128)} copy-done((f32[2,5,256,128]{3,2,1,0:T(8,128)}, f32[2,5,256,128]{3,2,1,0:T(8,128)S(1)}, u32[]{:S(2)}) %copy-start) | copy-done | bytes 1310744
  19.4 4.5 %shard_map.37.rest_2_ = f32[4,256,128]{2,1,0:T(8,128)} custom-call(s32[1]{0:T(128)} %bitcast.side_ref, s32[2,5]{1,0:T(2,128)} %scale_ref.3, s32[2,5]{1,0:T(2,128)} %get-tuple-element.9.keep_ref, f32[2,5,256,128]{3,2,1,0:T(8,128)} %mine_ref.3, f32[2,5,256,128]{3,2,1,0:T(8,128)} %copy-done), custom_call_target="tpu_custom_call" | custom-call | tf_op jit(solution)/shard_map/pallas_call | solution.py:104
  23.9 0.0 copy-start.2
  23.9 3.7 %collective-permute-done.2.rest_1_ = f32[4,256,128]{2,1,0:T(8,128)S(1)} collective-permute-done((f32[4,256,128]{2,1,0:T(8,128)S(1)}, f32[4,256,128]{2,1,0:T(8,128)S(1)}, u32[]{:S(2)}, u32[]{:S(2)}) %collective-permute-start.2) | collective-permute-done | bytes 524320 | tf_op jit(solution)/shard_map/ppermute | solution.py:25
  27.6 8.3 %collective-permute-done.1.rest_0_ = f32[4,256,128]{2,1,0:T(8,128)S(1)} collective-permute-done((f32[4,256,128]{2,1,0:T(8,128)S(1)}, f32[4,256,128]{2,1,0:T(8,128)S(1)}, u32[]{:S(2)}, u32[]{:S(2)}) %collective-permute-start.1) | collective-permute-done | bytes 524320 | tf_op jit(solution)/shard_map/ppermute | solution.py:24
  35.9 0.0 copy-done.3
  35.9 0.8 %copy-done.4 = f32[4,256,128]{2,1,0:T(8,128)} copy-done((f32[4,256,128]{2,1,0:T(8,128)}, f32[4,256,128]{2,1,0:T(8,128)S(1)}, u32[]{:S(2)}) %copy-start.4) | copy-done | bytes 524312
  36.7 5.4 %shard_map.38.mine_ref = f32[2,5,256,128]{3,2,1,0:T(8,128)} custom-call(s32[1]{0:T(128)} %bitcast.side_ref, s32[2,5]{1,0:T(2,128)} %scale_ref.3, s32[2,5]{1,0:T(2,128)} %get-tuple-element.9.keep_ref, f32[2,5,256,128]{3,2,1,0:T(8,128)} %mine_ref.3, f32[2,5,256,128]{3,2,1,0:T(8,128)} %copy-done, f32[4,256,128]{2,1,0:T(8,128)} %copy-done.4, ...), custom_call_target="tpu_custom_call" | custom-call | tf_op jit(solution)/shard_map/pallas_call | solution.py:104
  42.2 0.0 collective-permute-start.3
  42.2 0.0 copy-done.2
  42.2 1.9 %collective-permute-start.5 = (f32[4,256,128]{2,1,0:T(8,128)S(1)}, f32[4,256,128]{2,1,0:T(8,128)S(1)}, u32[]{:S(2)}, u32[]{:S(2)}) collective-permute-start(f32[4,256,128]{2,1,0:T(8,128)S(1)} %copy-done.2), channel_id=1, source_target_pairs={{2,0},{4,2},{6,4},{8,6},{10,8},{12,10},{14,12},{16,14},{18,16},{20... | collective-permute-start | bytes 1572872 | tf_op jit(solution)/shard_map/ppermute | solution.py:25
  44.1 3.9 %collective-permute-start.4 = (f32[4,256,128]{2,1,0:T(8,128)S(1)}, f32[4,256,128]{2,1,0:T(8,128)S(1)}, u32[]{:S(2)}, u32[]{:S(2)}) collective-permute-start(f32[4,256,128]{2,1,0:T(8,128)S(1)} %copy-done.2), channel_id=1, source_target_pairs={{0,2},{2,4},{4,6},{6,8},{8,10},{10,12},{12,14},{14,16},{16,18},{18... | collective-permute-start | bytes 1572872 | tf_op jit(solution)/shard_map/ppermute | solution.py:24
  48.0 0.0 collective-permute-done.3.other_ref
  48.0 0.0 copy-start.1
  48.1 0.6 broadcast_1_scale_ref.2.scale_ref
  48.6 0.5 copy-done.1
  49.1 4.6 %shard_map.39.rest_2_ = f32[4,256,128]{2,1,0:T(8,128)} custom-call(s32[1]{0:T(128)} %bitcast.side_ref, s32[2,5]{1,0:T(2,128)} %broadcast_1_scale_ref.2.scale_ref, s32[2,5]{1,0:T(2,128)} %get-tuple-element.10.keep_ref, f32[2,5,256,128]{3,2,1,0:T(8,128)} %shard_map.38.mine_ref, f32[2,5,256,128]{3,2,1,0:T(8,128)} %copy-done.1), custom_call_target="tpu_custom_call" | custom-call | tf_op jit(solution)/shard_map/pallas_call | solution.py:104
  53.7 4.7 %collective-permute-done.5.rest_1_ = f32[4,256,128]{2,1,0:T(8,128)S(1)} collective-permute-done((f32[4,256,128]{2,1,0:T(8,128)S(1)}, f32[4,256,128]{2,1,0:T(8,128)S(1)}, u32[]{:S(2)}, u32[]{:S(2)}) %collective-permute-start.5) | collective-permute-done | bytes 524320 | tf_op jit(solution)/shard_map/ppermute | solution.py:25
  58.4 6.1 %collective-permute-done.4.rest_0_ = f32[4,256,128]{2,1,0:T(8,128)S(1)} collective-permute-done((f32[4,256,128]{2,1,0:T(8,128)S(1)}, f32[4,256,128]{2,1,0:T(8,128)S(1)}, u32[]{:S(2)}, u32[]{:S(2)}) %collective-permute-start.4) | collective-permute-done | bytes 524320 | tf_op jit(solution)/shard_map/ppermute | solution.py:24
  64.5 0.0 copy-done.5
  64.5 0.8 %copy-done.6 = f32[4,256,128]{2,1,0:T(8,128)} copy-done((f32[4,256,128]{2,1,0:T(8,128)}, f32[4,256,128]{2,1,0:T(8,128)S(1)}, u32[]{:S(2)}) %copy-start.6) | copy-done | bytes 524312
  65.3 5.4 %shard_map.40 = f32[2,5,256,128]{3,2,1,0:T(8,128)} custom-call(s32[1]{0:T(128)} %bitcast.side_ref, s32[2,5]{1,0:T(2,128)} %broadcast_1_scale_ref.2.scale_ref, s32[2,5]{1,0:T(2,128)} %get-tuple-element.10.keep_ref, f32[2,5,256,128]{3,2,1,0:T(8,128)} %shard_map.38.mine_ref, f32[2,5,256,128]{3,2,1,0:T(8,128)} %copy-done.1, f32[4,256,128]{2,1,0:T(8,128)} %copy-done.6, ...), custom_call_target="tpu_custom_call" | custom-call | tf_op jit(solution)/shard_map/pallas_call | solution.py:104
  (5 shorter events, 0.0 us)
Async XLA Ops:
  0.0 17.7 %copy-start.7 = (s32[2,2,5]{2,1,0:T(2,128)S(1)}, s32[2,2,5]{2,1,0:T(2,128)}, u32[]{:S(2)}) copy-start(s32[2,2,5]{2,1,0:T(2,128)} %param.5) | copy-start | bytes 244
  0.0 18.3 %collective-permute-start = (f32[2,5,256,128]{3,2,1,0:T(8,128)}, f32[2,5,256,128]{3,2,1,0:T(8,128)S(1)}, u32[]{:S(2)}, u32[]{:S(2)}) collective-permute-start(f32[2,5,256,128]{3,2,1,0:T(8,128)} %mine_ref.3), channel_id=1, source_target_pairs={{0,1},{1,0},{2,3},{3,2},{4,5},{5,4},{6,7},{7,6},{8,9},{9,8},{10,11... | collective-permute-start | bytes 3932168 | tf_op jit(solution)/shard_map/ppermute | solution.py:19
  5.3 22.3 %collective-permute-start.2 = (f32[4,256,128]{2,1,0:T(8,128)S(1)}, f32[4,256,128]{2,1,0:T(8,128)S(1)}, u32[]{:S(2)}, u32[]{:S(2)}) collective-permute-start(f32[4,256,128]{2,1,0:T(8,128)S(1)} %pad_maximum_fusion), channel_id=1, source_target_pairs={{2,0},{4,2},{6,4},{8,6},{10,8},{12,10},{14,12},{16,14},{18,16},{20... | collective-permute-start | bytes 1572872 | tf_op jit(solution)/shard_map/ppermute | solution.py:25
  15.8 20.2 %collective-permute-start.1 = (f32[4,256,128]{2,1,0:T(8,128)S(1)}, f32[4,256,128]{2,1,0:T(8,128)S(1)}, u32[]{:S(2)}, u32[]{:S(2)}) collective-permute-start(f32[4,256,128]{2,1,0:T(8,128)S(1)} %pad_maximum_fusion), channel_id=1, source_target_pairs={{0,2},{2,4},{4,6},{6,8},{8,10},{10,12},{12,14},{14,16},{16,18},{18... | collective-permute-start | bytes 1572872 | tf_op jit(solution)/shard_map/ppermute | solution.py:24
  18.3 1.1 %copy-start = (f32[2,5,256,128]{3,2,1,0:T(8,128)}, f32[2,5,256,128]{3,2,1,0:T(8,128)S(1)}, u32[]{:S(2)}) copy-start(f32[2,5,256,128]{3,2,1,0:T(8,128)S(1)} %collective-permute-done.other_ref) | copy-start | bytes 3932164
  23.9 18.3 %copy-start.2 = (f32[4,256,128]{2,1,0:T(8,128)S(1)}, f32[4,256,128]{2,1,0:T(8,128)}, u32[]{:S(2)}) copy-start(f32[4,256,128]{2,1,0:T(8,128)} %shard_map.37.rest_2_) | copy-start | bytes 1572868
  27.6 8.3 %copy-start.3 = (f32[4,256,128]{2,1,0:T(8,128)}, f32[4,256,128]{2,1,0:T(8,128)S(1)}, u32[]{:S(2)}) copy-start(f32[4,256,128]{2,1,0:T(8,128)S(1)} %collective-permute-done.2.rest_1_) | copy-start | bytes 1572868
  35.9 0.8 %copy-start.4 = (f32[4,256,128]{2,1,0:T(8,128)}, f32[4,256,128]{2,1,0:T(8,128)S(1)}, u32[]{:S(2)}) copy-start(f32[4,256,128]{2,1,0:T(8,128)S(1)} %collective-permute-done.1.rest_0_) | copy-start | bytes 1572868
  42.2 5.9 %collective-permute-start.3 = (f32[2,5,256,128]{3,2,1,0:T(8,128)}, f32[2,5,256,128]{3,2,1,0:T(8,128)S(1)}, u32[]{:S(2)}, u32[]{:S(2)}) collective-permute-start(f32[2,5,256,128]{3,2,1,0:T(8,128)} %shard_map.38.mine_ref), channel_id=1, source_target_pairs={{0,1},{1,0},{2,3},{3,2},{4,5},{5,4},{6,7},{7,6},{8,9},{9,8},{10,11... | collective-permute-start | bytes 3932168 | tf_op jit(solution)/shard_map/ppermute | solution.py:19
  42.2 16.2 %collective-permute-start.5 = (f32[4,256,128]{2,1,0:T(8,128)S(1)}, f32[4,256,128]{2,1,0:T(8,128)S(1)}, u32[]{:S(2)}, u32[]{:S(2)}) collective-permute-start(f32[4,256,128]{2,1,0:T(8,128)S(1)} %copy-done.2), channel_id=1, source_target_pairs={{2,0},{4,2},{6,4},{8,6},{10,8},{12,10},{14,12},{16,14},{18,16},{20... | collective-permute-start | bytes 1572872 | tf_op jit(solution)/shard_map/ppermute | solution.py:25
  44.1 20.4 %collective-permute-start.4 = (f32[4,256,128]{2,1,0:T(8,128)S(1)}, f32[4,256,128]{2,1,0:T(8,128)S(1)}, u32[]{:S(2)}, u32[]{:S(2)}) collective-permute-start(f32[4,256,128]{2,1,0:T(8,128)S(1)} %copy-done.2), channel_id=1, source_target_pairs={{0,2},{2,4},{4,6},{6,8},{8,10},{10,12},{12,14},{14,16},{16,18},{18... | collective-permute-start | bytes 1572872 | tf_op jit(solution)/shard_map/ppermute | solution.py:24
  48.0 1.1 %copy-start.1 = (f32[2,5,256,128]{3,2,1,0:T(8,128)}, f32[2,5,256,128]{3,2,1,0:T(8,128)S(1)}, u32[]{:S(2)}) copy-start(f32[2,5,256,128]{3,2,1,0:T(8,128)S(1)} %collective-permute-done.3.other_ref) | copy-start | bytes 3932164
  58.4 6.1 %copy-start.5 = (f32[4,256,128]{2,1,0:T(8,128)}, f32[4,256,128]{2,1,0:T(8,128)S(1)}, u32[]{:S(2)}) copy-start(f32[4,256,128]{2,1,0:T(8,128)S(1)} %collective-permute-done.5.rest_1_) | copy-start | bytes 1572868
  64.5 0.8 %copy-start.6 = (f32[4,256,128]{2,1,0:T(8,128)}, f32[4,256,128]{2,1,0:T(8,128)S(1)}, u32[]{:S(2)}) copy-start(f32[4,256,128]{2,1,0:T(8,128)S(1)} %collective-permute-done.4.rest_0_) | copy-start | bytes 1572868

commit v5 on v4

v5 whole, which is shorter than its diff:
```python
import functools

import jax
import jax.numpy as jnp
from jax import lax
from jax.experimental import pallas as pl
from jax.experimental.pallas import tpu as pltpu
from jax.sharding import PartitionSpec as P


DIAG = ((0, 2), (0, 3), (1, 1), (1, 2))
OFF = ((0, 0), (0, 1), (0, 4), (1, 0), (1, 3), (1, 4))
ALL = tuple((row, slot) for row in range(2) for slot in range(5))
CONTRACT = (((1,), (0,)), ((), ()))
CONTRACT_T = (((1,), (1,)), ((), ()))


def swap_help(value):
    return lax.ppermute(value, "help", [(0, 1), (1, 0)])


def send_block(block):
    count = lax.axis_size("rows")
    from_left = lax.ppermute(block, "rows", [(i, i + 1) for i in range(count - 1)])
    from_right = lax.ppermute(block, "rows", [(i + 1, i) for i in range(count - 1)])
    return from_left, from_right


def split(x):
    high = x.astype(jnp.bfloat16)
    return high, (x - high.astype(jnp.float32)).astype(jnp.bfloat16)


def dot3(a_high, a_low, b, dims):
    b_high, b_low = split(b)
    def one(x, y):
        return lax.dot_general(x, y, dims, preferred_element_type=jnp.float32)
    return one(a_low, b_high) + one(a_high, b_low) + one(a_high, b_high)


class Tiles:
    def __init__(self, refs, scale):
        self.refs = refs
        self.scale = scale

    def __call__(self, row, slot, rows=slice(None)):
        if len(self.refs) == 1:
            value = self.refs[0][row, slot, rows, :]
        elif (row, slot) in DIAG:
            value = self.refs[0][DIAG.index((row, slot)), rows, :]
        else:
            value = self.refs[1][OFF.index((row, slot)), rows, :]
        if self.scale is not None:
            value = value * self.scale[row, slot].astype(jnp.float32)
        return value


def band_kernel(tiles, odd, parts, scaled, halo, side_ref, scale_ref, keep_ref, *rest):
    mine = Tiles(rest[:parts], scale_ref if scaled else None)
    other = Tiles(rest[parts : 2 * parts], scale_ref if scaled else None)
    rest = rest[2 * parts :]
    if halo:
        left_ref, right_ref = rest[:2]
        rest = rest[2:]
    out_ref, high_ref, low_ref = rest
    half = high_ref.shape[3] // 2
    side = side_ref[0]
    own = pl.ds(pl.multiple_of(side * half, half), half)
    far = pl.ds(pl.multiple_of((1 - side) * half, half), half)

    for row in range(2):
        for slot in range(5):
            high, low = split(jnp.concatenate([mine(row, slot), other(row, slot)], axis=1))
            high_ref[row, slot] = high
            low_ref[row, slot] = low
    for index, (row, slot) in enumerate(tiles):
        col = row + slot - 2
        acc = jnp.zeros((high_ref.shape[2], half), jnp.float32)
        for k in range(max(row, col) - 2, min(row, col) + 3):
            a_high = high_ref[row, k - row + 2]
            a_low = low_ref[row, k - row + 2]
            if k in (0, 1):
                b = col - k + 2
                right = jnp.concatenate([mine(k, b, own), mine(k, b, far)], axis=0)
                acc += dot3(a_high, a_low, right, CONTRACT)
            elif col not in (0, 1):
                src = left_ref if k < 0 else right_ref
                b = 2 * (k + 2) + (col + 2) if k < 0 else 2 * (k - 2) + (col - 2)
                right = jnp.concatenate([src[b, own, :], src[b, far, :]], axis=0)
                acc += dot3(a_high, a_low, right, CONTRACT)
            else:
                s = k - col + 2
                flipped = jnp.concatenate([mine(col, s, own), other(col, s, own)], axis=1)
                acc += dot3(a_high, a_low, flipped, CONTRACT_T)
        if odd:
            acc = 2.0 * mine(row, slot) - acc
        value = acc * keep_ref[row, slot].astype(jnp.float32)
        if len(tiles) == len(ALL):
            out_ref[row, slot] = value
        else:
            out_ref[index] = value


def band_call(tiles, odd, side, scale, keep, mine, other, halo=None, scaled=False):
    smem = pl.BlockSpec(memory_space=pltpu.SMEM)
    vmem = pl.BlockSpec(memory_space=pltpu.VMEM)
    args = [side, scale, keep] + list(mine) + list(other) + ([] if halo is None else list(halo))
    half = mine[0].shape[-1]
    tile = (mine[0].shape[-2], half)
    shape = (2, 5) + tile if len(tiles) == len(ALL) else (len(tiles),) + tile
    full = (2, 5, tile[0], 2 * half)
    return pl.pallas_call(
        functools.partial(band_kernel, tiles, odd, len(mine), scaled, halo is not None),
        out_shape=jax.ShapeDtypeStruct(shape, jnp.float32),
        in_specs=[smem, smem, smem] + [vmem] * (len(args) - 3),
        out_specs=vmem,
        scratch_shapes=[pltpu.VMEM(full, jnp.bfloat16), pltpu.VMEM(full, jnp.bfloat16)],
    )(*args)


def block_kernel(pattern_ref, density_ref, out_ref):
    for index, (row, slot) in enumerate(DIAG):
        out_ref[index] = density_ref[row, slot] * pattern_ref[row, slot].astype(jnp.float32)


def first_block(pattern, density):
    return pl.pallas_call(
        block_kernel,
        out_shape=jax.ShapeDtypeStruct((len(DIAG),) + density.shape[2:], jnp.float32),
        in_specs=[pl.BlockSpec(memory_space=pltpu.SMEM), pl.BlockSpec(memory_space=pltpu.VMEM)],
        out_specs=pl.BlockSpec(memory_space=pltpu.VMEM),
    )(pattern, density)


def purify(density, pattern, truncation):
    side = lax.axis_index("help").astype(jnp.int32).reshape(1)
    halo = send_block(first_block(pattern, density))
    other = swap_help(density)
    diag = band_call(DIAG, False, side, pattern, truncation[0], [density], [other], scaled=True)
    next_halo = send_block(diag)
    diag_other = swap_help(diag)
    off = band_call(OFF, False, side, pattern, truncation[0], [density], [other], halo, scaled=True)
    off_other = swap_help(off)
    return band_call(ALL, True, side, pattern, truncation[1], [diag, off], [diag_other, off_other], next_halo)


def solution(mesh):
    return jax.shard_map(
        purify,
        mesh=mesh,
        in_specs=(P("rows", None, None, "help"), P("rows", None), P(None, "rows", None)),
        out_specs=P("rows", None, None, "help"),
        check_vma=False,
    )
```

time: 71.1 us -> 75.1 us (1.056)
  waiting for transfers between devices: 22.9 us -> 34.5 us
  local copies, waits for them, and re-layouts: 5.85 us -> 3.02 us
  between operations: 2.66 us -> 0.09 us
  other arithmetic: 1.17 us -> 0 us
  Pallas kernels: 20 us -> 19 us
    ppermute x2, waiting for transfers between devices: 8.38 us -> 20.1 us  [send_block(): lax.ppermute(block, 'rows', [(i + 1, i) for i in range(count - 1)])]
    slice x1 -> x0, local copies, waits for them, and re-layouts: 1.5 us -> none  [purify(): pattern[row, slot].astype(jnp.float32)]
    mul x1 -> x0, other arithmetic: 1.14 us -> none  [purify(): density[row, slot] * pattern[row, slot].astype(jnp.float32)]
    pallas_call x4, Pallas kernels: 20 us -> 19 us  [the longest x3 16.8 us: band_call(): pl.pallas_call(functools.partial(band_kernel, tiles, odd, len(mine), scal...]
  transfers between devices with their start and end apart: 6 -> 7, of which waited for: 4 -> 4; matrix products, arithmetic and copies ran while one was open for 5% -> 1% of each run, Pallas kernels for 13% -> 9%
where the time goes in v5:
time: 75.1 us; the launch traced here: 74.9 us
  waiting for transfers between devices  34.5 us (46%)
  Pallas kernels  19 us (25%)
  starting transfers between devices  18.3 us (24%)
  local copies, waits for them, and re-layouts  3.02 us (4%)
    ppermute x2, waiting for transfers between devices, send_block(): lax.ppermute(block, 'rows', [(i + 1, i) for i in range(count - 1)])  20.1 us
    pallas_call x3, Pallas kernels, band_call(): pl.pallas_call(functools.partial(band_kernel, tiles, odd, len(mine), scal...  16.8 us
    ppermute x2, waiting for transfers between devices, send_block(): lax.ppermute(block, 'rows', [(i, i + 1) for i in range(count - 1)])  14.4 us
    ppermute x2, starting transfers between devices, send_block(): lax.ppermute(block, 'rows', [(i + 1, i) for i in range(count - 1)])  12.4 us
    ppermute x2, starting transfers between devices, send_block(): lax.ppermute(block, 'rows', [(i, i + 1) for i in range(count - 1)])  5.84 us
    unnamed x16, local copies, waits for them, and re-layouts  2.44 us
    pallas_call x1, Pallas kernels, first_block(): pl.pallas_call(block_kernel, out_shape=jax.ShapeDtypeStruct((len(DIAG),)...  2.17 us
  transfers between devices with their start and end apart: 7, of which 4 were waited for; matrix products, arithmetic and copies ran while one was open for 1% of the time, Pallas kernels for 9%

profile of v5, /device:TPU:6, one launch (start us, length us, event | category | flops | bytes accessed | tf_op | source)
XLA Modules:
  0.0 74.9 jit_solution(12484263047411305101)
XLA Ops:
  0.0 0.0 copy-start.7
  0.0 0.0 collective-permute-start
  0.0 2.2 %shard_map.38 = f32[4,256,128]{2,1,0:T(8,128)} custom-call(s32[2,5]{1,0:T(2,128)} %scale_ref.5, f32[2,5,256,128]{3,2,1,0:T(8,128)} %rest_0_.3), custom_call_target="tpu_custom_call" | custom-call | tf_op jit(solution)/shard_map/pallas_call | solution.py:127
  2.2 10.5 %collective-permute-start.2 = (f32[4,256,128]{2,1,0:T(8,128)}, f32[4,256,128]{2,1,0:T(8,128)S(1)}, u32[]{:S(2)}, u32[]{:S(2)}) collective-permute-start(f32[4,256,128]{2,1,0:T(8,128)} %shard_map.38), channel_id=1, source_target_pairs={{2,0},{4,2},{6,4},{8,6},{10,8},{12,10},{14,12},{16,14},{18,16},{20... | collective-permute-start | bytes 1572872 | tf_op jit(solution)/shard_map/ppermute | solution.py:25
  12.6 1.9 %collective-permute-start.1 = (f32[4,256,128]{2,1,0:T(8,128)}, f32[4,256,128]{2,1,0:T(8,128)S(1)}, u32[]{:S(2)}, u32[]{:S(2)}) collective-permute-start(f32[4,256,128]{2,1,0:T(8,128)} %shard_map.38), channel_id=1, source_target_pairs={{0,2},{2,4},{4,6},{6,8},{8,10},{10,12},{12,14},{14,16},{16,18},{18... | collective-permute-start | bytes 1572872 | tf_op jit(solution)/shard_map/ppermute | solution.py:24
  14.6 0.0 copy-done.7
  14.6 0.6 slice_bitcast_fusion
  15.2 9.6 %collective-permute-done.2.rest_3_ = f32[4,256,128]{2,1,0:T(8,128)S(1)} collective-permute-done((f32[4,256,128]{2,1,0:T(8,128)}, f32[4,256,128]{2,1,0:T(8,128)S(1)}, u32[]{:S(2)}, u32[]{:S(2)}) %collective-permute-start.2) | collective-permute-done | bytes 524320 | tf_op jit(solution)/shard_map/ppermute | solution.py:25
  24.8 0.0 copy-start.3
  24.8 8.2 %collective-permute-done.1.rest_2_ = f32[4,256,128]{2,1,0:T(8,128)S(1)} collective-permute-done((f32[4,256,128]{2,1,0:T(8,128)}, f32[4,256,128]{2,1,0:T(8,128)S(1)}, u32[]{:S(2)}, u32[]{:S(2)}) %collective-permute-start.1) | collective-permute-done | bytes 524320 | tf_op jit(solution)/shard_map/ppermute | solution.py:24
  33.0 0.0 copy-start.5
  33.0 0.0 collective-permute-done.rest_1_
  33.0 0.0 copy-start
  33.0 0.0 copy-done.3
  33.0 0.8 %copy-done.5 = f32[4,256,128]{2,1,0:T(8,128)} copy-done((f32[4,256,128]{2,1,0:T(8,128)}, f32[4,256,128]{2,1,0:T(8,128)S(1)}, u32[]{:S(2)}) %copy-start.5) | copy-done | bytes 524312
  33.8 0.4 copy-done
  34.2 5.1 %shard_map.39.rest_1_ = f32[6,256,128]{2,1,0:T(8,128)} custom-call(s32[1]{0:T(128)} %bitcast.side_ref, s32[2,5]{1,0:T(2,128)} %scale_ref.5, s32[2,5]{1,0:T(2,128)} %get-tuple-element.5.keep_ref, f32[2,5,256,128]{3,2,1,0:T(8,128)} %rest_0_.3, f32[2,5,256,128]{3,2,1,0:T(8,128)} %copy-done, f32[4,256,128]{2,1,0:T(8,128)} %copy-done.5, f32[4,256,128]{2,1,0:T(8,128)} %copy-done.3), custom_call_target="tpu_custom_call" | custom-call | tf_op jit(solution)/shard_map/pallas_call | solution.py:112
  39.4 0.0 collective-permute-start.4
  39.4 4.6 %shard_map.37.rest_0_ = f32[4,256,128]{2,1,0:T(8,128)} custom-call(s32[1]{0:T(128)} %bitcast.side_ref, s32[2,5]{1,0:T(2,128)} %scale_ref.5, s32[2,5]{1,0:T(2,128)} %get-tuple-element.5.keep_ref, f32[2,5,256,128]{3,2,1,0:T(8,128)} %rest_0_.3, f32[2,5,256,128]{3,2,1,0:T(8,128)} %copy-done), custom_call_target="tpu_custom_call" | custom-call | tf_op jit(solution)/shard_map/pallas_call | solution.py:112
  43.9 1.9 %collective-permute-start.6 = (f32[4,256,128]{2,1,0:T(8,128)}, f32[4,256,128]{2,1,0:T(8,128)S(1)}, u32[]{:S(2)}, u32[]{:S(2)}) collective-permute-start(f32[4,256,128]{2,1,0:T(8,128)} %shard_map.37.rest_0_), channel_id=1, source_target_pairs={{2,0},{4,2},{6,4},{8,6},{10,8},{12,10},{14,12},{16,14},{18,16},{20... | collective-permute-start | bytes 1572872 | tf_op jit(solution)/shard_map/ppermute | solution.py:25
  45.8 3.9 %collective-permute-start.5 = (f32[4,256,128]{2,1,0:T(8,128)}, f32[4,256,128]{2,1,0:T(8,128)S(1)}, u32[]{:S(2)}, u32[]{:S(2)}) collective-permute-start(f32[4,256,128]{2,1,0:T(8,128)} %shard_map.37.rest_0_), channel_id=1, source_target_pairs={{0,2},{2,4},{4,6},{6,8},{8,10},{10,12},{12,14},{14,16},{16,18},{18... | collective-permute-start | bytes 1572872 | tf_op jit(solution)/shard_map/ppermute | solution.py:24
  49.8 0.1 collective-permute-start.3
  49.9 10.5 %collective-permute-done.6.rest_5_ = f32[4,256,128]{2,1,0:T(8,128)S(1)} collective-permute-done((f32[4,256,128]{2,1,0:T(8,128)}, f32[4,256,128]{2,1,0:T(8,128)S(1)}, u32[]{:S(2)}, u32[]{:S(2)}) %collective-permute-start.6) | collective-permute-done | bytes 524320 | tf_op jit(solution)/shard_map/ppermute | solution.py:25
  60.4 6.1 %collective-permute-done.5.rest_4_ = f32[4,256,128]{2,1,0:T(8,128)S(1)} collective-permute-done((f32[4,256,128]{2,1,0:T(8,128)}, f32[4,256,128]{2,1,0:T(8,128)S(1)}, u32[]{:S(2)}, u32[]{:S(2)}) %collective-permute-start.5) | collective-permute-done | bytes 524320 | tf_op jit(solution)/shard_map/ppermute | solution.py:24
  66.5 0.0 collective-permute-done.3.rest_2_
  66.5 0.0 collective-permute-done.4.rest_3_
  66.5 0.0 copy-start.1
  66.5 0.0 copy-done.2
  66.5 0.8 %copy-done.4 = f32[4,256,128]{2,1,0:T(8,128)} copy-done((f32[4,256,128]{2,1,0:T(8,128)}, f32[4,256,128]{2,1,0:T(8,128)S(1)}, u32[]{:S(2)}) %copy-start.4) | copy-done | bytes 524312
  67.3 0.2 copy-done.6
  67.5 0.3 copy-done.1
  67.7 7.1 %shard_map.40 = f32[2,5,256,128]{3,2,1,0:T(8,128)} custom-call(s32[1]{0:T(128)} %bitcast.side_ref, s32[2,5]{1,0:T(2,128)} %scale_ref.5, s32[2,5]{1,0:T(2,128)} %get-tuple-element.6.keep_ref, f32[4,256,128]{2,1,0:T(8,128)} %shard_map.37.rest_0_, f32[6,256,128]{2,1,0:T(8,128)} %shard_map.39.rest_1_, f32[4,256,128]{2,1,0:T(8,128)} %copy-done.6, ...), custom_call_target="tpu_custom_call" | custom-call | tf_op jit(solution)/shard_map/pallas_call | solution.py:112
  (3 shorter events, 0.0 us)
Async XLA Ops:
  0.0 14.6 %copy-start.7 = (s32[2,2,5]{2,1,0:T(2,128)S(1)}, s32[2,2,5]{2,1,0:T(2,128)}, u32[]{:S(2)}) copy-start(s32[2,2,5]{2,1,0:T(2,128)} %param.5) | copy-start | bytes 244
  0.0 33.0 %collective-permute-start = (f32[2,5,256,128]{3,2,1,0:T(8,128)}, f32[2,5,256,128]{3,2,1,0:T(8,128)S(1)}, u32[]{:S(2)}, u32[]{:S(2)}) collective-permute-start(f32[2,5,256,128]{3,2,1,0:T(8,128)} %rest_0_.3), channel_id=1, source_target_pairs={{0,1},{1,0},{2,3},{3,2},{4,5},{5,4},{6,7},{7,6},{8,9},{9,8},{10,11... | collective-permute-start | bytes 3932168 | tf_op jit(solution)/shard_map/ppermute | solution.py:19
  2.2 22.6 %collective-permute-start.2 = (f32[4,256,128]{2,1,0:T(8,128)}, f32[4,256,128]{2,1,0:T(8,128)S(1)}, u32[]{:S(2)}, u32[]{:S(2)}) collective-permute-start(f32[4,256,128]{2,1,0:T(8,128)} %shard_map.38), channel_id=1, source_target_pairs={{2,0},{4,2},{6,4},{8,6},{10,8},{12,10},{14,12},{16,14},{18,16},{20... | collective-permute-start | bytes 1572872 | tf_op jit(solution)/shard_map/ppermute | solution.py:25
  12.6 20.4 %collective-permute-start.1 = (f32[4,256,128]{2,1,0:T(8,128)}, f32[4,256,128]{2,1,0:T(8,128)S(1)}, u32[]{:S(2)}, u32[]{:S(2)}) collective-permute-start(f32[4,256,128]{2,1,0:T(8,128)} %shard_map.38), channel_id=1, source_target_pairs={{0,2},{2,4},{4,6},{6,8},{8,10},{10,12},{12,14},{14,16},{16,18},{18... | collective-permute-start | bytes 1572872 | tf_op jit(solution)/shard_map/ppermute | solution.py:24
  24.8 8.2 %copy-start.3 = (f32[4,256,128]{2,1,0:T(8,128)}, f32[4,256,128]{2,1,0:T(8,128)S(1)}, u32[]{:S(2)}) copy-start(f32[4,256,128]{2,1,0:T(8,128)S(1)} %collective-permute-done.2.rest_3_) | copy-start | bytes 1572868
  33.0 0.8 %copy-start.5 = (f32[4,256,128]{2,1,0:T(8,128)}, f32[4,256,128]{2,1,0:T(8,128)S(1)}, u32[]{:S(2)}) copy-start(f32[4,256,128]{2,1,0:T(8,128)S(1)} %collective-permute-done.1.rest_2_) | copy-start | bytes 1572868
  33.0 1.2 %copy-start = (f32[2,5,256,128]{3,2,1,0:T(8,128)}, f32[2,5,256,128]{3,2,1,0:T(8,128)S(1)}, u32[]{:S(2)}) copy-start(f32[2,5,256,128]{3,2,1,0:T(8,128)S(1)} %collective-permute-done.rest_1_) | copy-start | bytes 3932164
  39.4 27.1 %collective-permute-start.4 = (f32[6,256,128]{2,1,0:T(8,128)}, f32[6,256,128]{2,1,0:T(8,128)S(1)}, u32[]{:S(2)}, u32[]{:S(2)}) collective-permute-start(f32[6,256,128]{2,1,0:T(8,128)} %shard_map.39.rest_1_), channel_id=1, source_target_pairs={{0,1},{1,0},{2,3},{3,2},{4,5},{5,4},{6,7},{7,6},{8,9},{9,8},{10,11... | collective-permute-start | bytes 2359304 | tf_op jit(solution)/shard_map/ppermute | solution.py:19
  43.9 16.4 %collective-permute-start.6 = (f32[4,256,128]{2,1,0:T(8,128)}, f32[4,256,128]{2,1,0:T(8,128)S(1)}, u32[]{:S(2)}, u32[]{:S(2)}) collective-permute-start(f32[4,256,128]{2,1,0:T(8,128)} %shard_map.37.rest_0_), channel_id=1, source_target_pairs={{2,0},{4,2},{6,4},{8,6},{10,8},{12,10},{14,12},{16,14},{18,16},{20... | collective-permute-start | bytes 1572872 | tf_op jit(solution)/shard_map/ppermute | solution.py:25
  45.8 20.7 %collective-permute-start.5 = (f32[4,256,128]{2,1,0:T(8,128)}, f32[4,256,128]{2,1,0:T(8,128)S(1)}, u32[]{:S(2)}, u32[]{:S(2)}) collective-permute-start(f32[4,256,128]{2,1,0:T(8,128)} %shard_map.37.rest_0_), channel_id=1, source_target_pairs={{0,2},{2,4},{4,6},{6,8},{8,10},{10,12},{12,14},{14,16},{16,18},{18... | collective-permute-start | bytes 1572872 | tf_op jit(solution)/shard_map/ppermute | solution.py:24
  49.8 16.7 %collective-permute-start.3 = (f32[4,256,128]{2,1,0:T(8,128)}, f32[4,256,128]{2,1,0:T(8,128)S(1)}, u32[]{:S(2)}, u32[]{:S(2)}) collective-permute-start(f32[4,256,128]{2,1,0:T(8,128)} %shard_map.37.rest_0_), channel_id=1, source_target_pairs={{0,1},{1,0},{2,3},{3,2},{4,5},{5,4},{6,7},{7,6},{8,9},{9,8},{10,11... | collective-permute-start | bytes 1572872 | tf_op jit(solution)/shard_map/ppermute | solution.py:19
  60.4 6.2 %copy-start.2 = (f32[4,256,128]{2,1,0:T(8,128)}, f32[4,256,128]{2,1,0:T(8,128)S(1)}, u32[]{:S(2)}) copy-start(f32[4,256,128]{2,1,0:T(8,128)S(1)} %collective-permute-done.6.rest_5_) | copy-start | bytes 1572868
  66.5 0.8 %copy-start.4 = (f32[4,256,128]{2,1,0:T(8,128)}, f32[4,256,128]{2,1,0:T(8,128)S(1)}, u32[]{:S(2)}) copy-start(f32[4,256,128]{2,1,0:T(8,128)S(1)} %collective-permute-done.5.rest_4_) | copy-start | bytes 1572868
  66.5 1.0 %copy-start.6 = (f32[4,256,128]{2,1,0:T(8,128)}, f32[4,256,128]{2,1,0:T(8,128)S(1)}, u32[]{:S(2)}) copy-start(f32[4,256,128]{2,1,0:T(8,128)S(1)} %collective-permute-done.3.rest_2_) | copy-start | bytes 1572868
  66.5 1.2 %copy-start.1 = (f32[6,256,128]{2,1,0:T(8,128)}, f32[6,256,128]{2,1,0:T(8,128)S(1)}, u32[]{:S(2)}) copy-start(f32[6,256,128]{2,1,0:T(8,128)S(1)} %collective-permute-done.4.rest_3_) | copy-start | bytes 2359300

commit v6 on v5

--- a/solution.py
+++ b/solution.py
@@ -12,7 +12,6 @@
 OFF = ((0, 0), (0, 1), (0, 4), (1, 0), (1, 3), (1, 4))
 ALL = tuple((row, slot) for row in range(2) for slot in range(5))
 CONTRACT = (((1,), (0,)), ((), ()))
-CONTRACT_T = (((1,), (1,)), ((), ()))
 
 
 def swap_help(value):
@@ -29,13 +28,6 @@
 def split(x):
     high = x.astype(jnp.bfloat16)
     return high, (x - high.astype(jnp.float32)).astype(jnp.bfloat16)
-
-
-def dot3(a_high, a_low, b, dims):
-    b_high, b_low = split(b)
-    def one(x, y):
-        return lax.dot_general(x, y, dims, preferred_element_type=jnp.float32)
-    return one(a_low, b_high) + one(a_high, b_low) + one(a_high, b_high)
 
 
 class Tiles:
@@ -62,43 +54,56 @@
     if halo:
         left_ref, right_ref = rest[:2]
         rest = rest[2:]
-    out_ref, high_ref, low_ref = rest
-    half = high_ref.shape[3] // 2
+    out_ref, lh_ref, ll_ref, rh_ref, rl_ref = rest
+    tile = lh_ref.shape[1]
+    half = tile // 2
     side = side_ref[0]
     own = pl.ds(pl.multiple_of(side * half, half), half)
     far = pl.ds(pl.multiple_of((1 - side) * half, half), half)
+    by_row = [[(index, slot) for index, (row, slot) in enumerate(tiles) if row == r] for r in range(2)]
 
     for row in range(2):
         for slot in range(5):
             high, low = split(jnp.concatenate([mine(row, slot), other(row, slot)], axis=1))
-            high_ref[row, slot] = high
-            low_ref[row, slot] = low
-    for index, (row, slot) in enumerate(tiles):
-        col = row + slot - 2
-        acc = jnp.zeros((high_ref.shape[2], half), jnp.float32)
-        for k in range(max(row, col) - 2, min(row, col) + 3):
-            a_high = high_ref[row, k - row + 2]
-            a_low = low_ref[row, k - row + 2]
-            if k in (0, 1):
-                b = col - k + 2
-                right = jnp.concatenate([mine(k, b, own), mine(k, b, far)], axis=0)
-                acc += dot3(a_high, a_low, right, CONTRACT)
-            elif col not in (0, 1):
-                src = left_ref if k < 0 else right_ref
-                b = 2 * (k + 2) + (col + 2) if k < 0 else 2 * (k - 2) + (col - 2)
-                right = jnp.concatenate([src[b, own, :], src[b, far, :]], axis=0)
-                acc += dot3(a_high, a_low, right, CONTRACT)
+            lh_ref[row, :, slot * tile : (slot + 1) * tile] = high
+            ll_ref[row, :, slot * tile : (slot + 1) * tile] = low
+        for offset in range(5):
+            k = row + offset - 2
+            for place, (index, slot) in enumerate(by_row[row]):
+                col = row + slot - 2
+                where = (row, slice(offset * tile, (offset + 1) * tile), slice(place * half, (place + 1) * half))
+                if abs(k - col) > 2:
+                    rh_ref[where] = jnp.zeros((tile, half), jnp.bfloat16)
+                    rl_ref[where] = jnp.zeros((tile, half), jnp.bfloat16)
+                    continue
+                if k in (0, 1):
+                    b = col - k + 2
+                    right = jnp.concatenate([mine(k, b, own), mine(k, b, far)], axis=0)
+                elif col not in (0, 1):
+                    src = left_ref if k < 0 else right_ref
+                    b = 2 * (k + 2) + (col + 2) if k < 0 else 2 * (k - 2) + (col - 2)
+                    right = jnp.concatenate([src[b, own, :], src[b, far, :]], axis=0)
+                else:
+                    s = k - col + 2
+                    right = jnp.concatenate([mine(col, s, own), other(col, s, own)], axis=1).T
+                high, low = split(right)
+                rh_ref[where] = high
+                rl_ref[where] = low
+    for row in range(2):
+        def one(x, y):
+            return lax.dot_general(x, y, CONTRACT, preferred_element_type=jnp.float32)
+        a_high = lh_ref[row]
+        b_high = rh_ref[row]
+        acc = one(ll_ref[row], b_high) + one(a_high, rl_ref[row]) + one(a_high, b_high)
+        for place, (index, slot) in enumerate(by_row[row]):
+            value = acc[:, place * half : (place + 1) * half]
+            if odd:
+                value = 2.0 * mine(row, slot) - value
+            value = value * keep_ref[row, slot].astype(jnp.float32)
+            if len(tiles) == len(ALL):
+                out_ref[row, slot] = value
             else:
-                s = k - col + 2
-                flipped = jnp.concatenate([mine(col, s, own), other(col, s, own)], axis=1)
-                acc += dot3(a_high, a_low, flipped, CONTRACT_T)
-        if odd:
-            acc = 2.0 * mine(row, slot) - acc
-        value = acc * keep_ref[row, slot].astype(jnp.float32)
-        if len(tiles) == len(ALL):
-            out_ref[row, slot] = value
-        else:
-            out_ref[index] = value
+                out_ref[index] = value
 
 
 def band_call(tiles, odd, side, scale, keep, mine, other, halo=None, scaled=False):
@@ -108,13 +113,15 @@
     half = mine[0].shape[-1]
     tile = (mine[0].shape[-2], half)
     shape = (2, 5) + tile if len(tiles) == len(ALL) else (len(tiles),) + tile
-    full = (2, 5, tile[0], 2 * half)
+    width = len(tiles) // 2
+    lefts = (2, tile[0], 5 * 2 * half)
+    rights = (2, 5 * tile[0], width * half)
     return pl.pallas_call(
         functools.partial(band_kernel, tiles, odd, len(mine), scaled, halo is not None),
         out_shape=jax.ShapeDtypeStruct(shape, jnp.float32),
         in_specs=[smem, smem, smem] + [vmem] * (len(args) - 3),
         out_specs=vmem,
-        scratch_shapes=[pltpu.VMEM(full, jnp.bfloat16), pltpu.VMEM(full, jnp.bfloat16)],
+        scratch_shapes=[pltpu.VMEM(lefts, jnp.bfloat16)] * 2 + [pltpu.VMEM(rights, jnp.bfloat16)] * 2,
     )(*args)
 
 

time: 75.1 us -> 74.8 us (level)
  no operation moved by 1% of the time
where the time goes in v6:
time: 74.8 us; the launch traced here: 74.6 us
  waiting for transfers between devices  34.5 us (46%)
  Pallas kernels  18.6 us (25%)
  starting transfers between devices  18.3 us (24%)
  local copies, waits for them, and re-layouts  3.02 us (4%)
    ppermute x2, waiting for transfers between devices, send_block(): lax.ppermute(block, 'rows', [(i + 1, i) for i in range(count - 1)])  20.1 us
    pallas_call x3, Pallas kernels, band_call(): pl.pallas_call(functools.partial(band_kernel, tiles, odd, len(mine), scal...  16.5 us
    ppermute x2, waiting for transfers between devices, send_block(): lax.ppermute(block, 'rows', [(i, i + 1) for i in range(count - 1)])  14.4 us
    ppermute x2, starting transfers between devices, send_block(): lax.ppermute(block, 'rows', [(i + 1, i) for i in range(count - 1)])  12.4 us
    ppermute x2, starting transfers between devices, send_block(): lax.ppermute(block, 'rows', [(i, i + 1) for i in range(count - 1)])  5.84 us
    unnamed x16, local copies, waits for them, and re-layouts  2.44 us
    pallas_call x1, Pallas kernels, first_block(): pl.pallas_call(block_kernel, out_shape=jax.ShapeDtypeStruct((len(DIAG),)...  2.17 us
  transfers between devices with their start and end apart: 7, of which 4 were waited for; matrix products, arithmetic and copies ran while one was open for 1% of the time, Pallas kernels for 9%

profile of v6, /device:TPU:6, one launch (start us, length us, event | category | flops | bytes accessed | tf_op | source)
XLA Modules:
  0.0 74.6 jit_solution(8807259104790619114)
XLA Ops:
  0.0 0.0 copy-start.7
  0.0 0.0 collective-permute-start
  0.0 2.2 %shard_map.38 = f32[4,256,128]{2,1,0:T(8,128)} custom-call(s32[2,5]{1,0:T(2,128)} %scale_ref.5, f32[2,5,256,128]{3,2,1,0:T(8,128)} %rest_0_.3), custom_call_target="tpu_custom_call" | custom-call | tf_op jit(solution)/shard_map/pallas_call | solution.py:134
  2.2 10.5 %collective-permute-start.2 = (f32[4,256,128]{2,1,0:T(8,128)}, f32[4,256,128]{2,1,0:T(8,128)S(1)}, u32[]{:S(2)}, u32[]{:S(2)}) collective-permute-start(f32[4,256,128]{2,1,0:T(8,128)} %shard_map.38), channel_id=1, source_target_pairs={{2,0},{4,2},{6,4},{8,6},{10,8},{12,10},{14,12},{16,14},{18,16},{20... | collective-permute-start | bytes 1572872 | tf_op jit(solution)/shard_map/ppermute | solution.py:24
  12.6 1.9 %collective-permute-start.1 = (f32[4,256,128]{2,1,0:T(8,128)}, f32[4,256,128]{2,1,0:T(8,128)S(1)}, u32[]{:S(2)}, u32[]{:S(2)}) collective-permute-start(f32[4,256,128]{2,1,0:T(8,128)} %shard_map.38), channel_id=1, source_target_pairs={{0,2},{2,4},{4,6},{6,8},{8,10},{10,12},{12,14},{14,16},{16,18},{18... | collective-permute-start | bytes 1572872 | tf_op jit(solution)/shard_map/ppermute | solution.py:23
  14.6 0.0 copy-done.7
  14.6 0.6 slice_bitcast_fusion
  15.2 9.6 %collective-permute-done.2.rest_3_ = f32[4,256,128]{2,1,0:T(8,128)S(1)} collective-permute-done((f32[4,256,128]{2,1,0:T(8,128)}, f32[4,256,128]{2,1,0:T(8,128)S(1)}, u32[]{:S(2)}, u32[]{:S(2)}) %collective-permute-start.2) | collective-permute-done | bytes 524320 | tf_op jit(solution)/shard_map/ppermute | solution.py:24
  24.8 0.0 copy-start.3
  24.8 8.2 %collective-permute-done.1.rest_2_ = f32[4,256,128]{2,1,0:T(8,128)S(1)} collective-permute-done((f32[4,256,128]{2,1,0:T(8,128)}, f32[4,256,128]{2,1,0:T(8,128)S(1)}, u32[]{:S(2)}, u32[]{:S(2)}) %collective-permute-start.1) | collective-permute-done | bytes 524320 | tf_op jit(solution)/shard_map/ppermute | solution.py:23
  33.0 0.0 copy-start.5
  33.0 0.0 collective-permute-done.rest_1_
  33.0 0.0 copy-start
  33.0 0.0 copy-done.3
  33.0 0.8 %copy-done.5 = f32[4,256,128]{2,1,0:T(8,128)} copy-done((f32[4,256,128]{2,1,0:T(8,128)}, f32[4,256,128]{2,1,0:T(8,128)S(1)}, u32[]{:S(2)}) %copy-start.5) | copy-done | bytes 524312
  33.8 0.4 copy-done
  34.2 5.5 %shard_map.39.rest_1_ = f32[6,256,128]{2,1,0:T(8,128)} custom-call(s32[1]{0:T(128)} %bitcast.side_ref, s32[2,5]{1,0:T(2,128)} %scale_ref.5, s32[2,5]{1,0:T(2,128)} %get-tuple-element.5.keep_ref, f32[2,5,256,128]{3,2,1,0:T(8,128)} %rest_0_.3, f32[2,5,256,128]{3,2,1,0:T(8,128)} %copy-done, f32[4,256,128]{2,1,0:T(8,128)} %copy-done.5, f32[4,256,128]{2,1,0:T(8,128)} %copy-done.3), custom_call_target="tpu_custom_call" | custom-call | tf_op jit(solution)/shard_map/pallas_call | solution.py:119
  39.7 0.0 collective-permute-start.4
  39.7 4.2 %shard_map.37.rest_0_ = f32[4,256,128]{2,1,0:T(8,128)} custom-call(s32[1]{0:T(128)} %bitcast.side_ref, s32[2,5]{1,0:T(2,128)} %scale_ref.5, s32[2,5]{1,0:T(2,128)} %get-tuple-element.5.keep_ref, f32[2,5,256,128]{3,2,1,0:T(8,128)} %rest_0_.3, f32[2,5,256,128]{3,2,1,0:T(8,128)} %copy-done), custom_call_target="tpu_custom_call" | custom-call | tf_op jit(solution)/shard_map/pallas_call | solution.py:119
  43.9 1.9 %collective-permute-start.6 = (f32[4,256,128]{2,1,0:T(8,128)}, f32[4,256,128]{2,1,0:T(8,128)S(1)}, u32[]{:S(2)}, u32[]{:S(2)}) collective-permute-start(f32[4,256,128]{2,1,0:T(8,128)} %shard_map.37.rest_0_), channel_id=1, source_target_pairs={{2,0},{4,2},{6,4},{8,6},{10,8},{12,10},{14,12},{16,14},{18,16},{20... | collective-permute-start | bytes 1572872 | tf_op jit(solution)/shard_map/ppermute | solution.py:24
  45.8 3.9 %collective-permute-start.5 = (f32[4,256,128]{2,1,0:T(8,128)}, f32[4,256,128]{2,1,0:T(8,128)S(1)}, u32[]{:S(2)}, u32[]{:S(2)}) collective-permute-start(f32[4,256,128]{2,1,0:T(8,128)} %shard_map.37.rest_0_), channel_id=1, source_target_pairs={{0,2},{2,4},{4,6},{6,8},{8,10},{10,12},{12,14},{14,16},{16,18},{18... | collective-permute-start | bytes 1572872 | tf_op jit(solution)/shard_map/ppermute | solution.py:23
  49.8 0.1 collective-permute-start.3
  49.9 10.5 %collective-permute-done.6.rest_5_ = f32[4,256,128]{2,1,0:T(8,128)S(1)} collective-permute-done((f32[4,256,128]{2,1,0:T(8,128)}, f32[4,256,128]{2,1,0:T(8,128)S(1)}, u32[]{:S(2)}, u32[]{:S(2)}) %collective-permute-start.6) | collective-permute-done | bytes 524320 | tf_op jit(solution)/shard_map/ppermute | solution.py:24
  60.4 6.1 %collective-permute-done.5.rest_4_ = f32[4,256,128]{2,1,0:T(8,128)S(1)} collective-permute-done((f32[4,256,128]{2,1,0:T(8,128)}, f32[4,256,128]{2,1,0:T(8,128)S(1)}, u32[]{:S(2)}, u32[]{:S(2)}) %collective-permute-start.5) | collective-permute-done | bytes 524320 | tf_op jit(solution)/shard_map/ppermute | solution.py:23
  66.5 0.0 collective-permute-done.3.rest_2_
  66.5 0.0 collective-permute-done.4.rest_3_
  66.5 0.0 copy-start.1
  66.5 0.0 copy-done.2
  66.5 0.8 %copy-done.4 = f32[4,256,128]{2,1,0:T(8,128)} copy-done((f32[4,256,128]{2,1,0:T(8,128)}, f32[4,256,128]{2,1,0:T(8,128)S(1)}, u32[]{:S(2)}) %copy-start.4) | copy-done | bytes 524312
  67.3 0.2 copy-done.6
  67.5 0.3 copy-done.1
  67.7 6.8 %shard_map.40 = f32[2,5,256,128]{3,2,1,0:T(8,128)} custom-call(s32[1]{0:T(128)} %bitcast.side_ref, s32[2,5]{1,0:T(2,128)} %scale_ref.5, s32[2,5]{1,0:T(2,128)} %get-tuple-element.6.keep_ref, f32[4,256,128]{2,1,0:T(8,128)} %shard_map.37.rest_0_, f32[6,256,128]{2,1,0:T(8,128)} %shard_map.39.rest_1_, f32[4,256,128]{2,1,0:T(8,128)} %copy-done.6, ...), custom_call_target="tpu_custom_call" | custom-call | tf_op jit(solution)/shard_map/pallas_call | solution.py:119
  (3 shorter events, 0.0 us)
Async XLA Ops:
  0.0 14.6 %copy-start.7 = (s32[2,2,5]{2,1,0:T(2,128)S(1)}, s32[2,2,5]{2,1,0:T(2,128)}, u32[]{:S(2)}) copy-start(s32[2,2,5]{2,1,0:T(2,128)} %param.5) | copy-start | bytes 244
  0.0 33.0 %collective-permute-start = (f32[2,5,256,128]{3,2,1,0:T(8,128)}, f32[2,5,256,128]{3,2,1,0:T(8,128)S(1)}, u32[]{:S(2)}, u32[]{:S(2)}) collective-permute-start(f32[2,5,256,128]{3,2,1,0:T(8,128)} %rest_0_.3), channel_id=1, source_target_pairs={{0,1},{1,0},{2,3},{3,2},{4,5},{5,4},{6,7},{7,6},{8,9},{9,8},{10,11... | collective-permute-start | bytes 3932168 | tf_op jit(solution)/shard_map/ppermute | solution.py:18
  2.2 22.6 %collective-permute-start.2 = (f32[4,256,128]{2,1,0:T(8,128)}, f32[4,256,128]{2,1,0:T(8,128)S(1)}, u32[]{:S(2)}, u32[]{:S(2)}) collective-permute-start(f32[4,256,128]{2,1,0:T(8,128)} %shard_map.38), channel_id=1, source_target_pairs={{2,0},{4,2},{6,4},{8,6},{10,8},{12,10},{14,12},{16,14},{18,16},{20... | collective-permute-start | bytes 1572872 | tf_op jit(solution)/shard_map/ppermute | solution.py:24
  12.6 20.4 %collective-permute-start.1 = (f32[4,256,128]{2,1,0:T(8,128)}, f32[4,256,128]{2,1,0:T(8,128)S(1)}, u32[]{:S(2)}, u32[]{:S(2)}) collective-permute-start(f32[4,256,128]{2,1,0:T(8,128)} %shard_map.38), channel_id=1, source_target_pairs={{0,2},{2,4},{4,6},{6,8},{8,10},{10,12},{12,14},{14,16},{16,18},{18... | collective-permute-start | bytes 1572872 | tf_op jit(solution)/shard_map/ppermute | solution.py:23
  24.8 8.2 %copy-start.3 = (f32[4,256,128]{2,1,0:T(8,128)}, f32[4,256,128]{2,1,0:T(8,128)S(1)}, u32[]{:S(2)}) copy-start(f32[4,256,128]{2,1,0:T(8,128)S(1)} %collective-permute-done.2.rest_3_) | copy-start | bytes 1572868
  33.0 0.8 %copy-start.5 = (f32[4,256,128]{2,1,0:T(8,128)}, f32[4,256,128]{2,1,0:T(8,128)S(1)}, u32[]{:S(2)}) copy-start(f32[4,256,128]{2,1,0:T(8,128)S(1)} %collective-permute-done.1.rest_2_) | copy-start | bytes 1572868
  33.0 1.2 %copy-start = (f32[2,5,256,128]{3,2,1,0:T(8,128)}, f32[2,5,256,128]{3,2,1,0:T(8,128)S(1)}, u32[]{:S(2)}) copy-start(f32[2,5,256,128]{3,2,1,0:T(8,128)S(1)} %collective-permute-done.rest_1_) | copy-start | bytes 3932164
  39.7 26.8 %collective-permute-start.4 = (f32[6,256,128]{2,1,0:T(8,128)}, f32[6,256,128]{2,1,0:T(8,128)S(1)}, u32[]{:S(2)}, u32[]{:S(2)}) collective-permute-start(f32[6,256,128]{2,1,0:T(8,128)} %shard_map.39.rest_1_), channel_id=1, source_target_pairs={{0,1},{1,0},{2,3},{3,2},{4,5},{5,4},{6,7},{7,6},{8,9},{9,8},{10,11... | collective-permute-start | bytes 2359304 | tf_op jit(solution)/shard_map/ppermute | solution.py:18
  43.9 16.4 %collective-permute-start.6 = (f32[4,256,128]{2,1,0:T(8,128)}, f32[4,256,128]{2,1,0:T(8,128)S(1)}, u32[]{:S(2)}, u32[]{:S(2)}) collective-permute-start(f32[4,256,128]{2,1,0:T(8,128)} %shard_map.37.rest_0_), channel_id=1, source_target_pairs={{2,0},{4,2},{6,4},{8,6},{10,8},{12,10},{14,12},{16,14},{18,16},{20... | collective-permute-start | bytes 1572872 | tf_op jit(solution)/shard_map/ppermute | solution.py:24
  45.8 20.7 %collective-permute-start.5 = (f32[4,256,128]{2,1,0:T(8,128)}, f32[4,256,128]{2,1,0:T(8,128)S(1)}, u32[]{:S(2)}, u32[]{:S(2)}) collective-permute-start(f32[4,256,128]{2,1,0:T(8,128)} %shard_map.37.rest_0_), channel_id=1, source_target_pairs={{0,2},{2,4},{4,6},{6,8},{8,10},{10,12},{12,14},{14,16},{16,18},{18... | collective-permute-start | bytes 1572872 | tf_op jit(solution)/shard_map/ppermute | solution.py:23
  49.8 16.7 %collective-permute-start.3 = (f32[4,256,128]{2,1,0:T(8,128)}, f32[4,256,128]{2,1,0:T(8,128)S(1)}, u32[]{:S(2)}, u32[]{:S(2)}) collective-permute-start(f32[4,256,128]{2,1,0:T(8,128)} %shard_map.37.rest_0_), channel_id=1, source_target_pairs={{0,1},{1,0},{2,3},{3,2},{4,5},{5,4},{6,7},{7,6},{8,9},{9,8},{10,11... | collective-permute-start | bytes 1572872 | tf_op jit(solution)/shard_map/ppermute | solution.py:18
  60.4 6.2 %copy-start.2 = (f32[4,256,128]{2,1,0:T(8,128)}, f32[4,256,128]{2,1,0:T(8,128)S(1)}, u32[]{:S(2)}) copy-start(f32[4,256,128]{2,1,0:T(8,128)S(1)} %collective-permute-done.6.rest_5_) | copy-start | bytes 1572868
  66.5 0.8 %copy-start.4 = (f32[4,256,128]{2,1,0:T(8,128)}, f32[4,256,128]{2,1,0:T(8,128)S(1)}, u32[]{:S(2)}) copy-start(f32[4,256,128]{2,1,0:T(8,128)S(1)} %collective-permute-done.5.rest_4_) | copy-start | bytes 1572868
  66.5 1.0 %copy-start.6 = (f32[4,256,128]{2,1,0:T(8,128)}, f32[4,256,128]{2,1,0:T(8,128)S(1)}, u32[]{:S(2)}) copy-start(f32[4,256,128]{2,1,0:T(8,128)S(1)} %collective-permute-done.3.rest_2_) | copy-start | bytes 1572868
  66.5 1.2 %copy-start.1 = (f32[6,256,128]{2,1,0:T(8,128)}, f32[6,256,128]{2,1,0:T(8,128)S(1)}, u32[]{:S(2)}) copy-start(f32[6,256,128]{2,1,0:T(8,128)S(1)} %collective-permute-done.4.rest_3_) | copy-start | bytes 2359300

commit v7 on v6

--- a/solution.py
+++ b/solution.py
@@ -47,19 +47,49 @@
         return value
 
 
-def band_kernel(tiles, odd, parts, scaled, halo, side_ref, scale_ref, keep_ref, *rest):
+QUARTERS = ((0, 2), (0, 3), (1, 2))
+FROM_QUARTER = {(0, 2): (0, False, (0, 2)), (0, 3): (1, False, (1, 1)), (1, 1): (1, True, (0, 3)), (1, 2): (2, False, (1, 2))}
+
+
+class Rebuilt:
+    def __init__(self, quarter_ref, off_ref, mine, side, own, far):
+        self.quarter_ref, self.off_ref, self.mine = quarter_ref, off_ref, mine
+        self.side, self.own, self.far = side, own, far
+
+    def __call__(self, row, slot, rows=slice(None)):
+        if (row, slot) not in DIAG:
+            return self.off_ref[OFF.index((row, slot)), rows, :]
+        index, flip, source = FROM_QUARTER[(row, slot)]
+        quarter = self.quarter_ref[index]
+        far_rows = quarter.T if flip else quarter
+        own_rows = self.mine(source[0], source[1], self.far).T
+        return jnp.where(
+            self.side == 0,
+            jnp.concatenate([own_rows, far_rows], axis=0),
+            jnp.concatenate([far_rows, own_rows], axis=0),
+        )
+
+
+def band_kernel(tiles, odd, parts, scaled, halo, quarters, side_ref, scale_ref, keep_ref, *rest):
     mine = Tiles(rest[:parts], scale_ref if scaled else None)
-    other = Tiles(rest[parts : 2 * parts], scale_ref if scaled else None)
+    other_refs = rest[parts : 2 * parts]
     rest = rest[2 * parts :]
     if halo:
         left_ref, right_ref = rest[:2]
         rest = rest[2:]
-    out_ref, lh_ref, ll_ref, rh_ref, rl_ref = rest
+    if quarters:
+        out_ref, quarter_ref, lh_ref, ll_ref, rh_ref, rl_ref = rest
+    else:
+        out_ref, lh_ref, ll_ref, rh_ref, rl_ref = rest
     tile = lh_ref.shape[1]
     half = tile // 2
     side = side_ref[0]
     own = pl.ds(pl.multiple_of(side * half, half), half)
     far = pl.ds(pl.multiple_of((1 - side) * half, half), half)
+    if other_refs[0].shape[-2] == half:
+        other = Rebuilt(other_refs[0], other_refs[1], mine, side, own, far)
+    else:
+        other = Tiles(other_refs, scale_ref if scaled else None)
     by_row = [[(index, slot) for index, (row, slot) in enumerate(tiles) if row == r] for r in range(2)]
 
     for row in range(2):
@@ -92,6 +122,7 @@
     for row in range(2):
         def one(x, y):
             return lax.dot_general(x, y, CONTRACT, preferred_element_type=jnp.float32)
+
         a_high = lh_ref[row]
         b_high = rh_ref[row]
         acc = one(ll_ref[row], b_high) + one(a_high, rl_ref[row]) + one(a_high, b_high)
@@ -104,9 +135,12 @@
                 out_ref[row, slot] = value
             else:
                 out_ref[index] = value
+    if quarters:
+        for index, key in enumerate(QUARTERS):
+            quarter_ref[index] = out_ref[tiles.index(key), own, :]
 
 
-def band_call(tiles, odd, side, scale, keep, mine, other, halo=None, scaled=False):
+def band_call(tiles, odd, side, scale, keep, mine, other, halo=None, scaled=False, quarters=False):
     smem = pl.BlockSpec(memory_space=pltpu.SMEM)
     vmem = pl.BlockSpec(memory_space=pltpu.VMEM)
     args = [side, scale, keep] + list(mine) + list(other) + ([] if halo is None else list(halo))
@@ -116,11 +150,14 @@
     width = len(tiles) // 2
     lefts = (2, tile[0], 5 * 2 * half)
     rights = (2, 5 * tile[0], width * half)
+    out_shape = jax.ShapeDtypeStruct(shape, jnp.float32)
+    if quarters:
+        out_shape = (out_shape, jax.ShapeDtypeStruct((len(QUARTERS), half, half), jnp.float32))
     return pl.pallas_call(
-        functools.partial(band_kernel, tiles, odd, len(mine), scaled, halo is not None),
-        out_shape=jax.ShapeDtypeStruct(shape, jnp.float32),
+        functools.partial(band_kernel, tiles, odd, len(mine), scaled, halo is not None, quarters),
+        out_shape=out_shape,
         in_specs=[smem, smem, smem] + [vmem] * (len(args) - 3),
-        out_specs=vmem,
+        out_specs=(vmem, vmem) if quarters else vmem,
         scratch_shapes=[pltpu.VMEM(lefts, jnp.bfloat16)] * 2 + [pltpu.VMEM(rights, jnp.bfloat16)] * 2,
     )(*args)
 
@@ -143,12 +180,12 @@
     side = lax.axis_index("help").astype(jnp.int32).reshape(1)
     halo = send_block(first_block(pattern, density))
     other = swap_help(density)
-    diag = band_call(DIAG, False, side, pattern, truncation[0], [density], [other], scaled=True)
+    diag, quarter = band_call(DIAG, False, side, pattern, truncation[0], [density], [other], scaled=True, quarters=True)
     next_halo = send_block(diag)
-    diag_other = swap_help(diag)
+    quarter_other = swap_help(quarter)
     off = band_call(OFF, False, side, pattern, truncation[0], [density], [other], halo, scaled=True)
     off_other = swap_help(off)
-    return band_call(ALL, True, side, pattern, truncation[1], [diag, off], [diag_other, off_other], next_halo)
+    return band_call(ALL, True, side, pattern, truncation[1], [diag, off], [quarter_other, off_other], next_halo)
 
 
 def solution(mesh):

time: 74.8 us -> 74.6 us (level)
    ppermute x2, waiting for transfers between devices: 20.1 us -> 18.4 us  [send_block(): lax.ppermute(block, 'rows', [(i + 1, i) for i in range(count - 1)])]
    ppermute x3, waiting for transfers between devices: 0.01 us -> 1.64 us  [swap_help(): return lax.ppermute(value, 'help', [(0, 1), (1, 0)])]
  transfers between devices with their start and end apart: 7 -> 7, of which waited for: 4 -> 5; matrix products, arithmetic and copies ran while one was open for 1% -> 1% of each run, Pallas kernels for 9% -> 9%
where the time goes in v7:
time: 74.6 us; the launch traced here: 74.3 us
  waiting for transfers between devices  34.5 us (46%)
  Pallas kernels  18.6 us (25%)
  starting transfers between devices  18.3 us (25%)
  local copies, waits for them, and re-layouts  2.89 us (4%)
    ppermute x2, waiting for transfers between devices, send_block(): lax.ppermute(block, 'rows', [(i + 1, i) for i in range(count - 1)])  18.4 us
    pallas_call x3, Pallas kernels, band_call(): pl.pallas_call(functools.partial(band_kernel, tiles, odd, len(mine), scal...  16.4 us
    ppermute x2, waiting for transfers between devices, send_block(): lax.ppermute(block, 'rows', [(i, i + 1) for i in range(count - 1)])  14.4 us
    ppermute x2, starting transfers between devices, send_block(): lax.ppermute(block, 'rows', [(i + 1, i) for i in range(count - 1)])  12.4 us
    ppermute x2, starting transfers between devices, send_block(): lax.ppermute(block, 'rows', [(i, i + 1) for i in range(count - 1)])  5.84 us
    unnamed x16, local copies, waits for them, and re-layouts  2.3 us
    pallas_call x1, Pallas kernels, first_block(): pl.pallas_call(block_kernel, out_shape=jax.ShapeDtypeStruct((len(DIAG),)...  2.17 us
    ppermute x3, waiting for transfers between devices, swap_help(): return lax.ppermute(value, 'help', [(0, 1), (1, 0)])  1.64 us
  transfers between devices with their start and end apart: 7, of which 5 were waited for; matrix products, arithmetic and copies ran while one was open for 1% of the time, Pallas kernels for 9%

profile of v7, /device:TPU:6, one launch (start us, length us, event | category | flops | bytes accessed | tf_op | source)
XLA Modules:
  0.0 74.3 jit_solution(4281797843029572276)
XLA Ops:
  0.0 0.0 copy-start.7
  0.0 0.0 collective-permute-start
  0.0 2.2 %shard_map.38 = f32[4,256,128]{2,1,0:T(8,128)} custom-call(s32[2,5]{1,0:T(2,128)} %scale_ref.5, f32[2,5,256,128]{3,2,1,0:T(8,128)} %rest_0_.3), custom_call_target="tpu_custom_call" | custom-call | tf_op jit(solution)/shard_map/pallas_call | solution.py:171
  2.2 10.5 %collective-permute-start.2 = (f32[4,256,128]{2,1,0:T(8,128)}, f32[4,256,128]{2,1,0:T(8,128)S(1)}, u32[]{:S(2)}, u32[]{:S(2)}) collective-permute-start(f32[4,256,128]{2,1,0:T(8,128)} %shard_map.38), channel_id=1, source_target_pairs={{2,0},{4,2},{6,4},{8,6},{10,8},{12,10},{14,12},{16,14},{18,16},{20... | collective-permute-start | bytes 1572872 | tf_op jit(solution)/shard_map/ppermute | solution.py:24
  12.6 1.9 %collective-permute-start.1 = (f32[4,256,128]{2,1,0:T(8,128)}, f32[4,256,128]{2,1,0:T(8,128)S(1)}, u32[]{:S(2)}, u32[]{:S(2)}) collective-permute-start(f32[4,256,128]{2,1,0:T(8,128)} %shard_map.38), channel_id=1, source_target_pairs={{0,2},{2,4},{4,6},{6,8},{8,10},{10,12},{12,14},{14,16},{16,18},{18... | collective-permute-start | bytes 1572872 | tf_op jit(solution)/shard_map/ppermute | solution.py:23
  14.6 0.0 copy-done.7
  14.6 0.6 slice_bitcast_fusion
  15.2 9.6 %collective-permute-done.2.rest_3_ = f32[4,256,128]{2,1,0:T(8,128)S(1)} collective-permute-done((f32[4,256,128]{2,1,0:T(8,128)}, f32[4,256,128]{2,1,0:T(8,128)S(1)}, u32[]{:S(2)}, u32[]{:S(2)}) %collective-permute-start.2) | collective-permute-done | bytes 524320 | tf_op jit(solution)/shard_map/ppermute | solution.py:24
  24.8 0.0 copy-start.4
  24.8 8.2 %collective-permute-done.1.rest_2_ = f32[4,256,128]{2,1,0:T(8,128)S(1)} collective-permute-done((f32[4,256,128]{2,1,0:T(8,128)}, f32[4,256,128]{2,1,0:T(8,128)S(1)}, u32[]{:S(2)}, u32[]{:S(2)}) %collective-permute-start.1) | collective-permute-done | bytes 524320 | tf_op jit(solution)/shard_map/ppermute | solution.py:23
  33.0 0.0 copy-start.5
  33.0 0.0 collective-permute-done.rest_1_
  33.0 0.0 copy-start
  33.0 0.0 copy-done.4
  33.0 0.8 %copy-done.5 = f32[4,256,128]{2,1,0:T(8,128)} copy-done((f32[4,256,128]{2,1,0:T(8,128)}, f32[4,256,128]{2,1,0:T(8,128)S(1)}, u32[]{:S(2)}) %copy-start.5) | copy-done | bytes 524312
  33.8 0.4 copy-done
  34.2 5.4 %shard_map.39.rest_1_ = f32[6,256,128]{2,1,0:T(8,128)} custom-call(s32[1]{0:T(128)} %bitcast.side_ref, s32[2,5]{1,0:T(2,128)} %scale_ref.5, s32[2,5]{1,0:T(2,128)} %get-tuple-element.9.keep_ref, f32[2,5,256,128]{3,2,1,0:T(8,128)} %rest_0_.3, f32[2,5,256,128]{3,2,1,0:T(8,128)} %copy-done, f32[4,256,128]{2,1,0:T(8,128)} %copy-done.5, f32[4,256,128]{2,1,0:T(8,128)} %copy-done.4), custom_call_target="tpu_custom_call" | custom-call | tf_op jit(solution)/shard_map/pallas_call | solution.py:156
  39.7 0.0 collective-permute-start.4
  39.7 4.3 %shard_map.37 = (f32[4,256,128]{2,1,0:T(8,128)}, f32[3,128,128]{2,1,0:T(8,128)}) custom-call(s32[1]{0:T(128)} %bitcast.side_ref, s32[2,5]{1,0:T(2,128)} %scale_ref.5, s32[2,5]{1,0:T(2,128)} %get-tuple-element.9.keep_ref, f32[2,5,256,128]{3,2,1,0:T(8,128)} %rest_0_.3, f32[2,5,256,128]{3,2,1,0:T(8,128)} %copy-done), custom_call_target="tpu_custom_call" | custom-call | tf_op jit(solution)/shard_map/pallas_call | solution.py:156
  44.0 1.9 %collective-permute-start.6 = (f32[4,256,128]{2,1,0:T(8,128)}, f32[4,256,128]{2,1,0:T(8,128)S(1)}, u32[]{:S(2)}, u32[]{:S(2)}) collective-permute-start(f32[4,256,128]{2,1,0:T(8,128)} %get-tuple-element.7.rest_0_), channel_id=1, source_target_pairs={{2,0},{4,2},{6,4},{8,6},{10,8},{12,10},{14,12},{16,14},{18,16},{20... | collective-permute-start | bytes 1572872 | tf_op jit(solution)/shard_map/ppermute | solution.py:24
  45.9 3.9 %collective-permute-start.5 = (f32[4,256,128]{2,1,0:T(8,128)}, f32[4,256,128]{2,1,0:T(8,128)S(1)}, u32[]{:S(2)}, u32[]{:S(2)}) collective-permute-start(f32[4,256,128]{2,1,0:T(8,128)} %get-tuple-element.7.rest_0_), channel_id=1, source_target_pairs={{0,2},{2,4},{4,6},{6,8},{8,10},{10,12},{12,14},{14,16},{16,18},{18... | collective-permute-start | bytes 1572872 | tf_op jit(solution)/shard_map/ppermute | solution.py:23
  49.8 0.1 collective-permute-start.3
  49.9 1.6 %collective-permute-done.3.rest_2_ = f32[3,128,128]{2,1,0:T(8,128)S(1)} collective-permute-done((f32[3,128,128]{2,1,0:T(8,128)}, f32[3,128,128]{2,1,0:T(8,128)S(1)}, u32[]{:S(2)}, u32[]{:S(2)}) %collective-permute-start.3) | collective-permute-done | bytes 196640 | tf_op jit(solution)/shard_map/ppermute | solution.py:18
  51.6 0.0 copy-start.6
  51.6 8.8 %collective-permute-done.6.rest_5_ = f32[4,256,128]{2,1,0:T(8,128)S(1)} collective-permute-done((f32[4,256,128]{2,1,0:T(8,128)}, f32[4,256,128]{2,1,0:T(8,128)S(1)}, u32[]{:S(2)}, u32[]{:S(2)}) %collective-permute-start.6) | collective-permute-done | bytes 524320 | tf_op jit(solution)/shard_map/ppermute | solution.py:24
  60.4 6.1 %collective-permute-done.5.rest_4_ = f32[4,256,128]{2,1,0:T(8,128)S(1)} collective-permute-done((f32[4,256,128]{2,1,0:T(8,128)}, f32[4,256,128]{2,1,0:T(8,128)S(1)}, u32[]{:S(2)}, u32[]{:S(2)}) %collective-permute-start.5) | collective-permute-done | bytes 524320 | tf_op jit(solution)/shard_map/ppermute | solution.py:23
  66.6 0.0 collective-permute-done.4.rest_3_
  66.6 0.0 copy-done.6
  66.6 0.0 copy-done.2
  66.6 0.8 %copy-done.3 = f32[4,256,128]{2,1,0:T(8,128)} copy-done((f32[4,256,128]{2,1,0:T(8,128)}, f32[4,256,128]{2,1,0:T(8,128)S(1)}, u32[]{:S(2)}) %copy-start.3) | copy-done | bytes 524312
  67.4 0.3 copy-done.1
  67.6 6.7 %shard_map.40 = f32[2,5,256,128]{3,2,1,0:T(8,128)} custom-call(s32[1]{0:T(128)} %bitcast.side_ref, s32[2,5]{1,0:T(2,128)} %scale_ref.5, s32[2,5]{1,0:T(2,128)} %get-tuple-element.10.keep_ref, f32[4,256,128]{2,1,0:T(8,128)} %get-tuple-element.7.rest_0_, f32[6,256,128]{2,1,0:T(8,128)} %shard_map.39.rest_1_, f32[3,128,128]{2,1,0:T(8,128)} %copy-done.6, ...), custom_call_target="tpu_custom_call" | custom-call | tf_op jit(solution)/shard_map/pallas_call | solution.py:156
  (3 shorter events, 0.0 us)
Async XLA Ops:
  0.0 14.6 %copy-start.7 = (s32[2,2,5]{2,1,0:T(2,128)S(1)}, s32[2,2,5]{2,1,0:T(2,128)}, u32[]{:S(2)}) copy-start(s32[2,2,5]{2,1,0:T(2,128)} %param.5) | copy-start | bytes 244
  0.0 33.0 %collective-permute-start = (f32[2,5,256,128]{3,2,1,0:T(8,128)}, f32[2,5,256,128]{3,2,1,0:T(8,128)S(1)}, u32[]{:S(2)}, u32[]{:S(2)}) collective-permute-start(f32[2,5,256,128]{3,2,1,0:T(8,128)} %rest_0_.3), channel_id=1, source_target_pairs={{0,1},{1,0},{2,3},{3,2},{4,5},{5,4},{6,7},{7,6},{8,9},{9,8},{10,11... | collective-permute-start | bytes 3932168 | tf_op jit(solution)/shard_map/ppermute | solution.py:18
  2.2 22.6 %collective-permute-start.2 = (f32[4,256,128]{2,1,0:T(8,128)}, f32[4,256,128]{2,1,0:T(8,128)S(1)}, u32[]{:S(2)}, u32[]{:S(2)}) collective-permute-start(f32[4,256,128]{2,1,0:T(8,128)} %shard_map.38), channel_id=1, source_target_pairs={{2,0},{4,2},{6,4},{8,6},{10,8},{12,10},{14,12},{16,14},{18,16},{20... | collective-permute-start | bytes 1572872 | tf_op jit(solution)/shard_map/ppermute | solution.py:24
  12.6 20.4 %collective-permute-start.1 = (f32[4,256,128]{2,1,0:T(8,128)}, f32[4,256,128]{2,1,0:T(8,128)S(1)}, u32[]{:S(2)}, u32[]{:S(2)}) collective-permute-start(f32[4,256,128]{2,1,0:T(8,128)} %shard_map.38), channel_id=1, source_target_pairs={{0,2},{2,4},{4,6},{6,8},{8,10},{10,12},{12,14},{14,16},{16,18},{18... | collective-permute-start | bytes 1572872 | tf_op jit(solution)/shard_map/ppermute | solution.py:23
  24.8 8.2 %copy-start.4 = (f32[4,256,128]{2,1,0:T(8,128)}, f32[4,256,128]{2,1,0:T(8,128)S(1)}, u32[]{:S(2)}) copy-start(f32[4,256,128]{2,1,0:T(8,128)S(1)} %collective-permute-done.2.rest_3_) | copy-start | bytes 1572868
  33.0 0.8 %copy-start.5 = (f32[4,256,128]{2,1,0:T(8,128)}, f32[4,256,128]{2,1,0:T(8,128)S(1)}, u32[]{:S(2)}) copy-start(f32[4,256,128]{2,1,0:T(8,128)S(1)} %collective-permute-done.1.rest_2_) | copy-start | bytes 1572868
  33.0 1.2 %copy-start = (f32[2,5,256,128]{3,2,1,0:T(8,128)}, f32[2,5,256,128]{3,2,1,0:T(8,128)S(1)}, u32[]{:S(2)}) copy-start(f32[2,5,256,128]{3,2,1,0:T(8,128)S(1)} %collective-permute-done.rest_1_) | copy-start | bytes 3932164
  39.7 26.9 %collective-permute-start.4 = (f32[6,256,128]{2,1,0:T(8,128)}, f32[6,256,128]{2,1,0:T(8,128)S(1)}, u32[]{:S(2)}, u32[]{:S(2)}) collective-permute-start(f32[6,256,128]{2,1,0:T(8,128)} %shard_map.39.rest_1_), channel_id=1, source_target_pairs={{0,1},{1,0},{2,3},{3,2},{4,5},{5,4},{6,7},{7,6},{8,9},{9,8},{10,11... | collective-permute-start | bytes 2359304 | tf_op jit(solution)/shard_map/ppermute | solution.py:18
  44.0 16.4 %collective-permute-start.6 = (f32[4,256,128]{2,1,0:T(8,128)}, f32[4,256,128]{2,1,0:T(8,128)S(1)}, u32[]{:S(2)}, u32[]{:S(2)}) collective-permute-start(f32[4,256,128]{2,1,0:T(8,128)} %get-tuple-element.7.rest_0_), channel_id=1, source_target_pairs={{2,0},{4,2},{6,4},{8,6},{10,8},{12,10},{14,12},{16,14},{18,16},{20... | collective-permute-start | bytes 1572872 | tf_op jit(solution)/shard_map/ppermute | solution.py:24
  45.9 20.7 %collective-permute-start.5 = (f32[4,256,128]{2,1,0:T(8,128)}, f32[4,256,128]{2,1,0:T(8,128)S(1)}, u32[]{:S(2)}, u32[]{:S(2)}) collective-permute-start(f32[4,256,128]{2,1,0:T(8,128)} %get-tuple-element.7.rest_0_), channel_id=1, source_target_pairs={{0,2},{2,4},{4,6},{6,8},{8,10},{10,12},{12,14},{14,16},{16,18},{18... | collective-permute-start | bytes 1572872 | tf_op jit(solution)/shard_map/ppermute | solution.py:23
  49.8 1.7 %collective-permute-start.3 = (f32[3,128,128]{2,1,0:T(8,128)}, f32[3,128,128]{2,1,0:T(8,128)S(1)}, u32[]{:S(2)}, u32[]{:S(2)}) collective-permute-start(f32[3,128,128]{2,1,0:T(8,128)} %get-tuple-element.8), channel_id=1, source_target_pairs={{0,1},{1,0},{2,3},{3,2},{4,5},{5,4},{6,7},{7,6},{8,9},{9,8},{10,11... | collective-permute-start | bytes 589832 | tf_op jit(solution)/shard_map/ppermute | solution.py:18
  51.6 15.0 %copy-start.6 = (f32[3,128,128]{2,1,0:T(8,128)}, f32[3,128,128]{2,1,0:T(8,128)S(1)}, u32[]{:S(2)}) copy-start(f32[3,128,128]{2,1,0:T(8,128)S(1)} %collective-permute-done.3.rest_2_) | copy-start | bytes 589828
  60.4 6.2 %copy-start.2 = (f32[4,256,128]{2,1,0:T(8,128)}, f32[4,256,128]{2,1,0:T(8,128)S(1)}, u32[]{:S(2)}) copy-start(f32[4,256,128]{2,1,0:T(8,128)S(1)} %collective-permute-done.6.rest_5_) | copy-start | bytes 1572868
  66.6 0.8 %copy-start.3 = (f32[4,256,128]{2,1,0:T(8,128)}, f32[4,256,128]{2,1,0:T(8,128)S(1)}, u32[]{:S(2)}) copy-start(f32[4,256,128]{2,1,0:T(8,128)S(1)} %collective-permute-done.5.rest_4_) | copy-start | bytes 1572868
  66.6 1.1 %copy-start.1 = (f32[6,256,128]{2,1,0:T(8,128)}, f32[6,256,128]{2,1,0:T(8,128)S(1)}, u32[]{:S(2)}) copy-start(f32[6,256,128]{2,1,0:T(8,128)S(1)} %collective-permute-done.4.rest_3_) | copy-start | bytes 2359300

commit v8 on v7

--- a/solution.py
+++ b/solution.py
@@ -28,6 +28,13 @@
 def split(x):
     high = x.astype(jnp.bfloat16)
     return high, (x - high.astype(jnp.float32)).astype(jnp.bfloat16)
+
+
+def dot3(a_high, a_low, b, dims):
+    b_high, b_low = split(b)
+    def one(x, y):
+        return lax.dot_general(x, y, dims, preferred_element_type=jnp.float32)
+    return one(a_low, b_high) + one(a_high, b_low) + one(a_high, b_high)
 
 
 class Tiles:
@@ -74,7 +81,7 @@
     mine = Tiles(rest[:parts], scale_ref if scaled else None)
     other_refs = rest[parts : 2 * parts]
     rest = rest[2 * parts :]
-    if halo:
+    if halo is True:
         left_ref, right_ref = rest[:2]
         rest = rest[2:]
     if quarters:
@@ -102,7 +109,7 @@
             for place, (index, slot) in enumerate(by_row[row]):
                 col = row + slot - 2
                 where = (row, slice(offset * tile, (offset + 1) * tile), slice(place * half, (place + 1) * half))
-                if abs(k - col) > 2:
+                if abs(k - col) > 2 or (halo == "skip" and k not in (0, 1) and col not in (0, 1)):
                     rh_ref[where] = jnp.zeros((tile, half), jnp.bfloat16)
                     rl_ref[where] = jnp.zeros((tile, half), jnp.bfloat16)
                     continue
@@ -122,12 +129,14 @@
     for row in range(2):
         def one(x, y):
             return lax.dot_general(x, y, CONTRACT, preferred_element_type=jnp.float32)
-
         a_high = lh_ref[row]
         b_high = rh_ref[row]
         acc = one(ll_ref[row], b_high) + one(a_high, rl_ref[row]) + one(a_high, b_high)
         for place, (index, slot) in enumerate(by_row[row]):
             value = acc[:, place * half : (place + 1) * half]
+            if halo == "skip":
+                out_ref[row, slot] = value
+                continue
             if odd:
                 value = 2.0 * mine(row, slot) - value
             value = value * keep_ref[row, slot].astype(jnp.float32)
@@ -143,7 +152,7 @@
 def band_call(tiles, odd, side, scale, keep, mine, other, halo=None, scaled=False, quarters=False):
     smem = pl.BlockSpec(memory_space=pltpu.SMEM)
     vmem = pl.BlockSpec(memory_space=pltpu.VMEM)
-    args = [side, scale, keep] + list(mine) + list(other) + ([] if halo is None else list(halo))
+    args = [side, scale, keep] + list(mine) + list(other) + (list(halo) if isinstance(halo, tuple) else [])
     half = mine[0].shape[-1]
     tile = (mine[0].shape[-2], half)
     shape = (2, 5) + tile if len(tiles) == len(ALL) else (len(tiles),) + tile
@@ -154,12 +163,49 @@
     if quarters:
         out_shape = (out_shape, jax.ShapeDtypeStruct((len(QUARTERS), half, half), jnp.float32))
     return pl.pallas_call(
-        functools.partial(band_kernel, tiles, odd, len(mine), scaled, halo is not None, quarters),
+        functools.partial(band_kernel, tiles, odd, len(mine), scaled, halo if halo == "skip" else halo is not None, quarters),
         out_shape=out_shape,
         in_specs=[smem, smem, smem] + [vmem] * (len(args) - 3),
         out_specs=(vmem, vmem) if quarters else vmem,
         scratch_shapes=[pltpu.VMEM(lefts, jnp.bfloat16)] * 2 + [pltpu.VMEM(rights, jnp.bfloat16)] * 2,
     )(*args)
+
+
+def finish_kernel(side_ref, keep_ref, partial_ref, diag_ref, off_ref, off_other_ref, left_ref, right_ref, out_ref):
+    half = out_ref.shape[3]
+    side = side_ref[0]
+    own = pl.ds(pl.multiple_of(side * half, half), half)
+    far = pl.ds(pl.multiple_of((1 - side) * half, half), half)
+    for row in range(2):
+        for slot in range(5):
+            col = row + slot - 2
+            value = partial_ref[row, slot]
+            if (row, slot) in DIAG:
+                mine = diag_ref[DIAG.index((row, slot))]
+            else:
+                mine = off_ref[OFF.index((row, slot))]
+                for k in range(max(row, col) - 2, min(row, col) + 3):
+                    if k in (0, 1):
+                        continue
+                    index = OFF.index((row, k - row + 2))
+                    full = jnp.concatenate([off_ref[index], off_other_ref[index]], axis=1)
+                    high, low = split(full)
+                    src = left_ref if k < 0 else right_ref
+                    b = 2 * (k + 2) + (col + 2) if k < 0 else 2 * (k - 2) + (col - 2)
+                    right = jnp.concatenate([src[b, own, :], src[b, far, :]], axis=0)
+                    value = value + dot3(high, low, right, CONTRACT)
+            out_ref[row, slot] = (2.0 * mine - value) * keep_ref[row, slot].astype(jnp.float32)
+
+
+def finish(side, keep, partial, diag, off, off_other, halo):
+    smem = pl.BlockSpec(memory_space=pltpu.SMEM)
+    vmem = pl.BlockSpec(memory_space=pltpu.VMEM)
+    return pl.pallas_call(
+        finish_kernel,
+        out_shape=jax.ShapeDtypeStruct(partial.shape, jnp.float32),
+        in_specs=[smem, smem] + [vmem] * 6,
+        out_specs=vmem,
+    )(side, keep, partial, diag, off, off_other, halo[0], halo[1])
 
 
 def block_kernel(pattern_ref, density_ref, out_ref):
@@ -185,7 +231,8 @@
     quarter_other = swap_help(quarter)
     off = band_call(OFF, False, side, pattern, truncation[0], [density], [other], halo, scaled=True)
     off_other = swap_help(off)
-    return band_call(ALL, True, side, pattern, truncation[1], [diag, off], [quarter_other, off_other], next_halo)
+    partial = band_call(ALL, True, side, pattern, truncation[1], [diag, off], [quarter_other, off_other], "skip")
+    return finish(side, truncation[1], partial, diag, off, off_other, next_halo)
 
 
 def solution(mesh):

time: 74.6 us -> 72.2 us (0.968)
  waiting for transfers between devices: 34.5 us -> 27 us
  Pallas kernels: 18.6 us -> 22.9 us
    ppermute x2, waiting for transfers between devices: 18.4 us -> 11 us  [send_block(): lax.ppermute(block, 'rows', [(i + 1, i) for i in range(count - 1)])]
    pallas_call x0 -> x1, Pallas kernels: none -> 4.51 us  [finish(): pl.pallas_call(finish_kernel, out_shape=jax.ShapeDtypeStruct(partial.shap...]
  transfers between devices with their start and end apart: 7 -> 7, of which waited for: 5 -> 5; matrix products, arithmetic and copies ran while one was open for 1% -> 1% of each run, Pallas kernels for 9% -> 18%
where the time goes in v8:
time: 72.2 us; the launch traced here: 71.9 us
  waiting for transfers between devices  27 us (37%)
  Pallas kernels  22.9 us (32%)
  starting transfers between devices  18.3 us (25%)
  local copies, waits for them, and re-layouts  3.58 us (5%)
    pallas_call x3, Pallas kernels, band_call(): pl.pallas_call(functools.partial(band_kernel, tiles, odd, len(mine), scal...  16.2 us
    ppermute x2, waiting for transfers between devices, send_block(): lax.ppermute(block, 'rows', [(i, i + 1) for i in range(count - 1)])  14.4 us
    ppermute x2, starting transfers between devices, send_block(): lax.ppermute(block, 'rows', [(i + 1, i) for i in range(count - 1)])  12.4 us
    ppermute x2, waiting for transfers between devices, send_block(): lax.ppermute(block, 'rows', [(i + 1, i) for i in range(count - 1)])  11 us
    ppermute x2, starting transfers between devices, send_block(): lax.ppermute(block, 'rows', [(i, i + 1) for i in range(count - 1)])  5.84 us
    pallas_call x1, Pallas kernels, finish(): pl.pallas_call(finish_kernel, out_shape=jax.ShapeDtypeStruct(partial.shap...  4.51 us
    unnamed x16, local copies, waits for them, and re-layouts  2.99 us
    pallas_call x1, Pallas kernels, first_block(): pl.pallas_call(block_kernel, out_shape=jax.ShapeDtypeStruct((len(DIAG),)...  2.17 us
  transfers between devices with their start and end apart: 7, of which 5 were waited for; matrix products, arithmetic and copies ran while one was open for 1% of the time, Pallas kernels for 18%

profile of v8, /device:TPU:6, one launch (start us, length us, event | category | flops | bytes accessed | tf_op | source)
XLA Modules:
  0.0 71.9 jit_solution(692649552418702367)
XLA Ops:
  0.0 0.0 copy-start.7
  0.0 0.0 collective-permute-start
  0.0 2.2 %shard_map.38 = f32[4,256,128]{2,1,0:T(8,128)} custom-call(s32[2,5]{1,0:T(2,128)} %scale_ref.5, f32[2,5,256,128]{3,2,1,0:T(8,128)} %rest_0_.3), custom_call_target="tpu_custom_call" | custom-call | tf_op jit(solution)/shard_map/pallas_call | solution.py:217
  2.2 10.5 %collective-permute-start.2 = (f32[4,256,128]{2,1,0:T(8,128)}, f32[4,256,128]{2,1,0:T(8,128)S(1)}, u32[]{:S(2)}, u32[]{:S(2)}) collective-permute-start(f32[4,256,128]{2,1,0:T(8,128)} %shard_map.38), channel_id=1, source_target_pairs={{2,0},{4,2},{6,4},{8,6},{10,8},{12,10},{14,12},{16,14},{18,16},{20... | collective-permute-start | bytes 1572872 | tf_op jit(solution)/shard_map/ppermute | solution.py:24
  12.6 1.9 %collective-permute-start.1 = (f32[4,256,128]{2,1,0:T(8,128)}, f32[4,256,128]{2,1,0:T(8,128)S(1)}, u32[]{:S(2)}, u32[]{:S(2)}) collective-permute-start(f32[4,256,128]{2,1,0:T(8,128)} %shard_map.38), channel_id=1, source_target_pairs={{0,2},{2,4},{4,6},{6,8},{8,10},{10,12},{12,14},{14,16},{16,18},{18... | collective-permute-start | bytes 1572872 | tf_op jit(solution)/shard_map/ppermute | solution.py:23
  14.6 0.0 copy-done.7
  14.6 0.6 slice_bitcast_fusion
  15.2 9.6 %collective-permute-done.2.rest_3_ = f32[4,256,128]{2,1,0:T(8,128)S(1)} collective-permute-done((f32[4,256,128]{2,1,0:T(8,128)}, f32[4,256,128]{2,1,0:T(8,128)S(1)}, u32[]{:S(2)}, u32[]{:S(2)}) %collective-permute-start.2) | collective-permute-done | bytes 524320 | tf_op jit(solution)/shard_map/ppermute | solution.py:24
  24.8 0.0 copy-start.4
  24.8 8.2 %collective-permute-done.1.rest_2_ = f32[4,256,128]{2,1,0:T(8,128)S(1)} collective-permute-done((f32[4,256,128]{2,1,0:T(8,128)}, f32[4,256,128]{2,1,0:T(8,128)S(1)}, u32[]{:S(2)}, u32[]{:S(2)}) %collective-permute-start.1) | collective-permute-done | bytes 524320 | tf_op jit(solution)/shard_map/ppermute | solution.py:23
  33.0 0.0 copy-start.5
  33.0 0.0 collective-permute-done.rest_1_
  33.0 0.0 copy-start
  33.0 0.0 copy-done.4
  33.0 0.8 %copy-done.5 = f32[4,256,128]{2,1,0:T(8,128)} copy-done((f32[4,256,128]{2,1,0:T(8,128)}, f32[4,256,128]{2,1,0:T(8,128)S(1)}, u32[]{:S(2)}) %copy-start.5) | copy-done | bytes 524312
  33.8 0.4 copy-done
  34.2 5.4 %shard_map.39.rest_1_.off_ref = f32[6,256,128]{2,1,0:T(8,128)} custom-call(s32[1]{0:T(128)} %bitcast.side_ref, s32[2,5]{1,0:T(2,128)} %scale_ref.5, s32[2,5]{1,0:T(2,128)} %get-tuple-element.9.keep_ref, f32[2,5,256,128]{3,2,1,0:T(8,128)} %rest_0_.3, f32[2,5,256,128]{3,2,1,0:T(8,128)} %copy-done, f32[4,256,128]{2,1,0:T(8,128)} %copy-done.5, ...), custom_call_target="tpu_custom_call" | custom-call | tf_op jit(solution)/shard_map/pallas_call | solution.py:165
  39.7 0.0 collective-permute-start.4
  39.7 4.3 %shard_map.37 = (f32[4,256,128]{2,1,0:T(8,128)}, f32[3,128,128]{2,1,0:T(8,128)}) custom-call(s32[1]{0:T(128)} %bitcast.side_ref, s32[2,5]{1,0:T(2,128)} %scale_ref.5, s32[2,5]{1,0:T(2,128)} %get-tuple-element.9.keep_ref, f32[2,5,256,128]{3,2,1,0:T(8,128)} %rest_0_.3, f32[2,5,256,128]{3,2,1,0:T(8,128)} %copy-done), custom_call_target="tpu_custom_call" | custom-call | tf_op jit(solution)/shard_map/pallas_call | solution.py:165
  44.0 1.9 %collective-permute-start.6 = (f32[4,256,128]{2,1,0:T(8,128)}, f32[4,256,128]{2,1,0:T(8,128)S(1)}, u32[]{:S(2)}, u32[]{:S(2)}) collective-permute-start(f32[4,256,128]{2,1,0:T(8,128)} %get-tuple-element.7.rest_0_.diag_ref), channel_id=1, source_target_pairs={{2,0},{4,2},{6,4},{8,6},{10,8},{12,10},{14,12},{16,14},{18,16},{20... | collective-permute-start | bytes 1572872 | tf_op jit(solution)/shard_map/ppermute | solution.py:24
  45.9 3.9 %collective-permute-start.5 = (f32[4,256,128]{2,1,0:T(8,128)}, f32[4,256,128]{2,1,0:T(8,128)S(1)}, u32[]{:S(2)}, u32[]{:S(2)}) collective-permute-start(f32[4,256,128]{2,1,0:T(8,128)} %get-tuple-element.7.rest_0_.diag_ref), channel_id=1, source_target_pairs={{0,2},{2,4},{4,6},{6,8},{8,10},{10,12},{12,14},{14,16},{16,18},{18... | collective-permute-start | bytes 1572872 | tf_op jit(solution)/shard_map/ppermute | solution.py:23
  49.8 0.1 collective-permute-start.3
  49.9 1.6 %collective-permute-done.3.rest_2_ = f32[3,128,128]{2,1,0:T(8,128)S(1)} collective-permute-done((f32[3,128,128]{2,1,0:T(8,128)}, f32[3,128,128]{2,1,0:T(8,128)S(1)}, u32[]{:S(2)}, u32[]{:S(2)}) %collective-permute-start.3) | collective-permute-done | bytes 196640 | tf_op jit(solution)/shard_map/ppermute | solution.py:18
  51.6 0.0 collective-permute-done.4.rest_3_.off_other_ref
  51.6 0.7 copy-done.6
  52.2 0.3 copy-done.1
  52.5 6.5 %shard_map.40.partial_ref = f32[2,5,256,128]{3,2,1,0:T(8,128)} custom-call(s32[1]{0:T(128)} %bitcast.side_ref, s32[2,5]{1,0:T(2,128)} %scale_ref.5, s32[2,5]{1,0:T(2,128)} %get-tuple-element.10.keep_ref, f32[4,256,128]{2,1,0:T(8,128)} %get-tuple-element.7.rest_0_.diag_ref, f32[6,256,128]{2,1,0:T(8,128)} %shard_map.39.rest_1_.off_ref, ...), custom_call_target="tpu_custom_call" | custom-call | tf_op jit(solution)/shard_map/pallas_call | solution.py:165
  59.0 1.4 %collective-permute-done.6.right_ref = f32[4,256,128]{2,1,0:T(8,128)S(1)} collective-permute-done((f32[4,256,128]{2,1,0:T(8,128)}, f32[4,256,128]{2,1,0:T(8,128)S(1)}, u32[]{:S(2)}, u32[]{:S(2)}) %collective-permute-start.6) | collective-permute-done | bytes 524320 | tf_op jit(solution)/shard_map/ppermute | solution.py:24
  60.4 6.1 %collective-permute-done.5.left_ref = f32[4,256,128]{2,1,0:T(8,128)S(1)} collective-permute-done((f32[4,256,128]{2,1,0:T(8,128)}, f32[4,256,128]{2,1,0:T(8,128)S(1)}, u32[]{:S(2)}, u32[]{:S(2)}) %collective-permute-start.5) | collective-permute-done | bytes 524320 | tf_op jit(solution)/shard_map/ppermute | solution.py:23
  66.6 0.0 copy-done.2
  66.6 0.8 %copy-done.3 = f32[4,256,128]{2,1,0:T(8,128)} copy-done((f32[4,256,128]{2,1,0:T(8,128)}, f32[4,256,128]{2,1,0:T(8,128)S(1)}, u32[]{:S(2)}) %copy-start.3) | copy-done | bytes 524312
  67.4 4.5 %shard_map.41 = f32[2,5,256,128]{3,2,1,0:T(8,128)} custom-call(s32[1]{0:T(128)} %bitcast.side_ref, s32[2,5]{1,0:T(2,128)} %get-tuple-element.10.keep_ref, f32[2,5,256,128]{3,2,1,0:T(8,128)} %shard_map.40.partial_ref, f32[4,256,128]{2,1,0:T(8,128)} %get-tuple-element.7.rest_0_.diag_ref, f32[6,256,128]{2,1,0:T(8,128)} %shard_map.39.rest_1_.off_ref, ...), custom_call_target="tpu_custom_call" | custom-call | tf_op jit(solution)/shard_map/pallas_call | solution.py:203
  (4 shorter events, 0.0 us)
Async XLA Ops:
  0.0 14.6 %copy-start.7 = (s32[2,2,5]{2,1,0:T(2,128)S(1)}, s32[2,2,5]{2,1,0:T(2,128)}, u32[]{:S(2)}) copy-start(s32[2,2,5]{2,1,0:T(2,128)} %param.5) | copy-start | bytes 244
  0.0 33.0 %collective-permute-start = (f32[2,5,256,128]{3,2,1,0:T(8,128)}, f32[2,5,256,128]{3,2,1,0:T(8,128)S(1)}, u32[]{:S(2)}, u32[]{:S(2)}) collective-permute-start(f32[2,5,256,128]{3,2,1,0:T(8,128)} %rest_0_.3), channel_id=1, source_target_pairs={{0,1},{1,0},{2,3},{3,2},{4,5},{5,4},{6,7},{7,6},{8,9},{9,8},{10,11... | collective-permute-start | bytes 3932168 | tf_op jit(solution)/shard_map/ppermute | solution.py:18
  2.2 22.6 %collective-permute-start.2 = (f32[4,256,128]{2,1,0:T(8,128)}, f32[4,256,128]{2,1,0:T(8,128)S(1)}, u32[]{:S(2)}, u32[]{:S(2)}) collective-permute-start(f32[4,256,128]{2,1,0:T(8,128)} %shard_map.38), channel_id=1, source_target_pairs={{2,0},{4,2},{6,4},{8,6},{10,8},{12,10},{14,12},{16,14},{18,16},{20... | collective-permute-start | bytes 1572872 | tf_op jit(solution)/shard_map/ppermute | solution.py:24
  12.6 20.4 %collective-permute-start.1 = (f32[4,256,128]{2,1,0:T(8,128)}, f32[4,256,128]{2,1,0:T(8,128)S(1)}, u32[]{:S(2)}, u32[]{:S(2)}) collective-permute-start(f32[4,256,128]{2,1,0:T(8,128)} %shard_map.38), channel_id=1, source_target_pairs={{0,2},{2,4},{4,6},{6,8},{8,10},{10,12},{12,14},{14,16},{16,18},{18... | collective-permute-start | bytes 1572872 | tf_op jit(solution)/shard_map/ppermute | solution.py:23
  24.8 8.2 %copy-start.4 = (f32[4,256,128]{2,1,0:T(8,128)}, f32[4,256,128]{2,1,0:T(8,128)S(1)}, u32[]{:S(2)}) copy-start(f32[4,256,128]{2,1,0:T(8,128)S(1)} %collective-permute-done.2.rest_3_) | copy-start | bytes 1572868
  33.0 0.8 %copy-start.5 = (f32[4,256,128]{2,1,0:T(8,128)}, f32[4,256,128]{2,1,0:T(8,128)S(1)}, u32[]{:S(2)}) copy-start(f32[4,256,128]{2,1,0:T(8,128)S(1)} %collective-permute-done.1.rest_2_) | copy-start | bytes 1572868
  33.0 1.2 %copy-start = (f32[2,5,256,128]{3,2,1,0:T(8,128)}, f32[2,5,256,128]{3,2,1,0:T(8,128)S(1)}, u32[]{:S(2)}) copy-start(f32[2,5,256,128]{3,2,1,0:T(8,128)S(1)} %collective-permute-done.rest_1_) | copy-start | bytes 3932164
  39.7 11.9 %collective-permute-start.4 = (f32[6,256,128]{2,1,0:T(8,128)}, f32[6,256,128]{2,1,0:T(8,128)S(1)}, u32[]{:S(2)}, u32[]{:S(2)}) collective-permute-start(f32[6,256,128]{2,1,0:T(8,128)} %shard_map.39.rest_1_.off_ref), channel_id=1, source_target_pairs={{0,1},{1,0},{2,3},{3,2},{4,5},{5,4},{6,7},{7,6},{8,9},{9,8},{10,11... | collective-permute-start | bytes 2359304 | tf_op jit(solution)/shard_map/ppermute | solution.py:18
  44.0 16.4 %collective-permute-start.6 = (f32[4,256,128]{2,1,0:T(8,128)}, f32[4,256,128]{2,1,0:T(8,128)S(1)}, u32[]{:S(2)}, u32[]{:S(2)}) collective-permute-start(f32[4,256,128]{2,1,0:T(8,128)} %get-tuple-element.7.rest_0_.diag_ref), channel_id=1, source_target_pairs={{2,0},{4,2},{6,4},{8,6},{10,8},{12,10},{14,12},{16,14},{18,16},{20... | collective-permute-start | bytes 1572872 | tf_op jit(solution)/shard_map/ppermute | solution.py:24
  45.9 20.7 %collective-permute-start.5 = (f32[4,256,128]{2,1,0:T(8,128)}, f32[4,256,128]{2,1,0:T(8,128)S(1)}, u32[]{:S(2)}, u32[]{:S(2)}) collective-permute-start(f32[4,256,128]{2,1,0:T(8,128)} %get-tuple-element.7.rest_0_.diag_ref), channel_id=1, source_target_pairs={{0,2},{2,4},{4,6},{6,8},{8,10},{10,12},{12,14},{14,16},{16,18},{18... | collective-permute-start | bytes 1572872 | tf_op jit(solution)/shard_map/ppermute | solution.py:23
  49.8 1.7 %collective-permute-start.3 = (f32[3,128,128]{2,1,0:T(8,128)}, f32[3,128,128]{2,1,0:T(8,128)S(1)}, u32[]{:S(2)}, u32[]{:S(2)}) collective-permute-start(f32[3,128,128]{2,1,0:T(8,128)} %get-tuple-element.8), channel_id=1, source_target_pairs={{0,1},{1,0},{2,3},{3,2},{4,5},{5,4},{6,7},{7,6},{8,9},{9,8},{10,11... | collective-permute-start | bytes 589832 | tf_op jit(solution)/shard_map/ppermute | solution.py:18
  51.6 0.7 copy-start.6
  51.6 1.0 %copy-start.1 = (f32[6,256,128]{2,1,0:T(8,128)}, f32[6,256,128]{2,1,0:T(8,128)S(1)}, u32[]{:S(2)}) copy-start(f32[6,256,128]{2,1,0:T(8,128)S(1)} %collective-permute-done.4.rest_3_.off_other_ref) | copy-start | bytes 2359300
  60.4 6.1 %copy-start.2 = (f32[4,256,128]{2,1,0:T(8,128)}, f32[4,256,128]{2,1,0:T(8,128)S(1)}, u32[]{:S(2)}) copy-start(f32[4,256,128]{2,1,0:T(8,128)S(1)} %collective-permute-done.6.right_ref) | copy-start | bytes 1572868
  66.6 0.8 %copy-start.3 = (f32[4,256,128]{2,1,0:T(8,128)}, f32[4,256,128]{2,1,0:T(8,128)S(1)}, u32[]{:S(2)}) copy-start(f32[4,256,128]{2,1,0:T(8,128)S(1)} %collective-permute-done.5.left_ref) | copy-start | bytes 1572868

commit v9 on v7

--- a/solution.py
+++ b/solution.py
@@ -70,13 +70,17 @@
         )
 
 
-def band_kernel(tiles, odd, parts, scaled, halo, quarters, side_ref, scale_ref, keep_ref, *rest):
+def band_kernel(tiles, odd, parts, scaled, mode, quarters, side_ref, scale_ref, keep_ref, *rest):
     mine = Tiles(rest[:parts], scale_ref if scaled else None)
-    other_refs = rest[parts : 2 * parts]
-    rest = rest[2 * parts :]
-    if halo:
+    rest = rest[parts:]
+    other_refs = rest[: len(rest) - 5 - (3 if mode == "halo" else (2 if mode == "plain" else 0)) - (1 if quarters else 0)]
+    rest = rest[len(other_refs) :]
+    if mode in ("plain", "halo"):
         left_ref, right_ref = rest[:2]
         rest = rest[2:]
+    if mode == "halo":
+        partial_ref = rest[0]
+        rest = rest[1:]
     if quarters:
         out_ref, quarter_ref, lh_ref, ll_ref, rh_ref, rl_ref = rest
     else:
@@ -87,21 +91,28 @@
     own = pl.ds(pl.multiple_of(side * half, half), half)
     far = pl.ds(pl.multiple_of((1 - side) * half, half), half)
     if other_refs[0].shape[-2] == half:
-        other = Rebuilt(other_refs[0], other_refs[1], mine, side, own, far)
+        other = Rebuilt(other_refs[0], other_refs[1] if len(other_refs) > 1 else None, mine, side, own, far)
     else:
         other = Tiles(other_refs, scale_ref if scaled else None)
     by_row = [[(index, slot) for index, (row, slot) in enumerate(tiles) if row == r] for r in range(2)]
 
+    def wanted(k):
+        if mode == "own":
+            return k in (0, 1)
+        if mode == "halo":
+            return k not in (0, 1)
+        return True
+
     for row in range(2):
-        for slot in range(5):
-            high, low = split(jnp.concatenate([mine(row, slot), other(row, slot)], axis=1))
-            lh_ref[row, :, slot * tile : (slot + 1) * tile] = high
-            ll_ref[row, :, slot * tile : (slot + 1) * tile] = low
-        for offset in range(5):
+        offsets = [o for o in range(5) if wanted(row + o - 2)]
+        for place_k, offset in enumerate(offsets):
+            high, low = split(jnp.concatenate([mine(row, offset), other(row, offset)], axis=1))
+            lh_ref[row, :, place_k * tile : (place_k + 1) * tile] = high
+            ll_ref[row, :, place_k * tile : (place_k + 1) * tile] = low
             k = row + offset - 2
             for place, (index, slot) in enumerate(by_row[row]):
                 col = row + slot - 2
-                where = (row, slice(offset * tile, (offset + 1) * tile), slice(place * half, (place + 1) * half))
+                where = (row, slice(place_k * tile, (place_k + 1) * tile), slice(place * half, (place + 1) * half))
                 if abs(k - col) > 2:
                     rh_ref[where] = jnp.zeros((tile, half), jnp.bfloat16)
                     rl_ref[where] = jnp.zeros((tile, half), jnp.bfloat16)
@@ -128,6 +139,11 @@
         acc = one(ll_ref[row], b_high) + one(a_high, rl_ref[row]) + one(a_high, b_high)
         for place, (index, slot) in enumerate(by_row[row]):
             value = acc[:, place * half : (place + 1) * half]
+            if mode == "own":
+                out_ref[row, slot] = value
+                continue
+            if mode == "halo":
+                value = value + partial_ref[row, slot]
             if odd:
                 value = 2.0 * mine(row, slot) - value
             value = value * keep_ref[row, slot].astype(jnp.float32)
@@ -140,21 +156,28 @@
             quarter_ref[index] = out_ref[tiles.index(key), own, :]
 
 
-def band_call(tiles, odd, side, scale, keep, mine, other, halo=None, scaled=False, quarters=False):
+def band_call(tiles, odd, side, scale, keep, mine, other, halo=None, scaled=False, quarters=False, mode=None, partial=None):
     smem = pl.BlockSpec(memory_space=pltpu.SMEM)
     vmem = pl.BlockSpec(memory_space=pltpu.VMEM)
-    args = [side, scale, keep] + list(mine) + list(other) + ([] if halo is None else list(halo))
+    if mode is None:
+        mode = "plain" if halo is not None else "none"
+    args = [side, scale, keep] + list(mine) + list(other)
+    if halo is not None:
+        args += list(halo)
+    if partial is not None:
+        args.append(partial)
     half = mine[0].shape[-1]
     tile = (mine[0].shape[-2], half)
     shape = (2, 5) + tile if len(tiles) == len(ALL) else (len(tiles),) + tile
     width = len(tiles) // 2
-    lefts = (2, tile[0], 5 * 2 * half)
-    rights = (2, 5 * tile[0], width * half)
+    count = {"own": 2, "halo": 3}.get(mode, 5)
+    lefts = (2, tile[0], count * 2 * half)
+    rights = (2, count * tile[0], width * half)
     out_shape = jax.ShapeDtypeStruct(shape, jnp.float32)
     if quarters:
         out_shape = (out_shape, jax.ShapeDtypeStruct((len(QUARTERS), half, half), jnp.float32))
     return pl.pallas_call(
-        functools.partial(band_kernel, tiles, odd, len(mine), scaled, halo is not None, quarters),
+        functools.partial(band_kernel, tiles, odd, len(mine), scaled, mode, quarters),
         out_shape=out_shape,
         in_specs=[smem, smem, smem] + [vmem] * (len(args) - 3),
         out_specs=(vmem, vmem) if quarters else vmem,
@@ -185,7 +208,10 @@
     quarter_other = swap_help(quarter)
     off = band_call(OFF, False, side, pattern, truncation[0], [density], [other], halo, scaled=True)
     off_other = swap_help(off)
-    return band_call(ALL, True, side, pattern, truncation[1], [diag, off], [quarter_other, off_other], next_halo)
+    partial = band_call(ALL, True, side, pattern, truncation[1], [diag, off], [quarter_other], mode="own")
+    return band_call(
+        ALL, True, side, pattern, truncation[1], [diag, off], [quarter_other, off_other], next_halo, mode="halo", partial=partial
+    )
 
 
 def solution(mesh):

time: 74.6 us -> 74.3 us (level)
  waiting for transfers between devices: 34.5 us -> 29.8 us
  Pallas kernels: 18.6 us -> 21.6 us
  local copies, waits for them, and re-layouts: 2.89 us -> 4.21 us
    ppermute x2, waiting for transfers between devices: 18.4 us -> 13.8 us  [send_block(): lax.ppermute(block, 'rows', [(i + 1, i) for i in range(count - 1)])]
    pallas_call x3 -> x4, Pallas kernels: 16.4 us -> 19.5 us  [band_call(): pl.pallas_call(functools.partial(band_kernel, tiles, odd, len(mine), scal...]
    unnamed x16, local copies, waits for them, and re-layouts: 2.3 us -> 3.61 us
  transfers between devices with their start and end apart: 7 -> 7, of which waited for: 5 -> 5; matrix products, arithmetic and copies ran while one was open for 1% -> 1% of each run, Pallas kernels for 9% -> 14%
where the time goes in v9:
time: 74.3 us; the launch traced here: 74 us
  waiting for transfers between devices  29.8 us (40%)
  Pallas kernels  21.6 us (29%)
  starting transfers between devices  18.3 us (25%)
  local copies, waits for them, and re-layouts  4.21 us (6%)
    pallas_call x4, Pallas kernels, band_call(): pl.pallas_call(functools.partial(band_kernel, tiles, odd, len(mine), scal...  19.5 us
    ppermute x2, waiting for transfers between devices, send_block(): lax.ppermute(block, 'rows', [(i, i + 1) for i in range(count - 1)])  14.4 us
    ppermute x2, waiting for transfers between devices, send_block(): lax.ppermute(block, 'rows', [(i + 1, i) for i in range(count - 1)])  13.8 us
    ppermute x2, starting transfers between devices, send_block(): lax.ppermute(block, 'rows', [(i + 1, i) for i in range(count - 1)])  12.4 us
    ppermute x2, starting transfers between devices, send_block(): lax.ppermute(block, 'rows', [(i, i + 1) for i in range(count - 1)])  5.84 us
    unnamed x16, local copies, waits for them, and re-layouts  3.61 us
    pallas_call x1, Pallas kernels, first_block(): pl.pallas_call(block_kernel, out_shape=jax.ShapeDtypeStruct((len(DIAG),)...  2.17 us
    ppermute x3, waiting for transfers between devices, swap_help(): return lax.ppermute(value, 'help', [(0, 1), (1, 0)])  1.64 us
  transfers between devices with their start and end apart: 7, of which 5 were waited for; matrix products, arithmetic and copies ran while one was open for 1% of the time, Pallas kernels for 14%

profile of v9, /device:TPU:6, one launch (start us, length us, event | category | flops | bytes accessed | tf_op | source)
XLA Modules:
  0.0 74.0 jit_solution(6695818481095923501)
XLA Ops:
  0.0 0.0 copy-start.7
  0.0 0.0 collective-permute-start
  0.0 2.2 %shard_map.38 = f32[4,256,128]{2,1,0:T(8,128)} custom-call(s32[2,5]{1,0:T(2,128)} %scale_ref.7, f32[2,5,256,128]{3,2,1,0:T(8,128)} %rest_0_.3), custom_call_target="tpu_custom_call" | custom-call | tf_op jit(solution)/shard_map/pallas_call | solution.py:194
  2.2 10.5 %collective-permute-start.2 = (f32[4,256,128]{2,1,0:T(8,128)}, f32[4,256,128]{2,1,0:T(8,128)S(1)}, u32[]{:S(2)}, u32[]{:S(2)}) collective-permute-start(f32[4,256,128]{2,1,0:T(8,128)} %shard_map.38), channel_id=1, source_target_pairs={{2,0},{4,2},{6,4},{8,6},{10,8},{12,10},{14,12},{16,14},{18,16},{20... | collective-permute-start | bytes 1572872 | tf_op jit(solution)/shard_map/ppermute | solution.py:24
  12.6 1.9 %collective-permute-start.1 = (f32[4,256,128]{2,1,0:T(8,128)}, f32[4,256,128]{2,1,0:T(8,128)S(1)}, u32[]{:S(2)}, u32[]{:S(2)}) collective-permute-start(f32[4,256,128]{2,1,0:T(8,128)} %shard_map.38), channel_id=1, source_target_pairs={{0,2},{2,4},{4,6},{6,8},{8,10},{10,12},{12,14},{14,16},{16,18},{18... | collective-permute-start | bytes 1572872 | tf_op jit(solution)/shard_map/ppermute | solution.py:23
  14.6 0.0 copy-done.7
  14.6 0.6 slice_bitcast_fusion
  15.2 9.6 %collective-permute-done.2.rest_3_ = f32[4,256,128]{2,1,0:T(8,128)S(1)} collective-permute-done((f32[4,256,128]{2,1,0:T(8,128)}, f32[4,256,128]{2,1,0:T(8,128)S(1)}, u32[]{:S(2)}, u32[]{:S(2)}) %collective-permute-start.2) | collective-permute-done | bytes 524320 | tf_op jit(solution)/shard_map/ppermute | solution.py:24
  24.8 0.0 copy-start.5
  24.8 8.2 %collective-permute-done.1.rest_2_ = f32[4,256,128]{2,1,0:T(8,128)S(1)} collective-permute-done((f32[4,256,128]{2,1,0:T(8,128)}, f32[4,256,128]{2,1,0:T(8,128)S(1)}, u32[]{:S(2)}, u32[]{:S(2)}) %collective-permute-start.1) | collective-permute-done | bytes 524320 | tf_op jit(solution)/shard_map/ppermute | solution.py:23
  33.0 0.0 copy-start.6
  33.0 0.0 collective-permute-done.rest_1_
  33.0 0.0 copy-start
  33.0 0.0 copy-done.5
  33.0 0.8 %copy-done.6 = f32[4,256,128]{2,1,0:T(8,128)} copy-done((f32[4,256,128]{2,1,0:T(8,128)}, f32[4,256,128]{2,1,0:T(8,128)S(1)}, u32[]{:S(2)}) %copy-start.6) | copy-done | bytes 524312
  33.8 0.4 copy-done
  34.2 5.4 %shard_map.39.rest_1_ = f32[6,256,128]{2,1,0:T(8,128)} custom-call(s32[1]{0:T(128)} %bitcast.side_ref, s32[2,5]{1,0:T(2,128)} %scale_ref.7, s32[2,5]{1,0:T(2,128)} %get-tuple-element.9.keep_ref, f32[2,5,256,128]{3,2,1,0:T(8,128)} %rest_0_.3, f32[2,5,256,128]{3,2,1,0:T(8,128)} %copy-done, f32[4,256,128]{2,1,0:T(8,128)} %copy-done.6, f32[4,256,128]{2,1,0:T(8,128)} %copy-done.5), custom_call_target="tpu_custom_call" | custom-call | tf_op jit(solution)/shard_map/pallas_call | solution.py:179
  39.7 0.0 collective-permute-start.4
  39.7 4.3 %shard_map.37 = (f32[4,256,128]{2,1,0:T(8,128)}, f32[3,128,128]{2,1,0:T(8,128)}) custom-call(s32[1]{0:T(128)} %bitcast.side_ref, s32[2,5]{1,0:T(2,128)} %scale_ref.7, s32[2,5]{1,0:T(2,128)} %get-tuple-element.9.keep_ref, f32[2,5,256,128]{3,2,1,0:T(8,128)} %rest_0_.3, f32[2,5,256,128]{3,2,1,0:T(8,128)} %copy-done), custom_call_target="tpu_custom_call" | custom-call | tf_op jit(solution)/shard_map/pallas_call | solution.py:179
  44.0 1.9 %collective-permute-start.6 = (f32[4,256,128]{2,1,0:T(8,128)}, f32[4,256,128]{2,1,0:T(8,128)S(1)}, u32[]{:S(2)}, u32[]{:S(2)}) collective-permute-start(f32[4,256,128]{2,1,0:T(8,128)} %get-tuple-element.7.rest_0_), channel_id=1, source_target_pairs={{2,0},{4,2},{6,4},{8,6},{10,8},{12,10},{14,12},{16,14},{18,16},{20... | collective-permute-start | bytes 1572872 | tf_op jit(solution)/shard_map/ppermute | solution.py:24
  45.9 3.9 %collective-permute-start.5 = (f32[4,256,128]{2,1,0:T(8,128)}, f32[4,256,128]{2,1,0:T(8,128)S(1)}, u32[]{:S(2)}, u32[]{:S(2)}) collective-permute-start(f32[4,256,128]{2,1,0:T(8,128)} %get-tuple-element.7.rest_0_), channel_id=1, source_target_pairs={{0,2},{2,4},{4,6},{6,8},{8,10},{10,12},{12,14},{14,16},{16,18},{18... | collective-permute-start | bytes 1572872 | tf_op jit(solution)/shard_map/ppermute | solution.py:23
  49.8 0.1 collective-permute-start.3
  49.9 1.6 %collective-permute-done.3.rest_2_ = f32[3,128,128]{2,1,0:T(8,128)S(1)} collective-permute-done((f32[3,128,128]{2,1,0:T(8,128)}, f32[3,128,128]{2,1,0:T(8,128)S(1)}, u32[]{:S(2)}, u32[]{:S(2)}) %collective-permute-start.3) | collective-permute-done | bytes 196640 | tf_op jit(solution)/shard_map/ppermute | solution.py:18
  51.6 0.7 copy-done.1
  52.2 4.0 %shard_map.40.rest_6_ = f32[2,5,256,128]{3,2,1,0:T(8,128)} custom-call(s32[1]{0:T(128)} %bitcast.side_ref, s32[2,5]{1,0:T(2,128)} %scale_ref.7, s32[2,5]{1,0:T(2,128)} %get-tuple-element.10.keep_ref, f32[4,256,128]{2,1,0:T(8,128)} %get-tuple-element.7.rest_0_, f32[6,256,128]{2,1,0:T(8,128)} %shard_map.39.rest_1_, f32[3,128,128]{2,1,0:T(8,128)} %copy-done.1), custom_call_target="tpu_custom_call" | custom-call | tf_op jit(solution)/shard_map/pallas_call | solution.py:179
  56.2 4.2 %collective-permute-done.6.rest_5_ = f32[4,256,128]{2,1,0:T(8,128)S(1)} collective-permute-done((f32[4,256,128]{2,1,0:T(8,128)}, f32[4,256,128]{2,1,0:T(8,128)S(1)}, u32[]{:S(2)}, u32[]{:S(2)}) %collective-permute-start.6) | collective-permute-done | bytes 524320 | tf_op jit(solution)/shard_map/ppermute | solution.py:24
  60.4 6.1 %collective-permute-done.5.rest_4_ = f32[4,256,128]{2,1,0:T(8,128)S(1)} collective-permute-done((f32[4,256,128]{2,1,0:T(8,128)}, f32[4,256,128]{2,1,0:T(8,128)S(1)}, u32[]{:S(2)}, u32[]{:S(2)}) %collective-permute-start.5) | collective-permute-done | bytes 524320 | tf_op jit(solution)/shard_map/ppermute | solution.py:23
  66.6 0.0 collective-permute-done.4.rest_3_
  66.6 0.0 copy-done.3
  66.6 0.8 %copy-done.4 = f32[4,256,128]{2,1,0:T(8,128)} copy-done((f32[4,256,128]{2,1,0:T(8,128)}, f32[4,256,128]{2,1,0:T(8,128)S(1)}, u32[]{:S(2)}) %copy-start.4) | copy-done | bytes 524312
  67.4 0.9 %copy-done.2 = f32[6,256,128]{2,1,0:T(8,128)} copy-done((f32[6,256,128]{2,1,0:T(8,128)}, f32[6,256,128]{2,1,0:T(8,128)S(1)}, u32[]{:S(2)}) %copy-start.2) | copy-done | bytes 786456
  68.3 5.8 %shard_map.41 = f32[2,5,256,128]{3,2,1,0:T(8,128)} custom-call(s32[1]{0:T(128)} %bitcast.side_ref, s32[2,5]{1,0:T(2,128)} %scale_ref.7, s32[2,5]{1,0:T(2,128)} %get-tuple-element.10.keep_ref, f32[4,256,128]{2,1,0:T(8,128)} %get-tuple-element.7.rest_0_, f32[6,256,128]{2,1,0:T(8,128)} %shard_map.39.rest_1_, f32[3,128,128]{2,1,0:T(8,128)} %copy-done.1, ...), custom_call_target="tpu_custom_call" | custom-call | tf_op jit(solution)/shard_map/pallas_call | solution.py:179
  (4 shorter events, 0.0 us)
Async XLA Ops:
  0.0 14.6 %copy-start.7 = (s32[2,2,5]{2,1,0:T(2,128)S(1)}, s32[2,2,5]{2,1,0:T(2,128)}, u32[]{:S(2)}) copy-start(s32[2,2,5]{2,1,0:T(2,128)} %param.5) | copy-start | bytes 244
  0.0 33.0 %collective-permute-start = (f32[2,5,256,128]{3,2,1,0:T(8,128)}, f32[2,5,256,128]{3,2,1,0:T(8,128)S(1)}, u32[]{:S(2)}, u32[]{:S(2)}) collective-permute-start(f32[2,5,256,128]{3,2,1,0:T(8,128)} %rest_0_.3), channel_id=1, source_target_pairs={{0,1},{1,0},{2,3},{3,2},{4,5},{5,4},{6,7},{7,6},{8,9},{9,8},{10,11... | collective-permute-start | bytes 3932168 | tf_op jit(solution)/shard_map/ppermute | solution.py:18
  2.2 22.6 %collective-permute-start.2 = (f32[4,256,128]{2,1,0:T(8,128)}, f32[4,256,128]{2,1,0:T(8,128)S(1)}, u32[]{:S(2)}, u32[]{:S(2)}) collective-permute-start(f32[4,256,128]{2,1,0:T(8,128)} %shard_map.38), channel_id=1, source_target_pairs={{2,0},{4,2},{6,4},{8,6},{10,8},{12,10},{14,12},{16,14},{18,16},{20... | collective-permute-start | bytes 1572872 | tf_op jit(solution)/shard_map/ppermute | solution.py:24
  12.6 20.4 %collective-permute-start.1 = (f32[4,256,128]{2,1,0:T(8,128)}, f32[4,256,128]{2,1,0:T(8,128)S(1)}, u32[]{:S(2)}, u32[]{:S(2)}) collective-permute-start(f32[4,256,128]{2,1,0:T(8,128)} %shard_map.38), channel_id=1, source_target_pairs={{0,2},{2,4},{4,6},{6,8},{8,10},{10,12},{12,14},{14,16},{16,18},{18... | collective-permute-start | bytes 1572872 | tf_op jit(solution)/shard_map/ppermute | solution.py:23
  24.8 8.2 %copy-start.5 = (f32[4,256,128]{2,1,0:T(8,128)}, f32[4,256,128]{2,1,0:T(8,128)S(1)}, u32[]{:S(2)}) copy-start(f32[4,256,128]{2,1,0:T(8,128)S(1)} %collective-permute-done.2.rest_3_) | copy-start | bytes 1572868
  33.0 0.8 %copy-start.6 = (f32[4,256,128]{2,1,0:T(8,128)}, f32[4,256,128]{2,1,0:T(8,128)S(1)}, u32[]{:S(2)}) copy-start(f32[4,256,128]{2,1,0:T(8,128)S(1)} %collective-permute-done.1.rest_2_) | copy-start | bytes 1572868
  33.0 1.2 %copy-start = (f32[2,5,256,128]{3,2,1,0:T(8,128)}, f32[2,5,256,128]{3,2,1,0:T(8,128)S(1)}, u32[]{:S(2)}) copy-start(f32[2,5,256,128]{3,2,1,0:T(8,128)S(1)} %collective-permute-done.rest_1_) | copy-start | bytes 3932164
  39.7 26.9 %collective-permute-start.4 = (f32[6,256,128]{2,1,0:T(8,128)}, f32[6,256,128]{2,1,0:T(8,128)S(1)}, u32[]{:S(2)}, u32[]{:S(2)}) collective-permute-start(f32[6,256,128]{2,1,0:T(8,128)} %shard_map.39.rest_1_), channel_id=1, source_target_pairs={{0,1},{1,0},{2,3},{3,2},{4,5},{5,4},{6,7},{7,6},{8,9},{9,8},{10,11... | collective-permute-start | bytes 2359304 | tf_op jit(solution)/shard_map/ppermute | solution.py:18
  44.0 16.4 %collective-permute-start.6 = (f32[4,256,128]{2,1,0:T(8,128)}, f32[4,256,128]{2,1,0:T(8,128)S(1)}, u32[]{:S(2)}, u32[]{:S(2)}) collective-permute-start(f32[4,256,128]{2,1,0:T(8,128)} %get-tuple-element.7.rest_0_), channel_id=1, source_target_pairs={{2,0},{4,2},{6,4},{8,6},{10,8},{12,10},{14,12},{16,14},{18,16},{20... | collective-permute-start | bytes 1572872 | tf_op jit(solution)/shard_map/ppermute | solution.py:24
  45.9 20.7 %collective-permute-start.5 = (f32[4,256,128]{2,1,0:T(8,128)}, f32[4,256,128]{2,1,0:T(8,128)S(1)}, u32[]{:S(2)}, u32[]{:S(2)}) collective-permute-start(f32[4,256,128]{2,1,0:T(8,128)} %get-tuple-element.7.rest_0_), channel_id=1, source_target_pairs={{0,2},{2,4},{4,6},{6,8},{8,10},{10,12},{12,14},{14,16},{16,18},{18... | collective-permute-start | bytes 1572872 | tf_op jit(solution)/shard_map/ppermute | solution.py:23
  49.8 1.7 %collective-permute-start.3 = (f32[3,128,128]{2,1,0:T(8,128)}, f32[3,128,128]{2,1,0:T(8,128)S(1)}, u32[]{:S(2)}, u32[]{:S(2)}) collective-permute-start(f32[3,128,128]{2,1,0:T(8,128)} %get-tuple-element.8), channel_id=1, source_target_pairs={{0,1},{1,0},{2,3},{3,2},{4,5},{5,4},{6,7},{7,6},{8,9},{9,8},{10,11... | collective-permute-start | bytes 589832 | tf_op jit(solution)/shard_map/ppermute | solution.py:18
  51.6 0.7 copy-start.1
  60.4 6.2 %copy-start.3 = (f32[4,256,128]{2,1,0:T(8,128)}, f32[4,256,128]{2,1,0:T(8,128)S(1)}, u32[]{:S(2)}) copy-start(f32[4,256,128]{2,1,0:T(8,128)S(1)} %collective-permute-done.6.rest_5_) | copy-start | bytes 1572868
  66.6 0.8 %copy-start.4 = (f32[4,256,128]{2,1,0:T(8,128)}, f32[4,256,128]{2,1,0:T(8,128)S(1)}, u32[]{:S(2)}) copy-start(f32[4,256,128]{2,1,0:T(8,128)S(1)} %collective-permute-done.5.rest_4_) | copy-start | bytes 1572868
  67.4 0.9 %copy-start.2 = (f32[6,256,128]{2,1,0:T(8,128)}, f32[6,256,128]{2,1,0:T(8,128)S(1)}, u32[]{:S(2)}) copy-start(f32[6,256,128]{2,1,0:T(8,128)S(1)} %collective-permute-done.4.rest_3_) | copy-start | bytes 2359300

commit v10 on v9

--- a/solution.py
+++ b/solution.py
@@ -12,6 +12,7 @@
 OFF = ((0, 0), (0, 1), (0, 4), (1, 0), (1, 3), (1, 4))
 ALL = tuple((row, slot) for row in range(2) for slot in range(5))
 CONTRACT = (((1,), (0,)), ((), ()))
+PRECISION = lax.Precision.HIGH
 
 
 def swap_help(value):
@@ -23,11 +24,6 @@
     from_left = lax.ppermute(block, "rows", [(i, i + 1) for i in range(count - 1)])
     from_right = lax.ppermute(block, "rows", [(i + 1, i) for i in range(count - 1)])
     return from_left, from_right
-
-
-def split(x):
-    high = x.astype(jnp.bfloat16)
-    return high, (x - high.astype(jnp.float32)).astype(jnp.bfloat16)
 
 
 class Tiles:
@@ -73,7 +69,7 @@
 def band_kernel(tiles, odd, parts, scaled, mode, quarters, side_ref, scale_ref, keep_ref, *rest):
     mine = Tiles(rest[:parts], scale_ref if scaled else None)
     rest = rest[parts:]
-    other_refs = rest[: len(rest) - 5 - (3 if mode == "halo" else (2 if mode == "plain" else 0)) - (1 if quarters else 0)]
+    other_refs = rest[: len(rest) - 3 - (3 if mode == "halo" else (2 if mode == "plain" else 0)) - (1 if quarters else 0)]
     rest = rest[len(other_refs) :]
     if mode in ("plain", "halo"):
         left_ref, right_ref = rest[:2]
@@ -82,9 +78,9 @@
         partial_ref = rest[0]
         rest = rest[1:]
     if quarters:
-        out_ref, quarter_ref, lh_ref, ll_ref, rh_ref, rl_ref = rest
+        out_ref, quarter_ref, lh_ref, rh_ref = rest
     else:
-        out_ref, lh_ref, ll_ref, rh_ref, rl_ref = rest
+        out_ref, lh_ref, rh_ref = rest
     tile = lh_ref.shape[1]
     half = tile // 2
     side = side_ref[0]
@@ -106,16 +102,13 @@
     for row in range(2):
         offsets = [o for o in range(5) if wanted(row + o - 2)]
         for place_k, offset in enumerate(offsets):
-            high, low = split(jnp.concatenate([mine(row, offset), other(row, offset)], axis=1))
-            lh_ref[row, :, place_k * tile : (place_k + 1) * tile] = high
-            ll_ref[row, :, place_k * tile : (place_k + 1) * tile] = low
+            lh_ref[row, :, place_k * tile : (place_k + 1) * tile] = jnp.concatenate([mine(row, offset), other(row, offset)], axis=1)
             k = row + offset - 2
             for place, (index, slot) in enumerate(by_row[row]):
                 col = row + slot - 2
                 where = (row, slice(place_k * tile, (place_k + 1) * tile), slice(place * half, (place + 1) * half))
                 if abs(k - col) > 2:
-                    rh_ref[where] = jnp.zeros((tile, half), jnp.bfloat16)
-                    rl_ref[where] = jnp.zeros((tile, half), jnp.bfloat16)
+                    rh_ref[where] = jnp.zeros((tile, half), jnp.float32)
                     continue
                 if k in (0, 1):
                     b = col - k + 2
@@ -127,16 +120,9 @@
                 else:
                     s = k - col + 2
                     right = jnp.concatenate([mine(col, s, own), other(col, s, own)], axis=1).T
-                high, low = split(right)
-                rh_ref[where] = high
-                rl_ref[where] = low
+                rh_ref[where] = right
     for row in range(2):
-        def one(x, y):
-            return lax.dot_general(x, y, CONTRACT, preferred_element_type=jnp.float32)
-
-        a_high = lh_ref[row]
-        b_high = rh_ref[row]
-        acc = one(ll_ref[row], b_high) + one(a_high, rl_ref[row]) + one(a_high, b_high)
+        acc = lax.dot_general(lh_ref[row], rh_ref[row], CONTRACT, precision=PRECISION, preferred_element_type=jnp.float32)
         for place, (index, slot) in enumerate(by_row[row]):
             value = acc[:, place * half : (place + 1) * half]
             if mode == "own":
@@ -181,7 +167,7 @@
         out_shape=out_shape,
         in_specs=[smem, smem, smem] + [vmem] * (len(args) - 3),
         out_specs=(vmem, vmem) if quarters else vmem,
-        scratch_shapes=[pltpu.VMEM(lefts, jnp.bfloat16)] * 2 + [pltpu.VMEM(rights, jnp.bfloat16)] * 2,
+        scratch_shapes=[pltpu.VMEM(lefts, jnp.float32), pltpu.VMEM(rights, jnp.float32)],
     )(*args)
 
 

time: 74.3 us -> 73.4 us (0.988)
  Pallas kernels: 21.6 us -> 20.6 us
    pallas_call x4, Pallas kernels: 19.5 us -> 18.4 us  [band_call(): pl.pallas_call(functools.partial(band_kernel, tiles, odd, len(mine), scal...]
where the time goes in v10:
time: 73.4 us; the launch traced here: 73.1 us
  waiting for transfers between devices  29.9 us (41%)
  Pallas kernels  20.6 us (28%)
  starting transfers between devices  18.3 us (25%)
  local copies, waits for them, and re-layouts  4.21 us (6%)
    pallas_call x4, Pallas kernels, band_call(): pl.pallas_call(functools.partial(band_kernel, tiles, odd, len(mine), scal...  18.4 us
    ppermute x2, waiting for transfers between devices, send_block(): lax.ppermute(block, 'rows', [(i, i + 1) for i in range(count - 1)])  14.4 us
    ppermute x2, waiting for transfers between devices, send_block(): lax.ppermute(block, 'rows', [(i + 1, i) for i in range(count - 1)])  13.9 us
    ppermute x2, starting transfers between devices, send_block(): lax.ppermute(block, 'rows', [(i + 1, i) for i in range(count - 1)])  12.4 us
    ppermute x2, starting transfers between devices, send_block(): lax.ppermute(block, 'rows', [(i, i + 1) for i in range(count - 1)])  5.84 us
    unnamed x16, local copies, waits for them, and re-layouts  3.61 us
    pallas_call x1, Pallas kernels, first_block(): pl.pallas_call(block_kernel, out_shape=jax.ShapeDtypeStruct((len(DIAG),)...  2.17 us
    ppermute x3, waiting for transfers between devices, swap_help(): return lax.ppermute(value, 'help', [(0, 1), (1, 0)])  1.64 us
  transfers between devices with their start and end apart: 7, of which 5 were waited for; matrix products, arithmetic and copies ran while one was open for 1% of the time, Pallas kernels for 14%

profile of v10, /device:TPU:6, one launch (start us, length us, event | category | flops | bytes accessed | tf_op | source)
XLA Modules:
  0.0 73.1 jit_solution(11990098044388544636)
XLA Ops:
  0.0 0.0 copy-start.7
  0.0 0.0 collective-permute-start
  0.0 2.2 %shard_map.38 = f32[4,256,128]{2,1,0:T(8,128)} custom-call(s32[2,5]{1,0:T(2,128)} %scale_ref.7, f32[2,5,256,128]{3,2,1,0:T(8,128)} %rest_0_.3), custom_call_target="tpu_custom_call" | custom-call | tf_op jit(solution)/shard_map/pallas_call | solution.py:180
  2.2 10.5 %collective-permute-start.2 = (f32[4,256,128]{2,1,0:T(8,128)}, f32[4,256,128]{2,1,0:T(8,128)S(1)}, u32[]{:S(2)}, u32[]{:S(2)}) collective-permute-start(f32[4,256,128]{2,1,0:T(8,128)} %shard_map.38), channel_id=1, source_target_pairs={{2,0},{4,2},{6,4},{8,6},{10,8},{12,10},{14,12},{16,14},{18,16},{20... | collective-permute-start | bytes 1572872 | tf_op jit(solution)/shard_map/ppermute | solution.py:25
  12.6 1.9 %collective-permute-start.1 = (f32[4,256,128]{2,1,0:T(8,128)}, f32[4,256,128]{2,1,0:T(8,128)S(1)}, u32[]{:S(2)}, u32[]{:S(2)}) collective-permute-start(f32[4,256,128]{2,1,0:T(8,128)} %shard_map.38), channel_id=1, source_target_pairs={{0,2},{2,4},{4,6},{6,8},{8,10},{10,12},{12,14},{14,16},{16,18},{18... | collective-permute-start | bytes 1572872 | tf_op jit(solution)/shard_map/ppermute | solution.py:24
  14.6 0.0 copy-done.7
  14.6 0.6 slice_bitcast_fusion
  15.2 9.6 %collective-permute-done.2.rest_3_ = f32[4,256,128]{2,1,0:T(8,128)S(1)} collective-permute-done((f32[4,256,128]{2,1,0:T(8,128)}, f32[4,256,128]{2,1,0:T(8,128)S(1)}, u32[]{:S(2)}, u32[]{:S(2)}) %collective-permute-start.2) | collective-permute-done | bytes 524320 | tf_op jit(solution)/shard_map/ppermute | solution.py:25
  24.8 0.0 copy-start.5
  24.8 8.2 %collective-permute-done.1.rest_2_ = f32[4,256,128]{2,1,0:T(8,128)S(1)} collective-permute-done((f32[4,256,128]{2,1,0:T(8,128)}, f32[4,256,128]{2,1,0:T(8,128)S(1)}, u32[]{:S(2)}, u32[]{:S(2)}) %collective-permute-start.1) | collective-permute-done | bytes 524320 | tf_op jit(solution)/shard_map/ppermute | solution.py:24
  33.0 0.0 copy-start.6
  33.0 0.0 collective-permute-done.rest_1_
  33.0 0.0 copy-start
  33.0 0.0 copy-done.5
  33.0 0.8 %copy-done.6 = f32[4,256,128]{2,1,0:T(8,128)} copy-done((f32[4,256,128]{2,1,0:T(8,128)}, f32[4,256,128]{2,1,0:T(8,128)S(1)}, u32[]{:S(2)}) %copy-start.6) | copy-done | bytes 524312
  33.8 0.4 copy-done
  34.2 5.1 %shard_map.39.rest_1_ = f32[6,256,128]{2,1,0:T(8,128)} custom-call(s32[1]{0:T(128)} %bitcast.side_ref, s32[2,5]{1,0:T(2,128)} %scale_ref.7, s32[2,5]{1,0:T(2,128)} %get-tuple-element.9.keep_ref, f32[2,5,256,128]{3,2,1,0:T(8,128)} %rest_0_.3, f32[2,5,256,128]{3,2,1,0:T(8,128)} %copy-done, f32[4,256,128]{2,1,0:T(8,128)} %copy-done.6, f32[4,256,128]{2,1,0:T(8,128)} %copy-done.5), custom_call_target="tpu_custom_call" | custom-call | tf_op jit(solution)/shard_map/pallas_call | solution.py:165
  39.3 0.0 collective-permute-start.4
  39.3 4.0 %shard_map.37 = (f32[4,256,128]{2,1,0:T(8,128)}, f32[3,128,128]{2,1,0:T(8,128)}) custom-call(s32[1]{0:T(128)} %bitcast.side_ref, s32[2,5]{1,0:T(2,128)} %scale_ref.7, s32[2,5]{1,0:T(2,128)} %get-tuple-element.9.keep_ref, f32[2,5,256,128]{3,2,1,0:T(8,128)} %rest_0_.3, f32[2,5,256,128]{3,2,1,0:T(8,128)} %copy-done), custom_call_target="tpu_custom_call" | custom-call | tf_op jit(solution)/shard_map/pallas_call | solution.py:165
  43.3 1.9 %collective-permute-start.6 = (f32[4,256,128]{2,1,0:T(8,128)}, f32[4,256,128]{2,1,0:T(8,128)S(1)}, u32[]{:S(2)}, u32[]{:S(2)}) collective-permute-start(f32[4,256,128]{2,1,0:T(8,128)} %get-tuple-element.7.rest_0_), channel_id=1, source_target_pairs={{2,0},{4,2},{6,4},{8,6},{10,8},{12,10},{14,12},{16,14},{18,16},{20... | collective-permute-start | bytes 1572872 | tf_op jit(solution)/shard_map/ppermute | solution.py:25
  45.3 3.9 %collective-permute-start.5 = (f32[4,256,128]{2,1,0:T(8,128)}, f32[4,256,128]{2,1,0:T(8,128)S(1)}, u32[]{:S(2)}, u32[]{:S(2)}) collective-permute-start(f32[4,256,128]{2,1,0:T(8,128)} %get-tuple-element.7.rest_0_), channel_id=1, source_target_pairs={{0,2},{2,4},{4,6},{6,8},{8,10},{10,12},{12,14},{14,16},{16,18},{18... | collective-permute-start | bytes 1572872 | tf_op jit(solution)/shard_map/ppermute | solution.py:24
  49.2 0.1 collective-permute-start.3
  49.3 1.6 %collective-permute-done.3.rest_2_ = f32[3,128,128]{2,1,0:T(8,128)S(1)} collective-permute-done((f32[3,128,128]{2,1,0:T(8,128)}, f32[3,128,128]{2,1,0:T(8,128)S(1)}, u32[]{:S(2)}, u32[]{:S(2)}) %collective-permute-start.3) | collective-permute-done | bytes 196640 | tf_op jit(solution)/shard_map/ppermute | solution.py:19
  50.9 0.7 copy-done.1
  51.6 3.9 %shard_map.40.rest_6_ = f32[2,5,256,128]{3,2,1,0:T(8,128)} custom-call(s32[1]{0:T(128)} %bitcast.side_ref, s32[2,5]{1,0:T(2,128)} %scale_ref.7, s32[2,5]{1,0:T(2,128)} %get-tuple-element.10.keep_ref, f32[4,256,128]{2,1,0:T(8,128)} %get-tuple-element.7.rest_0_, f32[6,256,128]{2,1,0:T(8,128)} %shard_map.39.rest_1_, f32[3,128,128]{2,1,0:T(8,128)} %copy-done.1), custom_call_target="tpu_custom_call" | custom-call | tf_op jit(solution)/shard_map/pallas_call | solution.py:165
  55.5 4.3 %collective-permute-done.6.rest_5_ = f32[4,256,128]{2,1,0:T(8,128)S(1)} collective-permute-done((f32[4,256,128]{2,1,0:T(8,128)}, f32[4,256,128]{2,1,0:T(8,128)S(1)}, u32[]{:S(2)}, u32[]{:S(2)}) %collective-permute-start.6) | collective-permute-done | bytes 524320 | tf_op jit(solution)/shard_map/ppermute | solution.py:25
  59.8 6.1 %collective-permute-done.5.rest_4_ = f32[4,256,128]{2,1,0:T(8,128)S(1)} collective-permute-done((f32[4,256,128]{2,1,0:T(8,128)}, f32[4,256,128]{2,1,0:T(8,128)S(1)}, u32[]{:S(2)}, u32[]{:S(2)}) %collective-permute-start.5) | collective-permute-done | bytes 524320 | tf_op jit(solution)/shard_map/ppermute | solution.py:24
  65.9 0.0 collective-permute-done.4.rest_3_
  65.9 0.0 copy-done.3
  65.9 0.8 %copy-done.4 = f32[4,256,128]{2,1,0:T(8,128)} copy-done((f32[4,256,128]{2,1,0:T(8,128)}, f32[4,256,128]{2,1,0:T(8,128)S(1)}, u32[]{:S(2)}) %copy-start.4) | copy-done | bytes 524312
  66.7 0.9 %copy-done.2 = f32[6,256,128]{2,1,0:T(8,128)} copy-done((f32[6,256,128]{2,1,0:T(8,128)}, f32[6,256,128]{2,1,0:T(8,128)S(1)}, u32[]{:S(2)}) %copy-start.2) | copy-done | bytes 786456
  67.6 5.5 %shard_map.41 = f32[2,5,256,128]{3,2,1,0:T(8,128)} custom-call(s32[1]{0:T(128)} %bitcast.side_ref, s32[2,5]{1,0:T(2,128)} %scale_ref.7, s32[2,5]{1,0:T(2,128)} %get-tuple-element.10.keep_ref, f32[4,256,128]{2,1,0:T(8,128)} %get-tuple-element.7.rest_0_, f32[6,256,128]{2,1,0:T(8,128)} %shard_map.39.rest_1_, f32[3,128,128]{2,1,0:T(8,128)} %copy-done.1, ...), custom_call_target="tpu_custom_call" | custom-call | tf_op jit(solution)/shard_map/pallas_call | solution.py:165
  (4 shorter events, 0.0 us)
Async XLA Ops:
  0.0 14.6 %copy-start.7 = (s32[2,2,5]{2,1,0:T(2,128)S(1)}, s32[2,2,5]{2,1,0:T(2,128)}, u32[]{:S(2)}) copy-start(s32[2,2,5]{2,1,0:T(2,128)} %param.5) | copy-start | bytes 244
  0.0 33.0 %collective-permute-start = (f32[2,5,256,128]{3,2,1,0:T(8,128)}, f32[2,5,256,128]{3,2,1,0:T(8,128)S(1)}, u32[]{:S(2)}, u32[]{:S(2)}) collective-permute-start(f32[2,5,256,128]{3,2,1,0:T(8,128)} %rest_0_.3), channel_id=1, source_target_pairs={{0,1},{1,0},{2,3},{3,2},{4,5},{5,4},{6,7},{7,6},{8,9},{9,8},{10,11... | collective-permute-start | bytes 3932168 | tf_op jit(solution)/shard_map/ppermute | solution.py:19
  2.2 22.6 %collective-permute-start.2 = (f32[4,256,128]{2,1,0:T(8,128)}, f32[4,256,128]{2,1,0:T(8,128)S(1)}, u32[]{:S(2)}, u32[]{:S(2)}) collective-permute-start(f32[4,256,128]{2,1,0:T(8,128)} %shard_map.38), channel_id=1, source_target_pairs={{2,0},{4,2},{6,4},{8,6},{10,8},{12,10},{14,12},{16,14},{18,16},{20... | collective-permute-start | bytes 1572872 | tf_op jit(solution)/shard_map/ppermute | solution.py:25
  12.6 20.4 %collective-permute-start.1 = (f32[4,256,128]{2,1,0:T(8,128)}, f32[4,256,128]{2,1,0:T(8,128)S(1)}, u32[]{:S(2)}, u32[]{:S(2)}) collective-permute-start(f32[4,256,128]{2,1,0:T(8,128)} %shard_map.38), channel_id=1, source_target_pairs={{0,2},{2,4},{4,6},{6,8},{8,10},{10,12},{12,14},{14,16},{16,18},{18... | collective-permute-start | bytes 1572872 | tf_op jit(solution)/shard_map/ppermute | solution.py:24
  24.8 8.2 %copy-start.5 = (f32[4,256,128]{2,1,0:T(8,128)}, f32[4,256,128]{2,1,0:T(8,128)S(1)}, u32[]{:S(2)}) copy-start(f32[4,256,128]{2,1,0:T(8,128)S(1)} %collective-permute-done.2.rest_3_) | copy-start | bytes 1572868
  33.0 0.8 %copy-start.6 = (f32[4,256,128]{2,1,0:T(8,128)}, f32[4,256,128]{2,1,0:T(8,128)S(1)}, u32[]{:S(2)}) copy-start(f32[4,256,128]{2,1,0:T(8,128)S(1)} %collective-permute-done.1.rest_2_) | copy-start | bytes 1572868
  33.0 1.2 %copy-start = (f32[2,5,256,128]{3,2,1,0:T(8,128)}, f32[2,5,256,128]{3,2,1,0:T(8,128)S(1)}, u32[]{:S(2)}) copy-start(f32[2,5,256,128]{3,2,1,0:T(8,128)S(1)} %collective-permute-done.rest_1_) | copy-start | bytes 3932164
  39.3 26.6 %collective-permute-start.4 = (f32[6,256,128]{2,1,0:T(8,128)}, f32[6,256,128]{2,1,0:T(8,128)S(1)}, u32[]{:S(2)}, u32[]{:S(2)}) collective-permute-start(f32[6,256,128]{2,1,0:T(8,128)} %shard_map.39.rest_1_), channel_id=1, source_target_pairs={{0,1},{1,0},{2,3},{3,2},{4,5},{5,4},{6,7},{7,6},{8,9},{9,8},{10,11... | collective-permute-start | bytes 2359304 | tf_op jit(solution)/shard_map/ppermute | solution.py:19
  43.3 16.4 %collective-permute-start.6 = (f32[4,256,128]{2,1,0:T(8,128)}, f32[4,256,128]{2,1,0:T(8,128)S(1)}, u32[]{:S(2)}, u32[]{:S(2)}) collective-permute-start(f32[4,256,128]{2,1,0:T(8,128)} %get-tuple-element.7.rest_0_), channel_id=1, source_target_pairs={{2,0},{4,2},{6,4},{8,6},{10,8},{12,10},{14,12},{16,14},{18,16},{20... | collective-permute-start | bytes 1572872 | tf_op jit(solution)/shard_map/ppermute | solution.py:25
  45.3 20.7 %collective-permute-start.5 = (f32[4,256,128]{2,1,0:T(8,128)}, f32[4,256,128]{2,1,0:T(8,128)S(1)}, u32[]{:S(2)}, u32[]{:S(2)}) collective-permute-start(f32[4,256,128]{2,1,0:T(8,128)} %get-tuple-element.7.rest_0_), channel_id=1, source_target_pairs={{0,2},{2,4},{4,6},{6,8},{8,10},{10,12},{12,14},{14,16},{16,18},{18... | collective-permute-start | bytes 1572872 | tf_op jit(solution)/shard_map/ppermute | solution.py:24
  49.2 1.7 %collective-permute-start.3 = (f32[3,128,128]{2,1,0:T(8,128)}, f32[3,128,128]{2,1,0:T(8,128)S(1)}, u32[]{:S(2)}, u32[]{:S(2)}) collective-permute-start(f32[3,128,128]{2,1,0:T(8,128)} %get-tuple-element.8), channel_id=1, source_target_pairs={{0,1},{1,0},{2,3},{3,2},{4,5},{5,4},{6,7},{7,6},{8,9},{9,8},{10,11... | collective-permute-start | bytes 589832 | tf_op jit(solution)/shard_map/ppermute | solution.py:19
  50.9 0.7 copy-start.1
  59.8 6.2 %copy-start.3 = (f32[4,256,128]{2,1,0:T(8,128)}, f32[4,256,128]{2,1,0:T(8,128)S(1)}, u32[]{:S(2)}) copy-start(f32[4,256,128]{2,1,0:T(8,128)S(1)} %collective-permute-done.6.rest_5_) | copy-start | bytes 1572868
  65.9 0.8 %copy-start.4 = (f32[4,256,128]{2,1,0:T(8,128)}, f32[4,256,128]{2,1,0:T(8,128)S(1)}, u32[]{:S(2)}) copy-start(f32[4,256,128]{2,1,0:T(8,128)S(1)} %collective-permute-done.5.rest_4_) | copy-start | bytes 1572868
  66.7 0.9 %copy-start.2 = (f32[6,256,128]{2,1,0:T(8,128)}, f32[6,256,128]{2,1,0:T(8,128)S(1)}, u32[]{:S(2)}) copy-start(f32[6,256,128]{2,1,0:T(8,128)S(1)} %collective-permute-done.4.rest_3_) | copy-start | bytes 2359300

commit v11 on v10

--- a/solution.py
+++ b/solution.py
@@ -12,7 +12,6 @@
 OFF = ((0, 0), (0, 1), (0, 4), (1, 0), (1, 3), (1, 4))
 ALL = tuple((row, slot) for row in range(2) for slot in range(5))
 CONTRACT = (((1,), (0,)), ((), ()))
-PRECISION = lax.Precision.HIGH
 
 
 def swap_help(value):
@@ -121,10 +120,27 @@
                     s = k - col + 2
                     right = jnp.concatenate([mine(col, s, own), other(col, s, own)], axis=1).T
                 rh_ref[where] = right
+
+    def one(x, y):
+        return lax.dot_general(x, y, CONTRACT, precision=lax.Precision.HIGH, preferred_element_type=jnp.float32)
+
     for row in range(2):
-        acc = lax.dot_general(lh_ref[row], rh_ref[row], CONTRACT, precision=PRECISION, preferred_element_type=jnp.float32)
-        for place, (index, slot) in enumerate(by_row[row]):
-            value = acc[:, place * half : (place + 1) * half]
+        offsets = [o for o in range(5) if wanted(row + o - 2)]
+        row_tiles = by_row[row]
+        values = []
+        for first in range(0, len(row_tiles), 2):
+            chunk = range(first, min(first + 2, len(row_tiles)))
+            used = [
+                place_k
+                for place_k, offset in enumerate(offsets)
+                if any(abs(offset - row_tiles[place][1]) <= 2 for place in chunk)
+            ]
+            ks = slice(used[0] * tile, (used[-1] + 1) * tile)
+            ns = slice(chunk[0] * half, (chunk[-1] + 1) * half)
+            acc = one(lh_ref[row, :, ks], rh_ref[row, ks, ns])
+            values += [acc[:, n * half : (n + 1) * half] for n in range(len(chunk))]
+        for place, (index, slot) in enumerate(row_tiles):
+            value = values[place]
             if mode == "own":
                 out_ref[row, slot] = value
                 continue

time: 73.4 us -> 72.3 us (0.985)
  Pallas kernels: 20.6 us -> 19.5 us
    pallas_call x4, Pallas kernels: 18.4 us -> 17.3 us  [band_call(): pl.pallas_call(functools.partial(band_kernel, tiles, odd, len(mine), scal...]
where the time goes in v11:
time: 72.3 us; the launch traced here: 72.1 us
  waiting for transfers between devices  30 us (41%)
  Pallas kernels  19.5 us (27%)
  starting transfers between devices  18.3 us (25%)
  local copies, waits for them, and re-layouts  4.21 us (6%)
    pallas_call x4, Pallas kernels, band_call(): pl.pallas_call(functools.partial(band_kernel, tiles, odd, len(mine), scal...  17.3 us
    ppermute x2, waiting for transfers between devices, send_block(): lax.ppermute(block, 'rows', [(i, i + 1) for i in range(count - 1)])  14.4 us
    ppermute x2, waiting for transfers between devices, send_block(): lax.ppermute(block, 'rows', [(i + 1, i) for i in range(count - 1)])  14 us
    ppermute x2, starting transfers between devices, send_block(): lax.ppermute(block, 'rows', [(i + 1, i) for i in range(count - 1)])  12.4 us
    ppermute x2, starting transfers between devices, send_block(): lax.ppermute(block, 'rows', [(i, i + 1) for i in range(count - 1)])  5.84 us
    unnamed x16, local copies, waits for them, and re-layouts  3.61 us
    pallas_call x1, Pallas kernels, first_block(): pl.pallas_call(block_kernel, out_shape=jax.ShapeDtypeStruct((len(DIAG),)...  2.17 us
    ppermute x3, waiting for transfers between devices, swap_help(): return lax.ppermute(value, 'help', [(0, 1), (1, 0)])  1.64 us
  transfers between devices with their start and end apart: 7, of which 5 were waited for; matrix products, arithmetic and copies ran while one was open for 1% of the time, Pallas kernels for 14%

profile of v11, /device:TPU:6, one launch (start us, length us, event | category | flops | bytes accessed | tf_op | source)
XLA Modules:
  0.0 72.1 jit_solution(3975972760506477184)
XLA Ops:
  0.0 0.0 copy-start.7
  0.0 0.0 collective-permute-start
  0.0 2.2 %shard_map.38 = f32[4,256,128]{2,1,0:T(8,128)} custom-call(s32[2,5]{1,0:T(2,128)} %scale_ref.7, f32[2,5,256,128]{3,2,1,0:T(8,128)} %rest_0_.3), custom_call_target="tpu_custom_call" | custom-call | tf_op jit(solution)/shard_map/pallas_call | solution.py:196
  2.2 10.5 %collective-permute-start.2 = (f32[4,256,128]{2,1,0:T(8,128)}, f32[4,256,128]{2,1,0:T(8,128)S(1)}, u32[]{:S(2)}, u32[]{:S(2)}) collective-permute-start(f32[4,256,128]{2,1,0:T(8,128)} %shard_map.38), channel_id=1, source_target_pairs={{2,0},{4,2},{6,4},{8,6},{10,8},{12,10},{14,12},{16,14},{18,16},{20... | collective-permute-start | bytes 1572872 | tf_op jit(solution)/shard_map/ppermute | solution.py:24
  12.6 1.9 %collective-permute-start.1 = (f32[4,256,128]{2,1,0:T(8,128)}, f32[4,256,128]{2,1,0:T(8,128)S(1)}, u32[]{:S(2)}, u32[]{:S(2)}) collective-permute-start(f32[4,256,128]{2,1,0:T(8,128)} %shard_map.38), channel_id=1, source_target_pairs={{0,2},{2,4},{4,6},{6,8},{8,10},{10,12},{12,14},{14,16},{16,18},{18... | collective-permute-start | bytes 1572872 | tf_op jit(solution)/shard_map/ppermute | solution.py:23
  14.6 0.0 copy-done.7
  14.6 0.6 slice_bitcast_fusion
  15.2 9.6 %collective-permute-done.2.rest_3_ = f32[4,256,128]{2,1,0:T(8,128)S(1)} collective-permute-done((f32[4,256,128]{2,1,0:T(8,128)}, f32[4,256,128]{2,1,0:T(8,128)S(1)}, u32[]{:S(2)}, u32[]{:S(2)}) %collective-permute-start.2) | collective-permute-done | bytes 524320 | tf_op jit(solution)/shard_map/ppermute | solution.py:24
  24.8 0.0 copy-start.5
  24.8 8.2 %collective-permute-done.1.rest_2_ = f32[4,256,128]{2,1,0:T(8,128)S(1)} collective-permute-done((f32[4,256,128]{2,1,0:T(8,128)}, f32[4,256,128]{2,1,0:T(8,128)S(1)}, u32[]{:S(2)}, u32[]{:S(2)}) %collective-permute-start.1) | collective-permute-done | bytes 524320 | tf_op jit(solution)/shard_map/ppermute | solution.py:23
  33.0 0.0 copy-start.6
  33.0 0.0 collective-permute-done.rest_1_
  33.0 0.0 copy-start
  33.0 0.0 copy-done.5
  33.0 0.8 %copy-done.6 = f32[4,256,128]{2,1,0:T(8,128)} copy-done((f32[4,256,128]{2,1,0:T(8,128)}, f32[4,256,128]{2,1,0:T(8,128)S(1)}, u32[]{:S(2)}) %copy-start.6) | copy-done | bytes 524312
  33.8 0.4 copy-done
  34.2 4.6 %shard_map.39.rest_1_ = f32[6,256,128]{2,1,0:T(8,128)} custom-call(s32[1]{0:T(128)} %bitcast.side_ref, s32[2,5]{1,0:T(2,128)} %scale_ref.7, s32[2,5]{1,0:T(2,128)} %get-tuple-element.9.keep_ref, f32[2,5,256,128]{3,2,1,0:T(8,128)} %rest_0_.3, f32[2,5,256,128]{3,2,1,0:T(8,128)} %copy-done, f32[4,256,128]{2,1,0:T(8,128)} %copy-done.6, f32[4,256,128]{2,1,0:T(8,128)} %copy-done.5), custom_call_target="tpu_custom_call" | custom-call | tf_op jit(solution)/shard_map/pallas_call | solution.py:181
  38.9 0.0 collective-permute-start.4
  38.9 4.0 %shard_map.37 = (f32[4,256,128]{2,1,0:T(8,128)}, f32[3,128,128]{2,1,0:T(8,128)}) custom-call(s32[1]{0:T(128)} %bitcast.side_ref, s32[2,5]{1,0:T(2,128)} %scale_ref.7, s32[2,5]{1,0:T(2,128)} %get-tuple-element.9.keep_ref, f32[2,5,256,128]{3,2,1,0:T(8,128)} %rest_0_.3, f32[2,5,256,128]{3,2,1,0:T(8,128)} %copy-done), custom_call_target="tpu_custom_call" | custom-call | tf_op jit(solution)/shard_map/pallas_call | solution.py:181
  42.9 1.9 %collective-permute-start.6 = (f32[4,256,128]{2,1,0:T(8,128)}, f32[4,256,128]{2,1,0:T(8,128)S(1)}, u32[]{:S(2)}, u32[]{:S(2)}) collective-permute-start(f32[4,256,128]{2,1,0:T(8,128)} %get-tuple-element.7.rest_0_), channel_id=1, source_target_pairs={{2,0},{4,2},{6,4},{8,6},{10,8},{12,10},{14,12},{16,14},{18,16},{20... | collective-permute-start | bytes 1572872 | tf_op jit(solution)/shard_map/ppermute | solution.py:24
  44.8 3.9 %collective-permute-start.5 = (f32[4,256,128]{2,1,0:T(8,128)}, f32[4,256,128]{2,1,0:T(8,128)S(1)}, u32[]{:S(2)}, u32[]{:S(2)}) collective-permute-start(f32[4,256,128]{2,1,0:T(8,128)} %get-tuple-element.7.rest_0_), channel_id=1, source_target_pairs={{0,2},{2,4},{4,6},{6,8},{8,10},{10,12},{12,14},{14,16},{16,18},{18... | collective-permute-start | bytes 1572872 | tf_op jit(solution)/shard_map/ppermute | solution.py:23
  48.7 0.1 collective-permute-start.3
  48.8 1.6 %collective-permute-done.3.rest_2_ = f32[3,128,128]{2,1,0:T(8,128)S(1)} collective-permute-done((f32[3,128,128]{2,1,0:T(8,128)}, f32[3,128,128]{2,1,0:T(8,128)S(1)}, u32[]{:S(2)}, u32[]{:S(2)}) %collective-permute-start.3) | collective-permute-done | bytes 196640 | tf_op jit(solution)/shard_map/ppermute | solution.py:18
  50.5 0.7 copy-done.1
  51.2 3.8 %shard_map.40.rest_6_ = f32[2,5,256,128]{3,2,1,0:T(8,128)} custom-call(s32[1]{0:T(128)} %bitcast.side_ref, s32[2,5]{1,0:T(2,128)} %scale_ref.7, s32[2,5]{1,0:T(2,128)} %get-tuple-element.10.keep_ref, f32[4,256,128]{2,1,0:T(8,128)} %get-tuple-element.7.rest_0_, f32[6,256,128]{2,1,0:T(8,128)} %shard_map.39.rest_1_, f32[3,128,128]{2,1,0:T(8,128)} %copy-done.1), custom_call_target="tpu_custom_call" | custom-call | tf_op jit(solution)/shard_map/pallas_call | solution.py:181
  54.9 4.4 %collective-permute-done.6.rest_5_ = f32[4,256,128]{2,1,0:T(8,128)S(1)} collective-permute-done((f32[4,256,128]{2,1,0:T(8,128)}, f32[4,256,128]{2,1,0:T(8,128)S(1)}, u32[]{:S(2)}, u32[]{:S(2)}) %collective-permute-start.6) | collective-permute-done | bytes 524320 | tf_op jit(solution)/shard_map/ppermute | solution.py:24
  59.3 6.1 %collective-permute-done.5.rest_4_ = f32[4,256,128]{2,1,0:T(8,128)S(1)} collective-permute-done((f32[4,256,128]{2,1,0:T(8,128)}, f32[4,256,128]{2,1,0:T(8,128)S(1)}, u32[]{:S(2)}, u32[]{:S(2)}) %collective-permute-start.5) | collective-permute-done | bytes 524320 | tf_op jit(solution)/shard_map/ppermute | solution.py:23
  65.5 0.0 collective-permute-done.4.rest_3_
  65.5 0.0 copy-done.3
  65.5 0.8 %copy-done.4 = f32[4,256,128]{2,1,0:T(8,128)} copy-done((f32[4,256,128]{2,1,0:T(8,128)}, f32[4,256,128]{2,1,0:T(8,128)S(1)}, u32[]{:S(2)}) %copy-start.4) | copy-done | bytes 524312
  66.3 0.9 %copy-done.2 = f32[6,256,128]{2,1,0:T(8,128)} copy-done((f32[6,256,128]{2,1,0:T(8,128)}, f32[6,256,128]{2,1,0:T(8,128)S(1)}, u32[]{:S(2)}) %copy-start.2) | copy-done | bytes 786456
  67.2 4.9 %shard_map.41 = f32[2,5,256,128]{3,2,1,0:T(8,128)} custom-call(s32[1]{0:T(128)} %bitcast.side_ref, s32[2,5]{1,0:T(2,128)} %scale_ref.7, s32[2,5]{1,0:T(2,128)} %get-tuple-element.10.keep_ref, f32[4,256,128]{2,1,0:T(8,128)} %get-tuple-element.7.rest_0_, f32[6,256,128]{2,1,0:T(8,128)} %shard_map.39.rest_1_, f32[3,128,128]{2,1,0:T(8,128)} %copy-done.1, ...), custom_call_target="tpu_custom_call" | custom-call | tf_op jit(solution)/shard_map/pallas_call | solution.py:181
  (4 shorter events, 0.0 us)
Async XLA Ops:
  0.0 14.6 %copy-start.7 = (s32[2,2,5]{2,1,0:T(2,128)S(1)}, s32[2,2,5]{2,1,0:T(2,128)}, u32[]{:S(2)}) copy-start(s32[2,2,5]{2,1,0:T(2,128)} %param.5) | copy-start | bytes 244
  0.0 33.0 %collective-permute-start = (f32[2,5,256,128]{3,2,1,0:T(8,128)}, f32[2,5,256,128]{3,2,1,0:T(8,128)S(1)}, u32[]{:S(2)}, u32[]{:S(2)}) collective-permute-start(f32[2,5,256,128]{3,2,1,0:T(8,128)} %rest_0_.3), channel_id=1, source_target_pairs={{0,1},{1,0},{2,3},{3,2},{4,5},{5,4},{6,7},{7,6},{8,9},{9,8},{10,11... | collective-permute-start | bytes 3932168 | tf_op jit(solution)/shard_map/ppermute | solution.py:18
  2.2 22.6 %collective-permute-start.2 = (f32[4,256,128]{2,1,0:T(8,128)}, f32[4,256,128]{2,1,0:T(8,128)S(1)}, u32[]{:S(2)}, u32[]{:S(2)}) collective-permute-start(f32[4,256,128]{2,1,0:T(8,128)} %shard_map.38), channel_id=1, source_target_pairs={{2,0},{4,2},{6,4},{8,6},{10,8},{12,10},{14,12},{16,14},{18,16},{20... | collective-permute-start | bytes 1572872 | tf_op jit(solution)/shard_map/ppermute | solution.py:24
  12.6 20.4 %collective-permute-start.1 = (f32[4,256,128]{2,1,0:T(8,128)}, f32[4,256,128]{2,1,0:T(8,128)S(1)}, u32[]{:S(2)}, u32[]{:S(2)}) collective-permute-start(f32[4,256,128]{2,1,0:T(8,128)} %shard_map.38), channel_id=1, source_target_pairs={{0,2},{2,4},{4,6},{6,8},{8,10},{10,12},{12,14},{14,16},{16,18},{18... | collective-permute-start | bytes 1572872 | tf_op jit(solution)/shard_map/ppermute | solution.py:23
  24.8 8.2 %copy-start.5 = (f32[4,256,128]{2,1,0:T(8,128)}, f32[4,256,128]{2,1,0:T(8,128)S(1)}, u32[]{:S(2)}) copy-start(f32[4,256,128]{2,1,0:T(8,128)S(1)} %collective-permute-done.2.rest_3_) | copy-start | bytes 1572868
  33.0 0.8 %copy-start.6 = (f32[4,256,128]{2,1,0:T(8,128)}, f32[4,256,128]{2,1,0:T(8,128)S(1)}, u32[]{:S(2)}) copy-start(f32[4,256,128]{2,1,0:T(8,128)S(1)} %collective-permute-done.1.rest_2_) | copy-start | bytes 1572868
  33.0 1.2 %copy-start = (f32[2,5,256,128]{3,2,1,0:T(8,128)}, f32[2,5,256,128]{3,2,1,0:T(8,128)S(1)}, u32[]{:S(2)}) copy-start(f32[2,5,256,128]{3,2,1,0:T(8,128)S(1)} %collective-permute-done.rest_1_) | copy-start | bytes 3932164
  38.9 26.6 %collective-permute-start.4 = (f32[6,256,128]{2,1,0:T(8,128)}, f32[6,256,128]{2,1,0:T(8,128)S(1)}, u32[]{:S(2)}, u32[]{:S(2)}) collective-permute-start(f32[6,256,128]{2,1,0:T(8,128)} %shard_map.39.rest_1_), channel_id=1, source_target_pairs={{0,1},{1,0},{2,3},{3,2},{4,5},{5,4},{6,7},{7,6},{8,9},{9,8},{10,11... | collective-permute-start | bytes 2359304 | tf_op jit(solution)/shard_map/ppermute | solution.py:18
  42.9 16.4 %collective-permute-start.6 = (f32[4,256,128]{2,1,0:T(8,128)}, f32[4,256,128]{2,1,0:T(8,128)S(1)}, u32[]{:S(2)}, u32[]{:S(2)}) collective-permute-start(f32[4,256,128]{2,1,0:T(8,128)} %get-tuple-element.7.rest_0_), channel_id=1, source_target_pairs={{2,0},{4,2},{6,4},{8,6},{10,8},{12,10},{14,12},{16,14},{18,16},{20... | collective-permute-start | bytes 1572872 | tf_op jit(solution)/shard_map/ppermute | solution.py:24
  44.8 20.7 %collective-permute-start.5 = (f32[4,256,128]{2,1,0:T(8,128)}, f32[4,256,128]{2,1,0:T(8,128)S(1)}, u32[]{:S(2)}, u32[]{:S(2)}) collective-permute-start(f32[4,256,128]{2,1,0:T(8,128)} %get-tuple-element.7.rest_0_), channel_id=1, source_target_pairs={{0,2},{2,4},{4,6},{6,8},{8,10},{10,12},{12,14},{14,16},{16,18},{18... | collective-permute-start | bytes 1572872 | tf_op jit(solution)/shard_map/ppermute | solution.py:23
  48.7 1.7 %collective-permute-start.3 = (f32[3,128,128]{2,1,0:T(8,128)}, f32[3,128,128]{2,1,0:T(8,128)S(1)}, u32[]{:S(2)}, u32[]{:S(2)}) collective-permute-start(f32[3,128,128]{2,1,0:T(8,128)} %get-tuple-element.8), channel_id=1, source_target_pairs={{0,1},{1,0},{2,3},{3,2},{4,5},{5,4},{6,7},{7,6},{8,9},{9,8},{10,11... | collective-permute-start | bytes 589832 | tf_op jit(solution)/shard_map/ppermute | solution.py:18
  50.5 0.7 copy-start.1
  59.3 6.2 %copy-start.3 = (f32[4,256,128]{2,1,0:T(8,128)}, f32[4,256,128]{2,1,0:T(8,128)S(1)}, u32[]{:S(2)}) copy-start(f32[4,256,128]{2,1,0:T(8,128)S(1)} %collective-permute-done.6.rest_5_) | copy-start | bytes 1572868
  65.5 0.8 %copy-start.4 = (f32[4,256,128]{2,1,0:T(8,128)}, f32[4,256,128]{2,1,0:T(8,128)S(1)}, u32[]{:S(2)}) copy-start(f32[4,256,128]{2,1,0:T(8,128)S(1)} %collective-permute-done.5.rest_4_) | copy-start | bytes 1572868
  66.3 0.9 %copy-start.2 = (f32[6,256,128]{2,1,0:T(8,128)}, f32[6,256,128]{2,1,0:T(8,128)S(1)}, u32[]{:S(2)}) copy-start(f32[6,256,128]{2,1,0:T(8,128)S(1)} %collective-permute-done.4.rest_3_) | copy-start | bytes 2359300
